TPU v7x, 512 devices: a whole 4x8x8 slice. The times are simulated.
512 devices in a mesh: gx: 16 (over y, z_hi), gy: 8 (over z_lo, core), gz: 4 (over x).
Axes of the slice: x: 4, y: 8, z: 8 (z_hi: 2, z_lo: 4; z = z_hi * 4 + z_lo), core: 2. Of those that a mesh axis runs over, the one named last changes fastest.
Arguments:
- charge: float32 [128, 256, 512], P('gx', 'gy', 'gz'), may hold values from -60 to 60
- texture: float32 [128, 256, 512], P('gx', 'gy', 'gz'), may hold values from 0.5 to 2
- material_eps: float32 [6], replicated, may hold values from 1 to 12
- layer_material: int32 [512], P('gz'), may hold values from 0 to 5
- gate_volts: float32 [1000], replicated, may hold values from -1 to 1
- block_cond: float32 [65536, 128], P(('gx', 'gy', 'gz')), may hold values from 2 to 20
- block_gate: int32 [65536], P(('gx', 'gy', 'gz')), may hold values from 0 to 999
- block_dest: int32 [65536], P(('gx', 'gy', 'gz')), may hold values from 0 to 127, as said below
- block_column: int32 [65536], P(('gx', 'gy', 'gz')), may hold values from 0 to 255
- initial: float32 [128, 256, 512], P('gx', 'gy', 'gz'), may hold values from -2 to 2
Outputs:
- potential: float32 [128, 256, 512], P('gx', 'gy', 'gz')
- residual_norm: float32 [], replicated
Inputs may be any that keep to these rules, and one draw needn't show every extreme that they name: `block_dest`: among the blocks of one device no value appears more than 4 times; one value appears exactly 4 times among the blocks of every device.
All inputs are finite; a program needn't handle non-finite values.
Results may differ from a plain program's by a relative error of at most 0.00002.
Values sent between devices are 32-bit elements; how exact they have to be, the bound alone decides.
No kernel may reach another device: no remote copies, remote signals or barrier semaphores. Data moves between devices by JAX's collectives and lax.ppermute only.
A program may use at most 64 MiB of HBM per device.

v0:
```python
import jax
import jax.numpy as jnp
from jax import lax
from jax.sharding import PartitionSpec as P

SWEEPS = 4


relaxation = 0.8


def with_halo(block, sides, width):
    for axis, dim in sides:
        count = lax.axis_size(axis)
        forward = [(i, i + 1) for i in range(count - 1)]
        backward = [(target, source) for source, target in forward]
        low = lax.ppermute(
            lax.slice_in_dim(block, block.shape[dim] - width, None, axis=dim), axis, forward
        )
        high = lax.ppermute(lax.slice_in_dim(block, 0, width, axis=dim), axis, backward)
        block = jnp.concatenate([low, block, high], axis=dim)
    return block


def shifted(padded):
    return [
        padded[:-2, 1:-1, 1:-1],
        padded[2:, 1:-1, 1:-1],
        padded[1:-1, :-2, 1:-1],
        padded[1:-1, 2:, 1:-1],
        padded[1:-1, 1:-1, :-2],
        padded[1:-1, 1:-1, 2:],
    ]


def face_coefficients(padded):
    centre = padded[1:-1, 1:-1, 1:-1]
    result = []
    for neighbour in shifted(padded):
        result.append(2.0 * centre * neighbour / (centre + neighbour))
    return result


def neighbour_sum(coefficients, padded):
    pieces = shifted(padded)
    total_sum = coefficients[0] * pieces[0]
    for index in range(1, 6):
        total_sum = total_sum + coefficients[index] * pieces[index]
    return total_sum


def with_rim(potential):
    return with_halo(potential, (("gx", 0), ("gy", 1), ("gz", 2)), 1)


def table_lookup(table, indices):
    labels = jnp.arange(table.shape[0], dtype=jnp.int32)
    matches = indices[:, None] == labels[None, :]
    return jnp.sum(jnp.where(matches, table[None, :], 0.0), axis=1)


def on_device(
    charge,
    texture,
    material_eps,
    layer_material,
    gate_volts,
    block_cond,
    block_gate,
    block_dest,
    block_column,
    initial,
):
    cells_x, cells_y, cells_z = charge.shape
    grid_x = lax.axis_size("gx")
    grid_y = lax.axis_size("gy")
    peer_count = grid_x * grid_y
    block_count = block_dest.shape[0]
    capacity = max(2, 4 * block_count // peer_count)
    slot_total = peer_count * capacity
    layer_eps = table_lookup(material_eps, layer_material)
    permittivity = texture * layer_eps[None, None, :]
    same_dest = block_dest[:, None] == block_dest[None, :]
    order = jnp.arange(block_count, dtype=jnp.int32)
    earlier = order[None, :] < order[:, None]
    slot_rank = jnp.sum((same_dest & earlier).astype(jnp.int32), axis=1)
    position = block_dest * capacity + slot_rank
    cond_buf = jnp.zeros((slot_total, cells_z), jnp.float32).at[position].set(block_cond)
    column_buf = jnp.zeros((slot_total,), jnp.int32).at[position].set(block_column)
    block_volts = table_lookup(gate_volts, block_gate)
    extra_buf = (
        jnp.zeros((slot_total, cells_z), jnp.float32)
        .at[position]
        .set(block_cond * block_volts[:, None])
    )
    cond_recv, extra_recv, column_recv = (
        lax.all_to_all(cond_buf, ("gx", "gy"), split_axis=0, concat_axis=0, tiled=True),
        lax.all_to_all(extra_buf, ("gx", "gy"), split_axis=0, concat_axis=0, tiled=True),
        lax.all_to_all(column_buf, ("gx", "gy"), split_axis=0, concat_axis=0, tiled=True),
    )
    empty = jnp.zeros((cells_x * cells_y, cells_z), jnp.float32)
    coupling = empty.at[column_recv].add(cond_recv).reshape(cells_x, cells_y, cells_z)
    injected = empty.at[column_recv].add(extra_recv).reshape(cells_x, cells_y, cells_z)
    forcing = charge + injected
    padded_eps = with_halo(permittivity, (("gx", 0), ("gy", 1), ("gz", 2)), 1)
    coefficients = face_coefficients(padded_eps)
    diagonal_sum = coefficients[0]
    for index in range(1, 6):
        diagonal_sum = diagonal_sum + coefficients[index]
    diagonal_sum = diagonal_sum + coupling
    potential = initial
    for sweep in range(SWEEPS):
        neighbours = neighbour_sum(coefficients, with_rim(potential))
        potential = (1.0 - relaxation) * potential + relaxation * (
            forcing + neighbours
        ) / diagonal_sum
    neighbours = neighbour_sum(coefficients, with_rim(potential))
    residual = forcing + neighbours - diagonal_sum * potential
    squared_total = lax.psum(jnp.sum(residual * residual), ("gx", "gy", "gz"))
    cell_count = cells_x * cells_y * cells_z * grid_x * grid_y * lax.axis_size("gz")
    residual_norm = jnp.sqrt(squared_total / cell_count)
    return (potential, residual_norm)


def solution(mesh):
    in_specs = (
        P("gx", "gy", "gz"),
        P("gx", "gy", "gz"),
        P(),
        P("gz"),
        P(),
        P(("gx", "gy", "gz"), None),
        P(("gx", "gy", "gz")),
        P(("gx", "gy", "gz")),
        P(("gx", "gy", "gz")),
        P("gx", "gy", "gz"),
    )
    out_specs = (P("gx", "gy", "gz"), P())
    return jax.shard_map(
        on_device, mesh=mesh, in_specs=in_specs, out_specs=out_specs, check_vma=False
    )
```

profile of v0, /device:TPU:1, one launch (start us, length us, event | category | flops | bytes accessed | tf_op | source)
XLA Modules:
  0.0 343.9 jit_solution(12263377830059414872)
XLA Ops:
  1.4 1.3 collective-permute-start.3
  2.7 12.1 %collective-permute-start.1 = (f32[1,32,128]{2,1,0:T(8,128)S(1)}, f32[1,32,128]{2,1,0:T(8,128)S(1)}, u32[]{:S(2)}, u32[]{:S(2)}) collective-permute-start(f32[1,32,128]{2,1,0:T(8,128)S(1)} %get-tuple-element.41), channel_id=1, source_target_pairs={{0,32},{32,64},{64,96},{96,128},{128,160},{160,192},{192,224},{224... | collective-permute-start | bytes 49160 | tf_op jit(solution)/shard_map/ppermute | solution.py:17
  14.8 0.9 convert_reduce_fusion
  16.4 1.1 scatter_custom_fusion
  18.2 15.8 %all-to-all-start = ((s32[128,4,1]{1,2,0:T(1,128)}), s32[128,4,1]{1,2,0:T(1,128)S(1)}, u32[]{:S(2)}, u32[]{:S(2)}) async-start(s32[128,4,1]{1,2,0:T(1,128)} %bitcast), calls=%async_computation | async-start | bytes 131072 | tf_op jit(solution)/shard_map/all_to_all | solution.py:99
  34.2 1.4 collective-permute-start.2
  35.6 7.9 %collective-permute-start = (f32[1,32,128]{2,1,0:T(8,128)S(1)}, f32[1,32,128]{2,1,0:T(8,128)S(1)}, u32[]{:S(2)}, u32[]{:S(2)}) collective-permute-start(f32[1,32,128]{2,1,0:T(8,128)S(1)} %get-tuple-element.39), channel_id=1, source_target_pairs={{0,32},{32,64},{64,96},{96,128},{128,160},{160,192},{192,224},{224... | collective-permute-start | bytes 49160 | tf_op jit(solution)/shard_map/ppermute | solution.py:17
  43.8 1.5 scatter_custom_fusion.3
  45.3 1.6 scatter_custom_fusion.1
  47.0 15.2 %all-to-all-start.1 = ((f32[128,4,128]{2,1,0:T(4,128)}), f32[128,4,128]{2,1,0:T(4,128)S(1)}, u32[]{:S(2)}, u32[]{:S(2)}) async-start(f32[128,4,128]{2,1,0:T(4,128)} %bitcast.2), calls=%async_computation.1 | async-start | bytes 524288 | tf_op jit(solution)/shard_map/all_to_all | solution.py:98
  63.7 3.5 %collective-permute-start.5 = (f32[10,1,128]{2,1,0:T(1,128)S(1)}, f32[10,1,128]{2,1,0:T(1,128)S(1)}, u32[]{:S(2)}, u32[]{:S(2)}) collective-permute-start(f32[10,1,128]{2,1,0:T(1,128)S(1)} %get-tuple-element.28), channel_id=1, source_target_pairs={{0,4},{4,8},{8,12},{12,16},{16,20},{20,24},{24,28},{1,5},{5,9},{9,... | collective-permute-start | bytes 15368 | tf_op jit(solution)/shard_map/ppermute | solution.py:17
  67.2 1.9 collective-permute-start.7
  69.2 1.9 collective-permute-start.6
  71.1 3.6 %collective-permute-start.4 = (f32[10,1,128]{2,1,0:T(1,128)S(1)}, f32[10,1,128]{2,1,0:T(1,128)S(1)}, u32[]{:S(2)}, u32[]{:S(2)}) collective-permute-start(f32[10,1,128]{2,1,0:T(1,128)S(1)} %get-tuple-element.27), channel_id=1, source_target_pairs={{0,4},{4,8},{8,12},{12,16},{16,20},{20,24},{24,28},{1,5},{5,9},{9,... | collective-permute-start | bytes 15368 | tf_op jit(solution)/shard_map/ppermute | solution.py:17
  75.0 3.1 collective-permute-start.9
  78.1 1.3 collective-permute-start.11
  79.4 12.4 %all-to-all-start.2 = ((f32[128,4,128]{2,1,0:T(4,128)}), f32[128,4,128]{2,1,0:T(4,128)S(1)}, u32[]{:S(2)}, u32[]{:S(2)}) async-start(f32[128,4,128]{2,1,0:T(4,128)} %bitcast.5), calls=%async_computation.2 | async-start | bytes 524288 | tf_op jit(solution)/shard_map/all_to_all | solution.py:97
  92.0 1.3 collective-permute-start.10
  93.3 4.6 %collective-permute-start.8 = (f32[10,34,1]{2,1,0:T(8,128)S(1)}, f32[10,34,1]{2,1,0:T(8,128)S(1)}, u32[]{:S(2)}, u32[]{:S(2)}) collective-permute-start(f32[10,34,1]{2,1,0:T(8,128)S(1)} %get-tuple-element.15), channel_id=1, source_target_pairs={{0,1},{1,2},{2,3},{4,5},{5,6},{6,7},{8,9},{9,10},{10,11},{12,13},{... | collective-permute-start | bytes 4088 | tf_op jit(solution)/shard_map/ppermute | solution.py:17
  98.0 3.4 scatter_custom_fusion.2
  101.4 4.7 %all-to-all-done.2 = f32[128,4,128]{2,1,0:T(4,128)S(1)} async-done(((f32[128,4,128]{2,1,0:T(4,128)}), f32[128,4,128]{2,1,0:T(4,128)S(1)}, u32[]{:S(2)}, u32[]{:S(2)}) %all-to-all-start.2) | async-done | bytes 262176 | tf_op jit(solution)/shard_map/all_to_all | solution.py:97
  106.0 3.2 scatter_custom_fusion.4
  109.8 4.3 %collective-permute-start.12 = (f32[1,32,128]{2,1,0:T(8,128)S(1)}, f32[1,32,128]{2,1,0:T(8,128)S(1)}, u32[]{:S(2)}, u32[]{:S(2)}) collective-permute-start(f32[1,32,128]{2,1,0:T(8,128)S(1)} %get-tuple-element.36), channel_id=1, source_target_pairs={{0,32},{32,64},{64,96},{96,128},{128,160},{160,192},{192,224},{224... | collective-permute-start | bytes 49160 | tf_op jit(solution)/shard_map/ppermute | solution.py:17
  114.1 1.3 collective-permute-start.13
  115.4 7.1 %collective-permute-done.13 = f32[1,32,128]{2,1,0:T(8,128)S(1)} collective-permute-done((f32[1,32,128]{2,1,0:T(8,128)S(1)}, f32[1,32,128]{2,1,0:T(8,128)S(1)}, u32[]{:S(2)}, u32[]{:S(2)}) %collective-permute-start.13) | collective-permute-done | bytes 16416 | tf_op jit(solution)/shard_map/ppermute | solution.py:20
  122.5 5.0 %collective-permute-start.14 = (f32[10,1,128]{2,1,0:T(1,128)S(1)}, f32[10,1,128]{2,1,0:T(1,128)S(1)}, u32[]{:S(2)}, u32[]{:S(2)}) collective-permute-start(f32[10,1,128]{2,1,0:T(1,128)S(1)} %get-tuple-element.24), channel_id=1, source_target_pairs={{0,4},{4,8},{8,12},{12,16},{16,20},{20,24},{24,28},{1,5},{5,9},{9,... | collective-permute-start | bytes 15368 | tf_op jit(solution)/shard_map/ppermute | solution.py:17
  127.5 1.9 collective-permute-start.15
  129.5 3.0 collective-permute-done.15
  132.6 4.1 %collective-permute-start.16 = (f32[10,34,1]{2,1,0:T(8,128)S(1)}, f32[10,34,1]{2,1,0:T(8,128)S(1)}, u32[]{:S(2)}, u32[]{:S(2)}) collective-permute-start(f32[10,34,1]{2,1,0:T(8,128)S(1)} %get-tuple-element.12), channel_id=1, source_target_pairs={{0,1},{1,2},{2,3},{4,5},{5,6},{6,7},{8,9},{9,10},{10,11},{12,13},{... | collective-permute-start | bytes 4088 | tf_op jit(solution)/shard_map/ppermute | solution.py:17
  136.7 1.3 collective-permute-start.17
  138.0 2.2 collective-permute-done.16
  140.2 4.1 %collective-permute-done.17 = f32[10,34,1]{2,1,0:T(8,128)S(1)} collective-permute-done((f32[10,34,1]{2,1,0:T(8,128)S(1)}, f32[10,34,1]{2,1,0:T(8,128)S(1)}, u32[]{:S(2)}, u32[]{:S(2)}) %collective-permute-start.17) | collective-permute-done | bytes 1392 | tf_op jit(solution)/shard_map/ppermute | solution.py:20
  144.6 6.2 %collective-permute-start.18 = (f32[1,32,128]{2,1,0:T(8,128)S(1)}, f32[1,32,128]{2,1,0:T(8,128)S(1)}, u32[]{:S(2)}, u32[]{:S(2)}) collective-permute-start(f32[1,32,128]{2,1,0:T(8,128)S(1)} %get-tuple-element.34), channel_id=1, source_target_pairs={{0,32},{32,64},{64,96},{96,128},{128,160},{160,192},{192,224},{224... | collective-permute-start | bytes 49160 | tf_op jit(solution)/shard_map/ppermute | solution.py:17
  150.8 1.3 collective-permute-start.19
  152.1 7.1 %collective-permute-done.19 = f32[1,32,128]{2,1,0:T(8,128)S(1)} collective-permute-done((f32[1,32,128]{2,1,0:T(8,128)S(1)}, f32[1,32,128]{2,1,0:T(8,128)S(1)}, u32[]{:S(2)}, u32[]{:S(2)}) %collective-permute-start.19) | collective-permute-done | bytes 16416 | tf_op jit(solution)/shard_map/ppermute | solution.py:20
  159.2 4.4 %collective-permute-start.20 = (f32[10,1,128]{2,1,0:T(1,128)S(1)}, f32[10,1,128]{2,1,0:T(1,128)S(1)}, u32[]{:S(2)}, u32[]{:S(2)}) collective-permute-start(f32[10,1,128]{2,1,0:T(1,128)S(1)} %get-tuple-element.22), channel_id=1, source_target_pairs={{0,4},{4,8},{8,12},{12,16},{16,20},{20,24},{24,28},{1,5},{5,9},{9,... | collective-permute-start | bytes 15368 | tf_op jit(solution)/shard_map/ppermute | solution.py:17
  163.6 1.9 collective-permute-start.21
  165.6 3.0 collective-permute-done.21
  168.7 3.1 collective-permute-start.22
  171.8 1.3 collective-permute-start.23
  173.1 2.2 collective-permute-done.22
  175.2 4.1 %collective-permute-done.23 = f32[10,34,1]{2,1,0:T(8,128)S(1)} collective-permute-done((f32[10,34,1]{2,1,0:T(8,128)S(1)}, f32[10,34,1]{2,1,0:T(8,128)S(1)}, u32[]{:S(2)}, u32[]{:S(2)}) %collective-permute-start.23) | collective-permute-done | bytes 1392 | tf_op jit(solution)/shard_map/ppermute | solution.py:20
  179.7 5.1 %collective-permute-start.24 = (f32[1,32,128]{2,1,0:T(8,128)S(1)}, f32[1,32,128]{2,1,0:T(8,128)S(1)}, u32[]{:S(2)}, u32[]{:S(2)}) collective-permute-start(f32[1,32,128]{2,1,0:T(8,128)S(1)} %get-tuple-element.32), channel_id=1, source_target_pairs={{0,32},{32,64},{64,96},{96,128},{128,160},{160,192},{192,224},{224... | collective-permute-start | bytes 49160 | tf_op jit(solution)/shard_map/ppermute | solution.py:17
  184.8 1.3 collective-permute-start.25
  186.1 7.1 %collective-permute-done.25 = f32[1,32,128]{2,1,0:T(8,128)S(1)} collective-permute-done((f32[1,32,128]{2,1,0:T(8,128)S(1)}, f32[1,32,128]{2,1,0:T(8,128)S(1)}, u32[]{:S(2)}, u32[]{:S(2)}) %collective-permute-start.25) | collective-permute-done | bytes 16416 | tf_op jit(solution)/shard_map/ppermute | solution.py:20
  193.2 5.5 %collective-permute-start.26 = (f32[10,1,128]{2,1,0:T(1,128)S(1)}, f32[10,1,128]{2,1,0:T(1,128)S(1)}, u32[]{:S(2)}, u32[]{:S(2)}) collective-permute-start(f32[10,1,128]{2,1,0:T(1,128)S(1)} %get-tuple-element.20), channel_id=1, source_target_pairs={{0,4},{4,8},{8,12},{12,16},{16,20},{20,24},{24,28},{1,5},{5,9},{9,... | collective-permute-start | bytes 15368 | tf_op jit(solution)/shard_map/ppermute | solution.py:17
  198.7 1.9 collective-permute-start.27
  200.7 3.0 collective-permute-done.27
  203.8 2.9 collective-permute-start.28
  206.7 1.3 collective-permute-start.29
  208.0 2.2 collective-permute-done.28
  210.2 4.1 %collective-permute-done.29 = f32[10,34,1]{2,1,0:T(8,128)S(1)} collective-permute-done((f32[10,34,1]{2,1,0:T(8,128)S(1)}, f32[10,34,1]{2,1,0:T(8,128)S(1)}, u32[]{:S(2)}, u32[]{:S(2)}) %collective-permute-start.29) | collective-permute-done | bytes 1392 | tf_op jit(solution)/shard_map/ppermute | solution.py:20
  214.7 6.6 %collective-permute-start.30 = (f32[1,32,128]{2,1,0:T(8,128)S(1)}, f32[1,32,128]{2,1,0:T(8,128)S(1)}, u32[]{:S(2)}, u32[]{:S(2)}) collective-permute-start(f32[1,32,128]{2,1,0:T(8,128)S(1)} %get-tuple-element.30), channel_id=1, source_target_pairs={{0,32},{32,64},{64,96},{96,128},{128,160},{160,192},{192,224},{224... | collective-permute-start | bytes 49160 | tf_op jit(solution)/shard_map/ppermute | solution.py:17
  221.3 1.3 collective-permute-start.31
  222.6 7.1 %collective-permute-done.31 = f32[1,32,128]{2,1,0:T(8,128)S(1)} collective-permute-done((f32[1,32,128]{2,1,0:T(8,128)S(1)}, f32[1,32,128]{2,1,0:T(8,128)S(1)}, u32[]{:S(2)}, u32[]{:S(2)}) %collective-permute-start.31) | collective-permute-done | bytes 16416 | tf_op jit(solution)/shard_map/ppermute | solution.py:20
  229.7 3.7 %collective-permute-start.32 = (f32[10,1,128]{2,1,0:T(1,128)S(1)}, f32[10,1,128]{2,1,0:T(1,128)S(1)}, u32[]{:S(2)}, u32[]{:S(2)}) collective-permute-start(f32[10,1,128]{2,1,0:T(1,128)S(1)} %get-tuple-element.18), channel_id=1, source_target_pairs={{0,4},{4,8},{8,12},{12,16},{16,20},{20,24},{24,28},{1,5},{5,9},{9,... | collective-permute-start | bytes 15368 | tf_op jit(solution)/shard_map/ppermute | solution.py:17
  233.4 1.9 collective-permute-start.33
  235.4 3.0 collective-permute-done.33
  238.5 1.9 collective-permute-start.34
  240.4 1.3 collective-permute-start.35
  241.7 2.2 collective-permute-done.34
  243.9 4.1 %collective-permute-done.35 = f32[10,34,1]{2,1,0:T(8,128)S(1)} collective-permute-done((f32[10,34,1]{2,1,0:T(8,128)S(1)}, f32[10,34,1]{2,1,0:T(8,128)S(1)}, u32[]{:S(2)}, u32[]{:S(2)}) %collective-permute-start.35) | collective-permute-done | bytes 1392 | tf_op jit(solution)/shard_map/ppermute | solution.py:20
  248.0 0.9 fusion.5
  248.9 93.2 %psum.7 = f32[]{:T(128)} all-reduce(f32[]{:T(128)} %fusion.5), channel_id=1, replica_groups=mesh['gx'=16,'gy'=8,'gz'=4] {'gx','gy','gz'}, use_global_device_ids=true, to_apply=%region_9.10 | all-reduce | flops 1 | bytes 8 | tf_op jit(solution)/shard_map/psum | solution.py:119
  (80 shorter events, 6.3 us)
Async XLA Ops:
  0.6 33.5 %copy-start.3 = (f32[8,32,128]{2,1,0:T(8,128)S(1)}, f32[8,32,128]{2,1,0:T(8,128)}, u32[]{:S(2)}) copy-start(f32[8,32,128]{2,1,0:T(8,128)} %param.11) | copy-start | bytes 393220
  1.4 62.2 %collective-permute-start.3 = (f32[1,32,128]{2,1,0:T(8,128)S(1)}, f32[1,32,128]{2,1,0:T(8,128)S(1)}, u32[]{:S(2)}, u32[]{:S(2)}) collective-permute-start(f32[1,32,128]{2,1,0:T(8,128)S(1)} %get-tuple-element.40), channel_id=1, source_target_pairs={{32,0},{64,32},{96,64},{128,96},{160,128},{192,160},{224,192},{256... | collective-permute-start | bytes 49160 | tf_op jit(solution)/shard_map/ppermute | solution.py:20
  2.7 60.9 %collective-permute-start.1 = (f32[1,32,128]{2,1,0:T(8,128)S(1)}, f32[1,32,128]{2,1,0:T(8,128)S(1)}, u32[]{:S(2)}, u32[]{:S(2)}) collective-permute-start(f32[1,32,128]{2,1,0:T(8,128)S(1)} %get-tuple-element.41), channel_id=1, source_target_pairs={{0,32},{32,64},{64,96},{96,128},{128,160},{160,192},{192,224},{224... | collective-permute-start | bytes 49160 | tf_op jit(solution)/shard_map/ppermute | solution.py:17
  18.2 15.8 %copy-start.7 = (f32[6]{0:T(128)S(1)}, f32[6]{0:T(128)}, u32[]{:S(2)}) copy-start(f32[6]{0:T(128)} %param.12) | copy-start | bytes 76
  18.2 15.8 %copy-start.8 = (s32[128]{0:T(128)S(1)}, s32[128]{0:T(128)}, u32[]{:S(2)}) copy-start(s32[128]{0:T(128)} %param.13) | copy-start | bytes 1540
  18.2 28.7 %all-to-all-start = ((s32[128,4,1]{1,2,0:T(1,128)}), s32[128,4,1]{1,2,0:T(1,128)S(1)}, u32[]{:S(2)}, u32[]{:S(2)}) async-start(s32[128,4,1]{1,2,0:T(1,128)} %bitcast), calls=%async_computation | async-start | bytes 131072 | tf_op jit(solution)/shard_map/all_to_all | solution.py:99
  34.1 9.4 %copy-start.5 = (f32[1000]{0:T(1024)S(1)}, f32[1000]{0:T(1024)}, u32[]{:S(2)}) copy-start(f32[1000]{0:T(1024)} %param.14) | copy-start | bytes 12004
  34.2 9.6 %copy-start.4 = (f32[128,128]{1,0:T(8,128)S(1)}, f32[128,128]{1,0:T(8,128)}, u32[]{:S(2)}) copy-start(f32[128,128]{1,0:T(8,128)} %param.15) | copy-start | bytes 196612
  34.2 9.4 %copy-start.6 = (s32[128]{0:T(128)S(1)}, s32[128]{0:T(128)}, u32[]{:S(2)}) copy-start(s32[128]{0:T(128)} %param.16) | copy-start | bytes 1540
  34.2 35.0 %collective-permute-start.2 = (f32[1,32,128]{2,1,0:T(8,128)S(1)}, f32[1,32,128]{2,1,0:T(8,128)S(1)}, u32[]{:S(2)}, u32[]{:S(2)}) collective-permute-start(f32[1,32,128]{2,1,0:T(8,128)S(1)} %get-tuple-element.38), channel_id=1, source_target_pairs={{32,0},{64,32},{96,64},{128,96},{160,128},{192,160},{224,192},{256... | collective-permute-start | bytes 49160 | tf_op jit(solution)/shard_map/ppermute | solution.py:20
  35.6 33.5 %collective-permute-start = (f32[1,32,128]{2,1,0:T(8,128)S(1)}, f32[1,32,128]{2,1,0:T(8,128)S(1)}, u32[]{:S(2)}, u32[]{:S(2)}) collective-permute-start(f32[1,32,128]{2,1,0:T(8,128)S(1)} %get-tuple-element.39), channel_id=1, source_target_pairs={{0,32},{32,64},{64,96},{96,128},{128,160},{160,192},{192,224},{224... | collective-permute-start | bytes 49160 | tf_op jit(solution)/shard_map/ppermute | solution.py:17
  47.0 32.4 %all-to-all-start.1 = ((f32[128,4,128]{2,1,0:T(4,128)}), f32[128,4,128]{2,1,0:T(4,128)S(1)}, u32[]{:S(2)}, u32[]{:S(2)}) async-start(f32[128,4,128]{2,1,0:T(4,128)} %bitcast.2), calls=%async_computation.1 | async-start | bytes 524288 | tf_op jit(solution)/shard_map/all_to_all | solution.py:98
  62.2 1.5 copy-start.1
  63.7 11.1 %collective-permute-start.5 = (f32[10,1,128]{2,1,0:T(1,128)S(1)}, f32[10,1,128]{2,1,0:T(1,128)S(1)}, u32[]{:S(2)}, u32[]{:S(2)}) collective-permute-start(f32[10,1,128]{2,1,0:T(1,128)S(1)} %get-tuple-element.28), channel_id=1, source_target_pairs={{0,4},{4,8},{8,12},{12,16},{16,20},{20,24},{24,28},{1,5},{5,9},{9,... | collective-permute-start | bytes 15368 | tf_op jit(solution)/shard_map/ppermute | solution.py:17
  67.2 7.6 %collective-permute-start.7 = (f32[10,1,128]{2,1,0:T(1,128)S(1)}, f32[10,1,128]{2,1,0:T(1,128)S(1)}, u32[]{:S(2)}, u32[]{:S(2)}) collective-permute-start(f32[10,1,128]{2,1,0:T(1,128)S(1)} %get-tuple-element.29), channel_id=1, source_target_pairs={{4,0},{8,4},{12,8},{16,12},{20,16},{24,20},{28,24},{5,1},{9,5},{13... | collective-permute-start | bytes 15368 | tf_op jit(solution)/shard_map/ppermute | solution.py:20
  69.2 22.6 %collective-permute-start.6 = (f32[10,1,128]{2,1,0:T(1,128)S(1)}, f32[10,1,128]{2,1,0:T(1,128)S(1)}, u32[]{:S(2)}, u32[]{:S(2)}) collective-permute-start(f32[10,1,128]{2,1,0:T(1,128)S(1)} %get-tuple-element.26), channel_id=1, source_target_pairs={{4,0},{8,4},{12,8},{16,12},{20,16},{24,20},{28,24},{5,1},{9,5},{13... | collective-permute-start | bytes 15368 | tf_op jit(solution)/shard_map/ppermute | solution.py:20
  71.1 20.7 %collective-permute-start.4 = (f32[10,1,128]{2,1,0:T(1,128)S(1)}, f32[10,1,128]{2,1,0:T(1,128)S(1)}, u32[]{:S(2)}, u32[]{:S(2)}) collective-permute-start(f32[10,1,128]{2,1,0:T(1,128)S(1)} %get-tuple-element.27), channel_id=1, source_target_pairs={{0,4},{4,8},{8,12},{12,16},{16,20},{20,24},{24,28},{1,5},{5,9},{9,... | collective-permute-start | bytes 15368 | tf_op jit(solution)/shard_map/ppermute | solution.py:17
  75.0 34.3 %collective-permute-start.9 = (f32[10,34,1]{2,1,0:T(8,128)S(1)}, f32[10,34,1]{2,1,0:T(8,128)S(1)}, u32[]{:S(2)}, u32[]{:S(2)}) collective-permute-start(f32[10,34,1]{2,1,0:T(8,128)S(1)} %get-tuple-element.16), channel_id=1, source_target_pairs={{0,1},{1,2},{2,3},{4,5},{5,6},{6,7},{8,9},{9,10},{10,11},{12,13},{... | collective-permute-start | bytes 4088 | tf_op jit(solution)/shard_map/ppermute | solution.py:17
  78.1 31.2 %collective-permute-start.11 = (f32[10,34,1]{2,1,0:T(8,128)S(1)}, f32[10,34,1]{2,1,0:T(8,128)S(1)}, u32[]{:S(2)}, u32[]{:S(2)}) collective-permute-start(f32[10,34,1]{2,1,0:T(8,128)S(1)} %get-tuple-element.17), channel_id=1, source_target_pairs={{1,0},{2,1},{3,2},{5,4},{6,5},{7,6},{9,8},{10,9},{11,10},{13,12},{... | collective-permute-start | bytes 4088 | tf_op jit(solution)/shard_map/ppermute | solution.py:20
  79.4 26.6 %all-to-all-start.2 = ((f32[128,4,128]{2,1,0:T(4,128)}), f32[128,4,128]{2,1,0:T(4,128)S(1)}, u32[]{:S(2)}, u32[]{:S(2)}) async-start(f32[128,4,128]{2,1,0:T(4,128)} %bitcast.5), calls=%async_computation.2 | async-start | bytes 524288 | tf_op jit(solution)/shard_map/all_to_all | solution.py:97
  92.0 17.3 %collective-permute-start.10 = (f32[10,34,1]{2,1,0:T(8,128)S(1)}, f32[10,34,1]{2,1,0:T(8,128)S(1)}, u32[]{:S(2)}, u32[]{:S(2)}) collective-permute-start(f32[10,34,1]{2,1,0:T(8,128)S(1)} %get-tuple-element.14), channel_id=1, source_target_pairs={{1,0},{2,1},{3,2},{5,4},{6,5},{7,6},{9,8},{10,9},{11,10},{13,12},{... | collective-permute-start | bytes 4088 | tf_op jit(solution)/shard_map/ppermute | solution.py:20
  93.3 16.0 %collective-permute-start.8 = (f32[10,34,1]{2,1,0:T(8,128)S(1)}, f32[10,34,1]{2,1,0:T(8,128)S(1)}, u32[]{:S(2)}, u32[]{:S(2)}) collective-permute-start(f32[10,34,1]{2,1,0:T(8,128)S(1)} %get-tuple-element.15), channel_id=1, source_target_pairs={{0,1},{1,2},{2,3},{4,5},{5,6},{6,7},{8,9},{9,10},{10,11},{12,13},{... | collective-permute-start | bytes 4088 | tf_op jit(solution)/shard_map/ppermute | solution.py:17
  97.9 11.4 %copy-start.2 = (f32[8,32,128]{2,1,0:T(8,128)S(1)}, f32[8,32,128]{2,1,0:T(8,128)}, u32[]{:S(2)}) copy-start(f32[8,32,128]{2,1,0:T(8,128)} %param.10) | copy-start | bytes 393220
  109.8 5.6 %collective-permute-start.12 = (f32[1,32,128]{2,1,0:T(8,128)S(1)}, f32[1,32,128]{2,1,0:T(8,128)S(1)}, u32[]{:S(2)}, u32[]{:S(2)}) collective-permute-start(f32[1,32,128]{2,1,0:T(8,128)S(1)} %get-tuple-element.36), channel_id=1, source_target_pairs={{0,32},{32,64},{64,96},{96,128},{128,160},{160,192},{192,224},{224... | collective-permute-start | bytes 49160 | tf_op jit(solution)/shard_map/ppermute | solution.py:17
  114.1 8.4 %collective-permute-start.13 = (f32[1,32,128]{2,1,0:T(8,128)S(1)}, f32[1,32,128]{2,1,0:T(8,128)S(1)}, u32[]{:S(2)}, u32[]{:S(2)}) collective-permute-start(f32[1,32,128]{2,1,0:T(8,128)S(1)} %get-tuple-element.37), channel_id=1, source_target_pairs={{32,0},{64,32},{96,64},{128,96},{160,128},{192,160},{224,192},{256... | collective-permute-start | bytes 49160 | tf_op jit(solution)/shard_map/ppermute | solution.py:20
  122.5 6.9 %collective-permute-start.14 = (f32[10,1,128]{2,1,0:T(1,128)S(1)}, f32[10,1,128]{2,1,0:T(1,128)S(1)}, u32[]{:S(2)}, u32[]{:S(2)}) collective-permute-start(f32[10,1,128]{2,1,0:T(1,128)S(1)} %get-tuple-element.24), channel_id=1, source_target_pairs={{0,4},{4,8},{8,12},{12,16},{16,20},{20,24},{24,28},{1,5},{5,9},{9,... | collective-permute-start | bytes 15368 | tf_op jit(solution)/shard_map/ppermute | solution.py:17
  127.5 4.9 %collective-permute-start.15 = (f32[10,1,128]{2,1,0:T(1,128)S(1)}, f32[10,1,128]{2,1,0:T(1,128)S(1)}, u32[]{:S(2)}, u32[]{:S(2)}) collective-permute-start(f32[10,1,128]{2,1,0:T(1,128)S(1)} %get-tuple-element.25), channel_id=1, source_target_pairs={{4,0},{8,4},{12,8},{16,12},{20,16},{24,20},{28,24},{5,1},{9,5},{13... | collective-permute-start | bytes 15368 | tf_op jit(solution)/shard_map/ppermute | solution.py:20
  132.6 7.6 %collective-permute-start.16 = (f32[10,34,1]{2,1,0:T(8,128)S(1)}, f32[10,34,1]{2,1,0:T(8,128)S(1)}, u32[]{:S(2)}, u32[]{:S(2)}) collective-permute-start(f32[10,34,1]{2,1,0:T(8,128)S(1)} %get-tuple-element.12), channel_id=1, source_target_pairs={{0,1},{1,2},{2,3},{4,5},{5,6},{6,7},{8,9},{9,10},{10,11},{12,13},{... | collective-permute-start | bytes 4088 | tf_op jit(solution)/shard_map/ppermute | solution.py:17
  136.7 7.6 %collective-permute-start.17 = (f32[10,34,1]{2,1,0:T(8,128)S(1)}, f32[10,34,1]{2,1,0:T(8,128)S(1)}, u32[]{:S(2)}, u32[]{:S(2)}) collective-permute-start(f32[10,34,1]{2,1,0:T(8,128)S(1)} %get-tuple-element.13), channel_id=1, source_target_pairs={{1,0},{2,1},{3,2},{5,4},{6,5},{7,6},{9,8},{10,9},{11,10},{13,12},{... | collective-permute-start | bytes 4088 | tf_op jit(solution)/shard_map/ppermute | solution.py:20
  144.6 7.5 %collective-permute-start.18 = (f32[1,32,128]{2,1,0:T(8,128)S(1)}, f32[1,32,128]{2,1,0:T(8,128)S(1)}, u32[]{:S(2)}, u32[]{:S(2)}) collective-permute-start(f32[1,32,128]{2,1,0:T(8,128)S(1)} %get-tuple-element.34), channel_id=1, source_target_pairs={{0,32},{32,64},{64,96},{96,128},{128,160},{160,192},{192,224},{224... | collective-permute-start | bytes 49160 | tf_op jit(solution)/shard_map/ppermute | solution.py:17
  150.8 8.4 %collective-permute-start.19 = (f32[1,32,128]{2,1,0:T(8,128)S(1)}, f32[1,32,128]{2,1,0:T(8,128)S(1)}, u32[]{:S(2)}, u32[]{:S(2)}) collective-permute-start(f32[1,32,128]{2,1,0:T(8,128)S(1)} %get-tuple-element.35), channel_id=1, source_target_pairs={{32,0},{64,32},{96,64},{128,96},{160,128},{192,160},{224,192},{256... | collective-permute-start | bytes 49160 | tf_op jit(solution)/shard_map/ppermute | solution.py:20
  159.2 6.3 %collective-permute-start.20 = (f32[10,1,128]{2,1,0:T(1,128)S(1)}, f32[10,1,128]{2,1,0:T(1,128)S(1)}, u32[]{:S(2)}, u32[]{:S(2)}) collective-permute-start(f32[10,1,128]{2,1,0:T(1,128)S(1)} %get-tuple-element.22), channel_id=1, source_target_pairs={{0,4},{4,8},{8,12},{12,16},{16,20},{20,24},{24,28},{1,5},{5,9},{9,... | collective-permute-start | bytes 15368 | tf_op jit(solution)/shard_map/ppermute | solution.py:17
  163.6 4.9 %collective-permute-start.21 = (f32[10,1,128]{2,1,0:T(1,128)S(1)}, f32[10,1,128]{2,1,0:T(1,128)S(1)}, u32[]{:S(2)}, u32[]{:S(2)}) collective-permute-start(f32[10,1,128]{2,1,0:T(1,128)S(1)} %get-tuple-element.23), channel_id=1, source_target_pairs={{4,0},{8,4},{12,8},{16,12},{20,16},{24,20},{28,24},{5,1},{9,5},{13... | collective-permute-start | bytes 15368 | tf_op jit(solution)/shard_map/ppermute | solution.py:20
  168.7 6.5 %collective-permute-start.22 = (f32[10,34,1]{2,1,0:T(8,128)S(1)}, f32[10,34,1]{2,1,0:T(8,128)S(1)}, u32[]{:S(2)}, u32[]{:S(2)}) collective-permute-start(f32[10,34,1]{2,1,0:T(8,128)S(1)} %get-tuple-element.10), channel_id=1, source_target_pairs={{0,1},{1,2},{2,3},{4,5},{5,6},{6,7},{8,9},{9,10},{10,11},{12,13},{... | collective-permute-start | bytes 4088 | tf_op jit(solution)/shard_map/ppermute | solution.py:17
  171.8 7.6 %collective-permute-start.23 = (f32[10,34,1]{2,1,0:T(8,128)S(1)}, f32[10,34,1]{2,1,0:T(8,128)S(1)}, u32[]{:S(2)}, u32[]{:S(2)}) collective-permute-start(f32[10,34,1]{2,1,0:T(8,128)S(1)} %get-tuple-element.11), channel_id=1, source_target_pairs={{1,0},{2,1},{3,2},{5,4},{6,5},{7,6},{9,8},{10,9},{11,10},{13,12},{... | collective-permute-start | bytes 4088 | tf_op jit(solution)/shard_map/ppermute | solution.py:20
  179.7 6.5 %collective-permute-start.24 = (f32[1,32,128]{2,1,0:T(8,128)S(1)}, f32[1,32,128]{2,1,0:T(8,128)S(1)}, u32[]{:S(2)}, u32[]{:S(2)}) collective-permute-start(f32[1,32,128]{2,1,0:T(8,128)S(1)} %get-tuple-element.32), channel_id=1, source_target_pairs={{0,32},{32,64},{64,96},{96,128},{128,160},{160,192},{192,224},{224... | collective-permute-start | bytes 49160 | tf_op jit(solution)/shard_map/ppermute | solution.py:17
  184.8 8.4 %collective-permute-start.25 = (f32[1,32,128]{2,1,0:T(8,128)S(1)}, f32[1,32,128]{2,1,0:T(8,128)S(1)}, u32[]{:S(2)}, u32[]{:S(2)}) collective-permute-start(f32[1,32,128]{2,1,0:T(8,128)S(1)} %get-tuple-element.33), channel_id=1, source_target_pairs={{32,0},{64,32},{96,64},{128,96},{160,128},{192,160},{224,192},{256... | collective-permute-start | bytes 49160 | tf_op jit(solution)/shard_map/ppermute | solution.py:20
  193.2 7.4 %collective-permute-start.26 = (f32[10,1,128]{2,1,0:T(1,128)S(1)}, f32[10,1,128]{2,1,0:T(1,128)S(1)}, u32[]{:S(2)}, u32[]{:S(2)}) collective-permute-start(f32[10,1,128]{2,1,0:T(1,128)S(1)} %get-tuple-element.20), channel_id=1, source_target_pairs={{0,4},{4,8},{8,12},{12,16},{16,20},{20,24},{24,28},{1,5},{5,9},{9,... | collective-permute-start | bytes 15368 | tf_op jit(solution)/shard_map/ppermute | solution.py:17
  198.7 4.9 %collective-permute-start.27 = (f32[10,1,128]{2,1,0:T(1,128)S(1)}, f32[10,1,128]{2,1,0:T(1,128)S(1)}, u32[]{:S(2)}, u32[]{:S(2)}) collective-permute-start(f32[10,1,128]{2,1,0:T(1,128)S(1)} %get-tuple-element.21), channel_id=1, source_target_pairs={{4,0},{8,4},{12,8},{16,12},{20,16},{24,20},{28,24},{5,1},{9,5},{13... | collective-permute-start | bytes 15368 | tf_op jit(solution)/shard_map/ppermute | solution.py:20
  203.8 6.4 %collective-permute-start.28 = (f32[10,34,1]{2,1,0:T(8,128)S(1)}, f32[10,34,1]{2,1,0:T(8,128)S(1)}, u32[]{:S(2)}, u32[]{:S(2)}) collective-permute-start(f32[10,34,1]{2,1,0:T(8,128)S(1)} %get-tuple-element.8), channel_id=1, source_target_pairs={{0,1},{1,2},{2,3},{4,5},{5,6},{6,7},{8,9},{9,10},{10,11},{12,13},{... | collective-permute-start | bytes 4088 | tf_op jit(solution)/shard_map/ppermute | solution.py:17
  206.7 7.6 %collective-permute-start.29 = (f32[10,34,1]{2,1,0:T(8,128)S(1)}, f32[10,34,1]{2,1,0:T(8,128)S(1)}, u32[]{:S(2)}, u32[]{:S(2)}) collective-permute-start(f32[10,34,1]{2,1,0:T(8,128)S(1)} %get-tuple-element.9), channel_id=1, source_target_pairs={{1,0},{2,1},{3,2},{5,4},{6,5},{7,6},{9,8},{10,9},{11,10},{13,12},{... | collective-permute-start | bytes 4088 | tf_op jit(solution)/shard_map/ppermute | solution.py:20
  214.6 33.4 %copy-start = (f32[8,32,128]{2,1,0:T(8,128)}, f32[8,32,128]{2,1,0:T(8,128)S(1)}, u32[]{:S(2)}) copy-start(f32[8,32,128]{2,1,0:T(8,128)S(1)} %fusion.20) | copy-start | bytes 393220
  214.7 7.9 %collective-permute-start.30 = (f32[1,32,128]{2,1,0:T(8,128)S(1)}, f32[1,32,128]{2,1,0:T(8,128)S(1)}, u32[]{:S(2)}, u32[]{:S(2)}) collective-permute-start(f32[1,32,128]{2,1,0:T(8,128)S(1)} %get-tuple-element.30), channel_id=1, source_target_pairs={{0,32},{32,64},{64,96},{96,128},{128,160},{160,192},{192,224},{224... | collective-permute-start | bytes 49160 | tf_op jit(solution)/shard_map/ppermute | solution.py:17
  221.3 8.4 %collective-permute-start.31 = (f32[1,32,128]{2,1,0:T(8,128)S(1)}, f32[1,32,128]{2,1,0:T(8,128)S(1)}, u32[]{:S(2)}, u32[]{:S(2)}) collective-permute-start(f32[1,32,128]{2,1,0:T(8,128)S(1)} %get-tuple-element.31), channel_id=1, source_target_pairs={{32,0},{64,32},{96,64},{128,96},{160,128},{192,160},{224,192},{256... | collective-permute-start | bytes 49160 | tf_op jit(solution)/shard_map/ppermute | solution.py:20
  229.7 5.7 %collective-permute-start.32 = (f32[10,1,128]{2,1,0:T(1,128)S(1)}, f32[10,1,128]{2,1,0:T(1,128)S(1)}, u32[]{:S(2)}, u32[]{:S(2)}) collective-permute-start(f32[10,1,128]{2,1,0:T(1,128)S(1)} %get-tuple-element.18), channel_id=1, source_target_pairs={{0,4},{4,8},{8,12},{12,16},{16,20},{20,24},{24,28},{1,5},{5,9},{9,... | collective-permute-start | bytes 15368 | tf_op jit(solution)/shard_map/ppermute | solution.py:17
  233.4 4.9 %collective-permute-start.33 = (f32[10,1,128]{2,1,0:T(1,128)S(1)}, f32[10,1,128]{2,1,0:T(1,128)S(1)}, u32[]{:S(2)}, u32[]{:S(2)}) collective-permute-start(f32[10,1,128]{2,1,0:T(1,128)S(1)} %get-tuple-element.19), channel_id=1, source_target_pairs={{4,0},{8,4},{12,8},{16,12},{20,16},{24,20},{28,24},{5,1},{9,5},{13... | collective-permute-start | bytes 15368 | tf_op jit(solution)/shard_map/ppermute | solution.py:20
  238.5 5.4 %collective-permute-start.34 = (f32[10,34,1]{2,1,0:T(8,128)S(1)}, f32[10,34,1]{2,1,0:T(8,128)S(1)}, u32[]{:S(2)}, u32[]{:S(2)}) collective-permute-start(f32[10,34,1]{2,1,0:T(8,128)S(1)} %get-tuple-element.6), channel_id=1, source_target_pairs={{0,1},{1,2},{2,3},{4,5},{5,6},{6,7},{8,9},{9,10},{10,11},{12,13},{... | collective-permute-start | bytes 4088 | tf_op jit(solution)/shard_map/ppermute | solution.py:17
  240.4 7.6 %collective-permute-start.35 = (f32[10,34,1]{2,1,0:T(8,128)S(1)}, f32[10,34,1]{2,1,0:T(8,128)S(1)}, u32[]{:S(2)}, u32[]{:S(2)}) collective-permute-start(f32[10,34,1]{2,1,0:T(8,128)S(1)} %get-tuple-element.7), channel_id=1, source_target_pairs={{1,0},{2,1},{3,2},{5,4},{6,5},{7,6},{9,8},{10,9},{11,10},{13,12},{... | collective-permute-start | bytes 4088 | tf_op jit(solution)/shard_map/ppermute | solution.py:20
where the time goes:
time: 346 us; the launch traced here: 344 us
  starting transfers between devices  158 us (46%)
  blocking collectives  93.2 us (27%)
  waiting for transfers between devices  70.2 us (20%)
  other arithmetic  13.4 us (4%)
  local copies, waits for them, and re-layouts  5.55 us (2%)
    psum x1, blocking collectives, on_device(): squared_total = lax.psum(jnp.sum(residual * residual), ('gx', 'gy', 'gz'))  93.2 us
    ppermute x18, starting transfers between devices, with_halo(): lax.ppermute(lax.slice_in_dim(block, block.shape[dim] - width, None, axis...  87.8 us
    ppermute x18, waiting for transfers between devices, with_halo(): lax.ppermute(lax.slice_in_dim(block, 0, width, axis=dim), axis, backward)  56.8 us
    ppermute x18, starting transfers between devices, with_halo(): lax.ppermute(lax.slice_in_dim(block, 0, width, axis=dim), axis, backward)  27.1 us
    all_to_all x1, starting transfers between devices, on_device(): lax.all_to_all(column_buf, ('gx', 'gy'), split_axis=0, concat_axis=0, til...  15.8 us
    all_to_all x1, starting transfers between devices, on_device(): lax.all_to_all(extra_buf, ('gx', 'gy'), split_axis=0, concat_axis=0, tile...  15.2 us
    all_to_all x1, starting transfers between devices, on_device(): lax.all_to_all(cond_buf, ('gx', 'gy'), split_axis=0, concat_axis=0, tiled...  12.4 us
    ppermute x18, waiting for transfers between devices, with_halo(): lax.ppermute(lax.slice_in_dim(block, block.shape[dim] - width, None, axis...  8.69 us
  transfers between devices with their start and end apart: 39, of which 17 were waited for; matrix products, arithmetic and copies ran while one was open for 4% of the time, Pallas kernels for 0%

commit v1 on v0

v1 whole, which is shorter than its diff:
```python
import jax
import jax.numpy as jnp
from jax import lax
from jax.sharding import PartitionSpec as P

SWEEPS = 4


relaxation = 0.8


def table_lookup(table, indices):
    labels = jnp.arange(table.shape[0], dtype=jnp.int32)
    matches = indices[:, None] == labels[None, :]
    return jnp.sum(jnp.where(matches, table[None, :], 0.0), axis=1)


def exchange(lo, hi, axis):
    count = lax.axis_size(axis)
    forward = [(i, i + 1) for i in range(count - 1)]
    backward = [(i + 1, i) for i in range(count - 1)]
    from_prev = lax.ppermute(hi, axis, forward)
    from_next = lax.ppermute(lo, axis, backward)
    return from_prev, from_next


def with_wide_halo(fields, width):
    prev, nxt = exchange(fields[:, :width], fields[:, -width:], "gx")
    fields = jnp.concatenate([prev, fields, nxt], axis=1)
    prev, nxt = exchange(fields[:, :, :width], fields[:, :, -width:], "gy")
    fields = jnp.concatenate([prev, fields, nxt], axis=2)
    nf, nx, ny, _ = fields.shape

    def pack(a):
        return jnp.moveaxis(a, 3, 1).reshape(nf * width, nx * ny)

    def unpack(a):
        return jnp.moveaxis(a.reshape(nf, width, nx, ny), 1, 3)

    prev, nxt = exchange(pack(fields[..., :width]), pack(fields[..., -width:]), "gz")
    return jnp.concatenate([unpack(prev), fields, unpack(nxt)], axis=3)


def shifted(padded):
    return [
        padded[:-2, 1:-1, 1:-1],
        padded[2:, 1:-1, 1:-1],
        padded[1:-1, :-2, 1:-1],
        padded[1:-1, 2:, 1:-1],
        padded[1:-1, 1:-1, :-2],
        padded[1:-1, 1:-1, 2:],
    ]


def face_coefficients(padded):
    centre = padded[1:-1, 1:-1, 1:-1]
    result = []
    for neighbour in shifted(padded):
        result.append(2.0 * centre * neighbour / (centre + neighbour))
    return result


def neighbour_sum(coefficients, padded):
    pieces = shifted(padded)
    total_sum = coefficients[0] * pieces[0]
    for index in range(1, 6):
        total_sum = total_sum + coefficients[index] * pieces[index]
    return total_sum


def trim(a, k):
    if k == 0:
        return a
    return a[k:-k, k:-k, k:-k]


def on_device(
    charge,
    texture,
    material_eps,
    layer_material,
    gate_volts,
    block_cond,
    block_gate,
    block_dest,
    block_column,
    initial,
):
    cells_x, cells_y, cells_z = charge.shape
    grid_x = lax.axis_size("gx")
    grid_y = lax.axis_size("gy")
    grid_z = lax.axis_size("gz")
    peer_count = grid_x * grid_y
    block_count = block_dest.shape[0]
    capacity = max(2, 4 * block_count // peer_count)
    slot_total = peer_count * capacity
    layer_eps = table_lookup(material_eps, layer_material)
    permittivity = texture * layer_eps[None, None, :]

    same_dest = block_dest[:, None] == block_dest[None, :]
    order = jnp.arange(block_count, dtype=jnp.int32)
    earlier = order[None, :] < order[:, None]
    slot_rank = jnp.sum((same_dest & earlier).astype(jnp.int32), axis=1)
    position = block_dest * capacity + slot_rank
    block_volts = table_lookup(gate_volts, block_gate)
    rows = jnp.concatenate(
        [
            block_cond,
            block_volts[:, None],
            block_column.astype(jnp.float32)[:, None],
        ],
        axis=1,
    )
    width_row = cells_z + 2
    send = jnp.zeros((slot_total, width_row), jnp.float32).at[position].set(rows)
    send = send.reshape(peer_count, capacity * width_row)
    recv = lax.all_to_all(send, ("gx", "gy"), split_axis=0, concat_axis=0, tiled=True)
    recv = recv.reshape(slot_total, width_row)
    cond_recv = recv[:, :cells_z]
    volt_recv = recv[:, cells_z]
    column_recv = recv[:, cells_z + 1].astype(jnp.int32)
    extra_recv = cond_recv * volt_recv[:, None]
    empty = jnp.zeros((cells_x * cells_y, 2, cells_z), jnp.float32)
    summed = empty.at[column_recv].add(jnp.stack([cond_recv, extra_recv], axis=1))
    coupling = summed[:, 0].reshape(cells_x, cells_y, cells_z)
    injected = summed[:, 1].reshape(cells_x, cells_y, cells_z)
    forcing = charge + injected

    halo = SWEEPS + 1
    fields = jnp.stack([permittivity, forcing, coupling, initial], axis=0)
    wide = with_wide_halo(fields, halo)
    eps_w, forcing_w, coupling_w, potential = wide[0], wide[1], wide[2], wide[3]

    coefficients = face_coefficients(eps_w)
    diagonal_sum = coefficients[0]
    for index in range(1, 6):
        diagonal_sum = diagonal_sum + coefficients[index]
    diagonal_sum = diagonal_sum + trim(coupling_w, 1)
    forcing_c = trim(forcing_w, 1)

    def inside_mask(k):
        def axis_mask(axis, cells):
            start = lax.axis_index(axis) * cells - k
            idx = start + jnp.arange(cells + 2 * k, dtype=jnp.int32)
            return (idx >= 0) & (idx < cells * lax.axis_size(axis))

        mx = axis_mask("gx", cells_x)
        my = axis_mask("gy", cells_y)
        mz = axis_mask("gz", cells_z)
        return mx[:, None, None] & my[None, :, None] & mz[None, None, :]

    for sweep in range(SWEEPS):
        k = halo - 1 - sweep
        off = sweep
        coeffs = [trim(c, off) for c in coefficients]
        neighbours = neighbour_sum(coeffs, potential)
        centre = potential[1:-1, 1:-1, 1:-1]
        updated = (1.0 - relaxation) * centre + relaxation * (
            trim(forcing_c, off) + neighbours
        ) / trim(diagonal_sum, off)
        if k > 0:
            updated = jnp.where(inside_mask(k), updated, 0.0)
        potential = updated

    off = SWEEPS
    coeffs = [trim(c, off) for c in coefficients]
    neighbours = neighbour_sum(coeffs, potential)
    centre = potential[1:-1, 1:-1, 1:-1]
    residual = trim(forcing_c, off) + neighbours - trim(diagonal_sum, off) * centre
    local_total = jnp.sum(residual * residual)
    device_count = grid_x * grid_y * grid_z
    gathered = lax.all_to_all(
        jnp.full((device_count,), local_total),
        ("gx", "gy", "gz"),
        split_axis=0,
        concat_axis=0,
        tiled=True,
    )
    squared_total = jnp.sum(gathered)
    cell_count = cells_x * cells_y * cells_z * device_count
    residual_norm = jnp.sqrt(squared_total / cell_count)
    return (centre, residual_norm)


def solution(mesh):
    in_specs = (
        P("gx", "gy", "gz"),
        P("gx", "gy", "gz"),
        P(),
        P("gz"),
        P(),
        P(("gx", "gy", "gz"), None),
        P(("gx", "gy", "gz")),
        P(("gx", "gy", "gz")),
        P(("gx", "gy", "gz")),
        P("gx", "gy", "gz"),
    )
    out_specs = (P("gx", "gy", "gz"), P())
    return jax.shard_map(
        on_device, mesh=mesh, in_specs=in_specs, out_specs=out_specs, check_vma=False
    )
```

time: 346 us -> 177 us (0.51)
  starting transfers between devices: 158 us -> 46 us
  blocking collectives: 93.2 us -> 33.3 us
  waiting for transfers between devices: 70.2 us -> 36.9 us
  other arithmetic: 13.4 us -> 44.8 us
  local copies, waits for them, and re-layouts: 5.55 us -> 12.8 us
    psum x1 -> x0, blocking collectives: 93.2 us -> none  [on_device(): squared_total = lax.psum(jnp.sum(residual * residual), ('gx', 'gy', 'gz'))]
    ppermute x36 -> x6, starting transfers between devices: 115 us -> 27.6 us  [the longest x3 23.1 us: exchange(): from_prev = lax.ppermute(hi, axis, forward)]
    ppermute x36 -> x6, waiting for transfers between devices: 65.5 us -> 23.4 us  [the longest x3 16.6 us: exchange(): from_next = lax.ppermute(lo, axis, backward)]
    all_to_all x0 -> x1, blocking collectives: none -> 33.3 us  [on_device(): lax.all_to_all(jnp.full((device_count,), local_total), ('gx', 'gy', 'gz')...]
    all_to_all x3 -> x1, starting transfers between devices: 43.4 us -> 18.4 us  [on_device(): lax.all_to_all(send, ('gx', 'gy'), split_axis=0, concat_axis=0, tiled=True)]
    scatter-add x2 -> x1, other arithmetic: 6.65 us -> 17.7 us  [on_device(): empty.at[column_recv].add(jnp.stack([cond_recv, extra_recv], axis=1))]
    all_to_all x3 -> x1, waiting for transfers between devices: 4.67 us -> 13.6 us  [on_device(): lax.all_to_all(send, ('gx', 'gy'), split_axis=0, concat_axis=0, tiled=True)]
    select_n x2 -> x6, other arithmetic: 0.67 us -> 9.38 us  [the longest x4 8.47 us: on_device(): updated = jnp.where(inside_mask(k), updated, 0.0)]
  transfers between devices with their start and end apart: 39 -> 7, of which waited for: 17 -> 6; matrix products, arithmetic and copies ran while one was open for 4% -> 3% of each run, Pallas kernels for 0% -> 0%
where the time goes in v1:
time: 177 us
  starting transfers between devices  46 us (26%)
  other arithmetic  44.8 us (25%)
  waiting for transfers between devices  36.9 us (21%)
  blocking collectives  33.3 us (19%)
  local copies, waits for them, and re-layouts  12.8 us (7%)
  between operations  2.91 us (2%)
    all_to_all x1, blocking collectives, on_device(): lax.all_to_all(jnp.full((device_count,), local_total), ('gx', 'gy', 'gz')...  33.3 us
    ppermute x3, starting transfers between devices, exchange(): from_prev = lax.ppermute(hi, axis, forward)  23.1 us
    all_to_all x1, starting transfers between devices, on_device(): lax.all_to_all(send, ('gx', 'gy'), split_axis=0, concat_axis=0, tiled=True)  18.4 us
    scatter-add x1, other arithmetic, on_device(): empty.at[column_recv].add(jnp.stack([cond_recv, extra_recv], axis=1))  17.7 us
    ppermute x3, waiting for transfers between devices, exchange(): from_next = lax.ppermute(lo, axis, backward)  16.6 us
    all_to_all x1, waiting for transfers between devices, on_device(): lax.all_to_all(send, ('gx', 'gy'), split_axis=0, concat_axis=0, tiled=True)  13.6 us
    select_n x4, other arithmetic, on_device(): updated = jnp.where(inside_mask(k), updated, 0.0)  8.47 us
    ppermute x3, waiting for transfers between devices, exchange(): from_prev = lax.ppermute(hi, axis, forward)  6.82 us
  transfers between devices with their start and end apart: 7, of which 6 were waited for; matrix products, arithmetic and copies ran while one was open for 3% of the time, Pallas kernels for 0%

profile of v1, /device:TPU:1, one launch (start us, length us, event | category | flops | bytes accessed | tf_op | source)
XLA Modules:
  0.0 176.7 jit_solution(7369579914003164277)
XLA Ops:
  0.7 0.9 select_reduce_fusion
  1.6 0.1 copy.37
  1.7 0.7 convert_bitcast_fusion
  2.3 0.1 copy.38
  2.5 0.9 convert_reduce_fusion
  3.4 0.7 compare_select_fusion.1
  4.0 1.5 scatter_custom_fusion
  5.6 1.4 all_to_all.13
  6.9 18.4 %all-to-all-start = ((f32[128,1,520]{2,1,0:T(1,128)}), f32[128,1,520]{2,1,0:T(1,128)S(1)}, u32[]{:S(2)}, u32[]{:S(2)}) async-start(f32[128,1,520]{2,1,0:T(1,128)} %all_to_all.13), calls=%async_computation | async-start | bytes 655360 | tf_op jit(solution)/shard_map/all_to_all | solution.py:117
  25.4 0.5 compare_and_fusion
  25.9 0.5 compare_and_fusion.3
  26.5 0.6 compare_and_fusion.6
  27.1 0.1 select_reduce_fusion.1
  27.2 0.1 broadcast_and_fusion
  27.2 0.1 broadcast_and_fusion.1
  27.3 13.6 %all-to-all-done = f32[128,1,520]{2,1,0:T(1,128)S(1)} async-done(((f32[128,1,520]{2,1,0:T(1,128)}), f32[128,1,520]{2,1,0:T(1,128)S(1)}, u32[]{:S(2)}, u32[]{:S(2)}) %all-to-all-start) | async-done | bytes 266272 | tf_op jit(solution)/shard_map/all_to_all | solution.py:117
  40.9 0.8 reduce.1
  41.7 0.3 reshape.245
  41.9 0.1 slice_reduce_fusion
  42.1 0.2 fusion.37
  42.3 0.1 slice_bitcast_fusion.6
  42.5 0.4 copy.40
  42.9 0.1 broadcast_in_dim.84
  43.0 17.7 %scatter_fusion = f32[256,2,128]{2,1,0:T(2,128)S(1)} fusion(f32[256,2,128]{2,1,0:T(2,128)S(1)} %broadcast_in_dim.84, s32[512]{0:T(512)S(1)} %fusion.37, f32[512,2,128]{2,1,0:T(2,128)S(1)} %copy.40), kind=kCustom, calls=%fused_computation.1 | custom fusion | flops 131072 | bytes 1574912 | tf_op jit(solution)/shard_map/scatter-add | solution.py:124
  60.7 0.2 fusion.57
  61.1 0.1 fusion.56
  61.2 4.2 %collective-permute-start = (f32[4,5,32,128]{3,2,1,0:T(8,128)S(1)}, f32[4,5,32,128]{3,2,1,0:T(8,128)S(1)}, u32[]{:S(2)}, u32[]{:S(2)}) collective-permute-start(f32[4,5,32,128]{3,2,1,0:T(8,128)S(1)} %get-tuple-element.19), channel_id=1, source_target_pairs={{0,32},{32,64},{64,96},{96,128},{128,160},{160,192},{192,224},{224... | collective-permute-start | bytes 983048 | tf_op jit(solution)/shard_map/ppermute | solution.py:22
  65.4 1.3 collective-permute-start.1
  66.7 0.1 broadcast_and_fusion.2
  66.8 5.2 %collective-permute-done = f32[4,5,32,128]{3,2,1,0:T(8,128)S(1)} collective-permute-done((f32[4,5,32,128]{3,2,1,0:T(8,128)S(1)}, f32[4,5,32,128]{3,2,1,0:T(8,128)S(1)}, u32[]{:S(2)}, u32[]{:S(2)}) %collective-permute-start) | collective-permute-done | bytes 327712 | tf_op jit(solution)/shard_map/ppermute | solution.py:22
  72.0 9.9 %collective-permute-done.1 = f32[4,5,32,128]{3,2,1,0:T(8,128)S(1)} collective-permute-done((f32[4,5,32,128]{3,2,1,0:T(8,128)S(1)}, f32[4,5,32,128]{3,2,1,0:T(8,128)S(1)}, u32[]{:S(2)}, u32[]{:S(2)}) %collective-permute-start.1) | collective-permute-done | bytes 327712 | tf_op jit(solution)/shard_map/ppermute | solution.py:23
  81.9 15.6 %collective-permute-start.2 = (f32[4,18,5,128]{3,2,1,0:T(8,128)S(1)}, f32[4,18,5,128]{3,2,1,0:T(8,128)S(1)}, u32[]{:S(2)}, u32[]{:S(2)}) collective-permute-start(f32[4,18,5,128]{3,2,1,0:T(8,128)S(1)} %get-tuple-element.17), channel_id=1, source_target_pairs={{0,4},{4,8},{8,12},{12,16},{16,20},{20,24},{24,28},{1,5},{5,9},{9,... | collective-permute-start | bytes 552968 | tf_op jit(solution)/shard_map/ppermute | solution.py:22
  97.5 1.9 %collective-permute-start.3 = (f32[4,18,5,128]{3,2,1,0:T(8,128)S(1)}, f32[4,18,5,128]{3,2,1,0:T(8,128)S(1)}, u32[]{:S(2)}, u32[]{:S(2)}) collective-permute-start(f32[4,18,5,128]{3,2,1,0:T(8,128)S(1)} %get-tuple-element.18), channel_id=1, source_target_pairs={{4,0},{8,4},{12,8},{16,12},{20,16},{24,20},{28,24},{5,1},{9,5},{13... | collective-permute-start | bytes 552968 | tf_op jit(solution)/shard_map/ppermute | solution.py:23
  99.4 0.1 broadcast_and_fusion.3
  99.5 1.6 collective-permute-done.2
  101.1 4.4 %collective-permute-done.3 = f32[4,18,5,128]{3,2,1,0:T(8,128)S(1)} collective-permute-done((f32[4,18,5,128]{3,2,1,0:T(8,128)S(1)}, f32[4,18,5,128]{3,2,1,0:T(8,128)S(1)}, u32[]{:S(2)}, u32[]{:S(2)}) %collective-permute-start.3) | collective-permute-done | bytes 184352 | tf_op jit(solution)/shard_map/ppermute | solution.py:23
  105.6 0.7 copy-done.7
  106.3 0.3 pad_maximum_fusion.1
  106.6 0.6 slice_bitcast_fusion.1
  107.2 1.6 copy.41
  108.8 1.1 reshape.246
  109.8 3.2 %collective-permute-start.4 = (f32[20,756]{1,0:T(8,128)S(1)}, f32[20,756]{1,0:T(8,128)S(1)}, u32[]{:S(2)}, u32[]{:S(2)}) collective-permute-start(f32[20,756]{1,0:T(8,128)S(1)} %reshape.246), channel_id=1, source_target_pairs={{0,1},{1,2},{2,3},{4,5},{5,6},{6,7},{8,9},{9,10},{10,11},{12,13},{... | collective-permute-start | bytes 181448 | tf_op jit(solution)/shard_map/ppermute | solution.py:22
  113.0 0.9 copy.42
  113.9 0.1 reshape.248
  114.1 1.3 collective-permute-start.5
  115.4 0.6 compare_and_fusion.9
  116.0 0.1 reshape.247
  116.1 0.8 copy.43
  116.8 2.3 %collective-permute-done.5 = f32[20,756]{1,0:T(8,128)S(1)} collective-permute-done((f32[20,756]{1,0:T(8,128)S(1)}, f32[20,756]{1,0:T(8,128)S(1)}, u32[]{:S(2)}, u32[]{:S(2)}) %collective-permute-start.5) | collective-permute-done | bytes 60512 | tf_op jit(solution)/shard_map/ppermute | solution.py:23
  119.1 0.8 reshape.249
  120.0 1.7 copy.44
  121.7 6.4 %pad_maximum_fusion = f32[4,18,42,138]{3,2,1,0:T(8,128)S(1)} fusion(f32[4,18,42,5]{3,2,1,0:T(8,128)S(1)} %copy.44, f32[4,18,5,128]{3,2,1,0:T(8,128)} %copy-done.7, f32[4,5,32,128]{3,2,1,0:T(8,128)} %copy-done.4, f32[1,8,32,128]{3,2,1,0:T(8,128)} %bitcast.36, f32[1,8,32,128]{3,2,1,0:T(8,128)} %bitcast.35, f32[1,8,32,128]{3,2,1,0:T(8,128)} %copy-done.1, ...), kind=kLoop, calls=%fused_computation.2 | loop fusion | flops 3755808 | bytes 3338496 | tf_op jit(solution)/shard_map/concatenate | solution.py:41
  128.1 0.3 slice_bitcast_fusion.3
  128.4 0.3 copy-done.10
  128.7 2.7 %fusion.5 = (f32[16,40,136]{2,1,0:T(8,128)S(1)}, f32[16,40,136]{2,1,0:T(8,128)S(1)}, f32[16,40,136]{2,1,0:T(8,128)S(1)}, f32[16,40,136]{2,1,0:T(8,128)S(1)}, f32...) fusion(f32[18,42,138]{2,1,0:T(8,128)S(1)} %get-tuple-element.14, ...), kind=kLoop, calls=%fused_computation.18 | loop fusion | flops 3742720 | bytes 8008456 | tf_op jit(solution)/shard_map/jit(_where)/select_n | solution.py:162
  131.4 0.3 slice_add_fusion
  131.8 0.3 copy-done.13
  132.0 2.2 %fusion.11 = f32[14,38,134]{2,1,0:T(8,128)S(1)} fusion(f32[16,40,136]{2,1,0:T(8,128)S(1)} %slice_add_fusion, f32[16,40,136]{2,1,0:T(8,128)S(1)} %get-tuple-element.4, f32[16,40,136]{2,1,0:T(8,128)S(1)} %get-tuple-element.10, f32[16,40,136]{2,1,0:T(8,128)S(1)} %get-tuple-element.9, f32[16,40,136]{2,1,0:T(8,128)S(1)} %get-tuple-element.8, ...), kind=kLoop, calls=%fused_computation.37 | loop fusion | flops 1283184 | bytes 4563098 | tf_op jit(solution)/shard_map/jit(_where)/select_n | solution.py:162
  134.3 1.9 %fusion.20 = f32[12,36,132]{2,1,0:T(8,128)S(1)} fusion(f32[16,40,136]{2,1,0:T(8,128)S(1)} %slice_add_fusion, f32[14,38,134]{2,1,0:T(8,128)S(1)} %fusion.11, f32[16,40,136]{2,1,0:T(8,128)S(1)} %get-tuple-element.10, f32[16,40,136]{2,1,0:T(8,128)S(1)} %get-tuple-element.9, f32[16,40,136]{2,1,0:T(8,128)S(1)} %get-tuple-element.8, ...), kind=kLoop, calls=%fused_computation.58 | loop fusion | flops 1026432 | bytes 3650100 | tf_op jit(solution)/shard_map/jit(_where)/select_n | solution.py:162
  136.2 1.6 fusion.29
  137.9 1.8 %fusion.42 = (f32[]{:T(128)}, f32[8,32,128]{2,1,0:T(8,128)}) fusion(f32[16,40,136]{2,1,0:T(8,128)S(1)} %slice_add_fusion, f32[10,34,130]{2,1,0:T(8,128)S(1)} %fusion.29, f32[16,40,136]{2,1,0:T(8,128)S(1)} %get-tuple-element.10, f32[16,40,136]{2,1,0:T(8,128)S(1)} %get-tuple-element.9, f32[16,40,136]{2,1,0:T(8,128)S(1)} %get-tuple-element.8, ...), kind=kLoop, calls=%fused_computation.106 | loop fusion | flops 524287 | bytes 2097156 | tf_op jit(solution)/shard_map/reduce_sum | solution.py:170
  139.7 0.8 broadcast_in_dim.95
  140.5 33.3 %all_to_all.16 = f32[512,1,1]{2,1,0:T(1,128)S(1)} all-to-all(f32[512,1,1]{2,1,0:T(1,128)S(1)} %broadcast_in_dim.95), channel_id=1, replica_groups=mesh['gx'=16,'gy'=8,'gz'=4] {'gx','gy','gz'}, dimensions={0} | all-to-all | bytes 4096 | tf_op jit(solution)/shard_map/all_to_all | solution.py:172
  173.8 1.1 reduce_sum.49
  (42 shorter events, 0.3 us)
Async XLA Ops:
  0.6 26.4 %copy-start.14 = (f32[6]{0:T(128)S(1)}, f32[6]{0:T(128)}, u32[]{:S(2)}) copy-start(f32[6]{0:T(128)} %param.12) | copy-start | bytes 76
  0.6 26.4 %copy-start.15 = (s32[128]{0:T(128)S(1)}, s32[128]{0:T(128)}, u32[]{:S(2)}) copy-start(s32[128]{0:T(128)} %param.13) | copy-start | bytes 1540
  6.9 33.9 %all-to-all-start = ((f32[128,1,520]{2,1,0:T(1,128)}), f32[128,1,520]{2,1,0:T(1,128)S(1)}, u32[]{:S(2)}, u32[]{:S(2)}) async-start(f32[128,1,520]{2,1,0:T(1,128)} %all_to_all.13), calls=%async_computation | async-start | bytes 655360 | tf_op jit(solution)/shard_map/all_to_all | solution.py:117
  42.5 18.5 %copy-start.8 = (f32[8,32,128]{2,1,0:T(8,128)S(1)}, f32[8,32,128]{2,1,0:T(8,128)}, u32[]{:S(2)}) copy-start(f32[8,32,128]{2,1,0:T(8,128)} %param.10) | copy-start | bytes 393220
  42.5 18.5 %copy-start.9 = (f32[8,32,128]{2,1,0:T(8,128)S(1)}, f32[8,32,128]{2,1,0:T(8,128)}, u32[]{:S(2)}) copy-start(f32[8,32,128]{2,1,0:T(8,128)} %param.11) | copy-start | bytes 393220
  42.9 18.1 %copy-start.5 = (f32[8,32,128]{2,1,0:T(8,128)S(1)}, f32[8,32,128]{2,1,0:T(8,128)}, u32[]{:S(2)}) copy-start(f32[8,32,128]{2,1,0:T(8,128)} %param.19) | copy-start | bytes 393220
  61.0 44.6 %copy-start = (f32[256,1,128]{2,1,0:T(1,128)}, f32[256,1,128]{2,1,0:T(1,128)S(1)}, u32[]{:S(2)}) copy-start(f32[256,1,128]{2,1,0:T(1,128)S(1)} %get-tuple-element.24) | copy-start | bytes 393220
  61.0 44.5 %copy-start.1 = (f32[1,8,32,128]{3,2,1,0:T(8,128)}, f32[1,8,32,128]{3,2,1,0:T(8,128)S(1)}, u32[]{:S(2)}) copy-start(f32[1,8,32,128]{3,2,1,0:T(8,128)S(1)} %get-tuple-element.25) | copy-start | bytes 393220
  61.0 44.5 %copy-start.2 = (f32[1,8,32,128]{3,2,1,0:T(8,128)}, f32[1,8,32,128]{3,2,1,0:T(8,128)S(1)}, u32[]{:S(2)}) copy-start(f32[1,8,32,128]{3,2,1,0:T(8,128)S(1)} %get-tuple-element.26) | copy-start | bytes 393220
  61.2 10.8 %collective-permute-start = (f32[4,5,32,128]{3,2,1,0:T(8,128)S(1)}, f32[4,5,32,128]{3,2,1,0:T(8,128)S(1)}, u32[]{:S(2)}, u32[]{:S(2)}) collective-permute-start(f32[4,5,32,128]{3,2,1,0:T(8,128)S(1)} %get-tuple-element.19), channel_id=1, source_target_pairs={{0,32},{32,64},{64,96},{96,128},{128,160},{160,192},{192,224},{224... | collective-permute-start | bytes 983048 | tf_op jit(solution)/shard_map/ppermute | solution.py:22
  65.4 16.4 %collective-permute-start.1 = (f32[4,5,32,128]{3,2,1,0:T(8,128)S(1)}, f32[4,5,32,128]{3,2,1,0:T(8,128)S(1)}, u32[]{:S(2)}, u32[]{:S(2)}) collective-permute-start(f32[4,5,32,128]{3,2,1,0:T(8,128)S(1)} %get-tuple-element.20), channel_id=1, source_target_pairs={{32,0},{64,32},{96,64},{128,96},{160,128},{192,160},{224,192},{256... | collective-permute-start | bytes 983048 | tf_op jit(solution)/shard_map/ppermute | solution.py:23
  72.0 33.6 %copy-start.3 = (f32[4,5,32,128]{3,2,1,0:T(8,128)}, f32[4,5,32,128]{3,2,1,0:T(8,128)S(1)}, u32[]{:S(2)}) copy-start(f32[4,5,32,128]{3,2,1,0:T(8,128)S(1)} %collective-permute-done) | copy-start | bytes 983044
  81.8 23.8 %copy-start.4 = (f32[4,5,32,128]{3,2,1,0:T(8,128)}, f32[4,5,32,128]{3,2,1,0:T(8,128)S(1)}, u32[]{:S(2)}) copy-start(f32[4,5,32,128]{3,2,1,0:T(8,128)S(1)} %collective-permute-done.1) | copy-start | bytes 983044
  81.9 19.3 %collective-permute-start.2 = (f32[4,18,5,128]{3,2,1,0:T(8,128)S(1)}, f32[4,18,5,128]{3,2,1,0:T(8,128)S(1)}, u32[]{:S(2)}, u32[]{:S(2)}) collective-permute-start(f32[4,18,5,128]{3,2,1,0:T(8,128)S(1)} %get-tuple-element.17), channel_id=1, source_target_pairs={{0,4},{4,8},{8,12},{12,16},{16,20},{20,24},{24,28},{1,5},{5,9},{9,... | collective-permute-start | bytes 552968 | tf_op jit(solution)/shard_map/ppermute | solution.py:22
  97.5 8.0 %collective-permute-start.3 = (f32[4,18,5,128]{3,2,1,0:T(8,128)S(1)}, f32[4,18,5,128]{3,2,1,0:T(8,128)S(1)}, u32[]{:S(2)}, u32[]{:S(2)}) collective-permute-start(f32[4,18,5,128]{3,2,1,0:T(8,128)S(1)} %get-tuple-element.18), channel_id=1, source_target_pairs={{4,0},{8,4},{12,8},{16,12},{20,16},{24,20},{28,24},{5,1},{9,5},{13... | collective-permute-start | bytes 552968 | tf_op jit(solution)/shard_map/ppermute | solution.py:23
  101.1 4.4 %copy-start.6 = (f32[4,18,5,128]{3,2,1,0:T(8,128)}, f32[4,18,5,128]{3,2,1,0:T(8,128)S(1)}, u32[]{:S(2)}) copy-start(f32[4,18,5,128]{3,2,1,0:T(8,128)S(1)} %collective-permute-done.2) | copy-start | bytes 552964
  105.6 0.7 copy-start.7
  109.8 6.1 %collective-permute-start.4 = (f32[20,756]{1,0:T(8,128)S(1)}, f32[20,756]{1,0:T(8,128)S(1)}, u32[]{:S(2)}, u32[]{:S(2)}) collective-permute-start(f32[20,756]{1,0:T(8,128)S(1)} %reshape.246), channel_id=1, source_target_pairs={{0,1},{1,2},{2,3},{4,5},{5,6},{6,7},{8,9},{9,10},{10,11},{12,13},{... | collective-permute-start | bytes 181448 | tf_op jit(solution)/shard_map/ppermute | solution.py:22
  114.1 5.1 %collective-permute-start.5 = (f32[20,756]{1,0:T(8,128)S(1)}, f32[20,756]{1,0:T(8,128)S(1)}, u32[]{:S(2)}, u32[]{:S(2)}) collective-permute-start(f32[20,756]{1,0:T(8,128)S(1)} %reshape.248), channel_id=1, source_target_pairs={{1,0},{2,1},{3,2},{5,4},{6,5},{7,6},{9,8},{10,9},{11,10},{13,12},{... | collective-permute-start | bytes 181448 | tf_op jit(solution)/shard_map/ppermute | solution.py:23
  128.1 0.7 copy-start.10
  131.4 0.6 copy-start.13
  132.0 2.2 %copy-start.11 = (pred[132]{0:T(512)(128)(4,1)S(1)}, pred[132]{0:T(512)(128)(4,1)}, u32[]{:S(2)}) copy-start(pred[132]{0:T(512)(128)(4,1)} %compare_and_fusion.6) | copy-start | bytes 400
  134.3 1.9 %copy-start.12 = (pred[130]{0:T(512)(128)(4,1)S(1)}, pred[130]{0:T(512)(128)(4,1)}, u32[]{:S(2)}) copy-start(pred[130]{0:T(512)(128)(4,1)} %compare_and_fusion.9) | copy-start | bytes 394

commit v2 on v1

--- a/solution.py
+++ b/solution.py
@@ -24,11 +24,21 @@
     return from_prev, from_next
 
 
+def exchange_x(fields, width):
+    return exchange(fields[:, :width], fields[:, -width:], "gx")
+
+
 def with_wide_halo(fields, width):
-    prev, nxt = exchange(fields[:, :width], fields[:, -width:], "gx")
-    fields = jnp.concatenate([prev, fields, nxt], axis=1)
-    prev, nxt = exchange(fields[:, :, :width], fields[:, :, -width:], "gy")
-    fields = jnp.concatenate([prev, fields, nxt], axis=2)
+    nf, nx, ny, nz = fields.shape
+
+    def pack_y(a):
+        return a.reshape(nf * nx * width, nz)
+
+    def unpack_y(a):
+        return a.reshape(nf, nx, width, nz)
+
+    prev, nxt = exchange(pack_y(fields[:, :, :width]), pack_y(fields[:, :, -width:]), "gy")
+    fields = jnp.concatenate([unpack_y(prev), fields, unpack_y(nxt)], axis=2)
     nf, nx, ny, _ = fields.shape
 
     def pack(a):
@@ -120,16 +130,36 @@
     volt_recv = recv[:, cells_z]
     column_recv = recv[:, cells_z + 1].astype(jnp.int32)
     extra_recv = cond_recv * volt_recv[:, None]
-    empty = jnp.zeros((cells_x * cells_y, 2, cells_z), jnp.float32)
-    summed = empty.at[column_recv].add(jnp.stack([cond_recv, extra_recv], axis=1))
-    coupling = summed[:, 0].reshape(cells_x, cells_y, cells_z)
-    injected = summed[:, 1].reshape(cells_x, cells_y, cells_z)
+    columns = jnp.arange(cells_x * cells_y, dtype=jnp.int32)
+    one_hot = (columns[:, None] == column_recv[None, :]).astype(jnp.float32)
+    summed = jnp.dot(
+        one_hot,
+        jnp.concatenate([cond_recv, extra_recv], axis=1),
+        precision=lax.Precision.HIGHEST,
+        preferred_element_type=jnp.float32,
+    )
+    coupling = summed[:, :cells_z].reshape(cells_x, cells_y, cells_z)
+    injected = summed[:, cells_z:].reshape(cells_x, cells_y, cells_z)
     forcing = charge + injected
 
     halo = SWEEPS + 1
-    fields = jnp.stack([permittivity, forcing, coupling, initial], axis=0)
-    wide = with_wide_halo(fields, halo)
-    eps_w, forcing_w, coupling_w, potential = wide[0], wide[1], wide[2], wide[3]
+    early = jnp.stack([permittivity, initial], axis=0)
+    early_prev, early_next = exchange_x(early, halo)
+    late = jnp.stack([forcing, coupling], axis=0)
+    late_prev, late_next = exchange_x(late, halo - 1)
+    pad = jnp.zeros((2, 1, cells_y, cells_z), jnp.float32)
+    late_prev = jnp.concatenate([pad, late_prev], axis=1)
+    late_next = jnp.concatenate([late_next, pad], axis=1)
+    fields_x = jnp.concatenate(
+        [
+            jnp.concatenate([early_prev, early, early_next], axis=1),
+            jnp.concatenate([late_prev, late, late_next], axis=1),
+        ],
+        axis=0,
+    )
+    wide = with_wide_halo(fields_x, halo)
+    eps_w, initial_w, forcing_w, coupling_w = wide[0], wide[1], wide[2], wide[3]
+    potential = initial_w
 
     coefficients = face_coefficients(eps_w)
     diagonal_sum = coefficients[0]

time: 177 us -> 142 us (0.80)
  other arithmetic: 44.8 us -> 26.4 us
  waiting for transfers between devices: 36.9 us -> 29.4 us
  starting transfers between devices: 46 us -> 40.2 us
  blocking collectives: 33.3 us -> 30 us
    scatter-add x1 -> x0, other arithmetic: 17.7 us -> none  [on_device(): empty.at[column_recv].add(jnp.stack([cond_recv, extra_recv], axis=1))]
    ppermute x3 -> x4, starting transfers between devices: 23.1 us -> 15.4 us  [exchange(): from_prev = lax.ppermute(hi, axis, forward)]
    all_to_all x1, waiting for transfers between devices: 13.6 us -> 6.11 us  [on_device(): lax.all_to_all(send, ('gx', 'gy'), split_axis=0, concat_axis=0, tiled=True)]
    ppermute x3 -> x4, waiting for transfers between devices: 6.82 us -> 1.21 us  [exchange(): from_prev = lax.ppermute(hi, axis, forward)]
    ppermute x3 -> x4, waiting for transfers between devices: 16.6 us -> 22.1 us  [exchange(): from_next = lax.ppermute(lo, axis, backward)]
    all_to_all x1, blocking collectives: 33.3 us -> 30 us  [on_device(): lax.all_to_all(jnp.full((device_count,), local_total), ('gx', 'gy', 'gz')...]
    ppermute x3 -> x4, starting transfers between devices: 4.5 us -> 6.47 us  [exchange(): from_next = lax.ppermute(lo, axis, backward)]
  transfers between devices with their start and end apart: 7 -> 9, of which waited for: 6 -> 5; matrix products, arithmetic and copies ran while one was open for 3% -> 5% of each run, Pallas kernels for 0% -> 0%
where the time goes in v2:
time: 142 us
  starting transfers between devices  40.2 us (28%)
  blocking collectives  30 us (21%)
  waiting for transfers between devices  29.4 us (21%)
  other arithmetic  26.4 us (19%)
  local copies, waits for them, and re-layouts  12.3 us (9%)
  between operations  2.98 us (2%)
    all_to_all x1, blocking collectives, on_device(): lax.all_to_all(jnp.full((device_count,), local_total), ('gx', 'gy', 'gz')...  30 us
    ppermute x4, waiting for transfers between devices, exchange(): from_next = lax.ppermute(lo, axis, backward)  22.1 us
    all_to_all x1, starting transfers between devices, on_device(): lax.all_to_all(send, ('gx', 'gy'), split_axis=0, concat_axis=0, tiled=True)  18.4 us
    ppermute x4, starting transfers between devices, exchange(): from_prev = lax.ppermute(hi, axis, forward)  15.4 us
    select_n x4, other arithmetic, on_device(): updated = jnp.where(inside_mask(k), updated, 0.0)  8.47 us
    ppermute x4, starting transfers between devices, exchange(): from_next = lax.ppermute(lo, axis, backward)  6.47 us
    all_to_all x1, waiting for transfers between devices, on_device(): lax.all_to_all(send, ('gx', 'gy'), split_axis=0, concat_axis=0, tiled=True)  6.11 us
    concatenate x1, other arithmetic, with_wide_halo(): return jnp.concatenate([unpack(prev), fields, unpack(nxt)], axis=3)  4.81 us
  transfers between devices with their start and end apart: 9, of which 5 were waited for; matrix products, arithmetic and copies ran while one was open for 5% of the time, Pallas kernels for 0%

profile of v2, /device:TPU:1, one launch (start us, length us, event | category | flops | bytes accessed | tf_op | source)
XLA Modules:
  0.0 141.8 jit_solution(9880228840118210638)
XLA Ops:
  0.7 0.0 copy-start.3
  0.7 0.9 select_reduce_fusion
  1.6 0.1 copy.34
  1.7 0.7 convert_bitcast_fusion
  2.4 0.1 copy.35
  2.5 0.9 convert_reduce_fusion
  3.4 0.7 compare_select_fusion
  4.1 1.5 %scatter_custom_fusion = f32[512,130]{1,0:T(8,128)S(1)} fusion(s32[128]{0:T(128)S(1)} %compare_select_fusion, f32[]{:T(128)} %constant.36.clone.1, f32[128,1]{1,0:T(8,128)S(1)} %copy.35, f32[]{:T(128)} %constant.49, f32[128,1]{1,0:T(8,128)S(1)} %copy.34, f32[128,128]{1,0:T(8,128)} %param.15), kind=kCustom, calls=%fused_computation.108 | custom fusion | flops 33280 | bytes 462856 | tf_op jit(solution)/shard_map/scatter | solution.py:125
  5.6 1.4 all_to_all.13
  7.0 18.4 %all-to-all-start = ((f32[128,1,520]{2,1,0:T(1,128)}), f32[128,1,520]{2,1,0:T(1,128)S(1)}, u32[]{:S(2)}, u32[]{:S(2)}) async-start(f32[128,1,520]{2,1,0:T(1,128)} %all_to_all.13), calls=%async_computation | async-start | bytes 655360 | tf_op jit(solution)/shard_map/all_to_all | solution.py:127
  25.4 0.1 select_reduce_fusion.1
  25.5 0.0 copy-start.1
  25.6 7.2 %collective-permute-start = (f32[2,5,32,128]{3,2,1,0:T(8,128)S(1)}, f32[2,5,32,128]{3,2,1,0:T(8,128)S(1)}, u32[]{:S(2)}, u32[]{:S(2)}) collective-permute-start(f32[2,5,32,128]{3,2,1,0:T(8,128)S(1)} %get-tuple-element.21), channel_id=1, source_target_pairs={{0,32},{32,64},{64,96},{96,128},{128,160},{160,192},{192,224},{224... | collective-permute-start | bytes 491528 | tf_op jit(solution)/shard_map/ppermute | solution.py:22
  32.8 1.3 collective-permute-start.1
  34.1 0.5 compare_and_fusion
  34.7 0.6 compare_and_fusion.3
  35.2 0.6 compare_and_fusion.6
  35.8 0.1 broadcast_and_fusion
  35.9 0.1 broadcast_and_fusion.1
  36.0 0.1 broadcast_and_fusion.2
  36.1 6.1 %all-to-all-done = f32[128,1,520]{2,1,0:T(1,128)S(1)} async-done(((f32[128,1,520]{2,1,0:T(1,128)}), f32[128,1,520]{2,1,0:T(1,128)S(1)}, u32[]{:S(2)}, u32[]{:S(2)}) %all-to-all-start) | async-done | bytes 266272 | tf_op jit(solution)/shard_map/all_to_all | solution.py:127
  42.2 0.8 reduce.1
  43.0 0.0 copy-start.6
  43.0 0.3 reshape.266
  43.2 0.1 slice_reduce_fusion
  43.4 0.2 fusion.42
  43.6 0.1 fusion.65
  43.8 0.5 fusion.19
  44.3 3.1 %collective-permute-start.2 = (f32[2,4,32,128]{3,2,1,0:T(8,128)S(1)}, f32[2,4,32,128]{3,2,1,0:T(8,128)S(1)}, u32[]{:S(2)}, u32[]{:S(2)}) collective-permute-start(f32[2,4,32,128]{3,2,1,0:T(8,128)S(1)} %get-tuple-element.24), channel_id=1, source_target_pairs={{0,32},{32,64},{64,96},{96,128},{128,160},{160,192},{192,224},{224... | collective-permute-start | bytes 393224 | tf_op jit(solution)/shard_map/ppermute | solution.py:22
  47.5 1.3 collective-permute-start.3
  48.8 1.2 collective-permute-done.2
  50.0 15.5 %collective-permute-done.3 = f32[2,4,32,128]{3,2,1,0:T(8,128)S(1)} collective-permute-done((f32[2,4,32,128]{3,2,1,0:T(8,128)S(1)}, f32[2,4,32,128]{3,2,1,0:T(8,128)S(1)}, u32[]{:S(2)}, u32[]{:S(2)}) %collective-permute-start.3) | collective-permute-done | bytes 131104 | tf_op jit(solution)/shard_map/ppermute | solution.py:23
  65.7 1.9 %collective-permute-start.4 = (f32[360,128]{1,0:T(8,128)S(1)}, f32[360,128]{1,0:T(8,128)S(1)}, u32[]{:S(2)}, u32[]{:S(2)}) collective-permute-start(f32[360,128]{1,0:T(8,128)S(1)} %reshape.268), channel_id=1, source_target_pairs={{0,4},{4,8},{8,12},{12,16},{16,20},{20,24},{24,28},{1,5},{5,9},{9,... | collective-permute-start | bytes 552968 | tf_op jit(solution)/shard_map/ppermute | solution.py:22
  67.7 2.4 %collective-permute-start.5 = (f32[360,128]{1,0:T(8,128)S(1)}, f32[360,128]{1,0:T(8,128)S(1)}, u32[]{:S(2)}, u32[]{:S(2)}) collective-permute-start(f32[360,128]{1,0:T(8,128)S(1)} %reshape.270), channel_id=1, source_target_pairs={{4,0},{8,4},{12,8},{16,12},{20,16},{24,20},{28,24},{5,1},{9,5},{13... | collective-permute-start | bytes 552968 | tf_op jit(solution)/shard_map/ppermute | solution.py:23
  70.1 0.1 broadcast_and_fusion.3
  70.2 4.3 %collective-permute-done.5 = f32[360,128]{1,0:T(8,128)S(1)} collective-permute-done((f32[360,128]{1,0:T(8,128)S(1)}, f32[360,128]{1,0:T(8,128)S(1)}, u32[]{:S(2)}, u32[]{:S(2)}) %collective-permute-start.5) | collective-permute-done | bytes 184352 | tf_op jit(solution)/shard_map/ppermute | solution.py:23
  74.5 0.7 reshape.271
  75.3 1.2 pad_maximum_fusion.1
  76.5 0.6 slice_bitcast_fusion.1
  77.1 1.6 %copy.37 = f32[4,5,18,42]{3,2,1,0:T(8,128)} copy(f32[4,5,18,42]{1,3,2,0:T(8,128)S(1)} %get-tuple-element.15) | data formatting | bytes 120960 | tf_op jit(solution)/shard_map/transpose | solution.py:45
  78.7 1.1 reshape.272
  79.8 3.1 %collective-permute-start.6 = (f32[20,756]{1,0:T(8,128)S(1)}, f32[20,756]{1,0:T(8,128)S(1)}, u32[]{:S(2)}, u32[]{:S(2)}) collective-permute-start(f32[20,756]{1,0:T(8,128)S(1)} %reshape.272), channel_id=1, source_target_pairs={{0,1},{1,2},{2,3},{4,5},{5,6},{6,7},{8,9},{9,10},{10,11},{12,13},{... | collective-permute-start | bytes 181448 | tf_op jit(solution)/shard_map/ppermute | solution.py:22
  82.9 0.9 copy.38
  83.8 0.1 reshape.274
  83.9 1.5 %collective-permute-start.7 = (f32[20,756]{1,0:T(8,128)S(1)}, f32[20,756]{1,0:T(8,128)S(1)}, u32[]{:S(2)}, u32[]{:S(2)}) collective-permute-start(f32[20,756]{1,0:T(8,128)S(1)} %reshape.274), channel_id=1, source_target_pairs={{1,0},{2,1},{3,2},{5,4},{6,5},{7,6},{9,8},{10,9},{11,10},{13,12},{... | collective-permute-start | bytes 181448 | tf_op jit(solution)/shard_map/ppermute | solution.py:23
  85.4 0.5 compare_and_fusion.9
  85.9 0.1 reshape.273
  86.0 0.8 copy.39
  86.8 2.2 %collective-permute-done.7 = f32[20,756]{1,0:T(8,128)S(1)} collective-permute-done((f32[20,756]{1,0:T(8,128)S(1)}, f32[20,756]{1,0:T(8,128)S(1)}, u32[]{:S(2)}, u32[]{:S(2)}) %collective-permute-start.7) | collective-permute-done | bytes 60512 | tf_op jit(solution)/shard_map/ppermute | solution.py:23
  89.0 0.8 reshape.275
  89.8 1.7 %copy.40 = f32[4,18,42,5]{3,2,1,0:T(8,128)S(1)} copy(f32[4,18,42,5]{2,1,3,0:T(8,128)} %bitcast.31) | data formatting | bytes 120960 | tf_op jit(solution)/shard_map/transpose | solution.py:48
  91.5 4.8 %pad_maximum_fusion = f32[4,18,42,138]{3,2,1,0:T(8,128)S(1)} fusion(f32[4,18,42,5]{3,2,1,0:T(8,128)S(1)} %copy.40, f32[4,18,5,128]{3,2,1,0:T(8,128)} %reshape.271, f32[2,18,32,128]{3,2,1,0:T(8,128)} %copy-done, f32[2,5,32,128]{3,2,1,0:T(8,128)} %copy-done.5, f32[1,8,32,128]{3,2,1,0:T(8,128)} %bitcast.24, f32[1,8,32,128]{3,2,1,0:T(8,128)} %copy-done.1, ...), kind=kLoop, calls=%fused_computation.1 | loop fusion | flops 3338496 | bytes 3338496 | tf_op jit(solution)/shard_map/concatenate | solution.py:51
  96.4 0.3 slice_bitcast_fusion.3
  96.7 0.3 copy-done.8
  97.0 2.7 %fusion.5 = (f32[16,40,136]{2,1,0:T(8,128)S(1)}, f32[16,40,136]{2,1,0:T(8,128)S(1)}, f32[16,40,136]{2,1,0:T(8,128)S(1)}, f32[16,40,136]{2,1,0:T(8,128)S(1)}, f32...) fusion(f32[18,42,138]{2,1,0:T(8,128)S(1)} %get-tuple-element.14, ...), kind=kLoop, calls=%fused_computation.16 | loop fusion | flops 3742720 | bytes 8008456 | tf_op jit(solution)/shard_map/jit(_where)/select_n | solution.py:192
  99.7 0.3 slice_add_fusion
  100.1 0.3 copy-done.11
  100.4 2.2 %fusion.11 = f32[14,38,134]{2,1,0:T(8,128)S(1)} fusion(f32[16,40,136]{2,1,0:T(8,128)S(1)} %slice_add_fusion, f32[16,40,136]{2,1,0:T(8,128)S(1)} %get-tuple-element.4, f32[16,40,136]{2,1,0:T(8,128)S(1)} %get-tuple-element.10, f32[16,40,136]{2,1,0:T(8,128)S(1)} %get-tuple-element.9, f32[16,40,136]{2,1,0:T(8,128)S(1)} %get-tuple-element.8, ...), kind=kLoop, calls=%fused_computation.35 | loop fusion | flops 1283184 | bytes 4563098 | tf_op jit(solution)/shard_map/jit(_where)/select_n | solution.py:192
  102.6 1.9 %fusion.24 = f32[12,36,132]{2,1,0:T(8,128)S(1)} fusion(f32[16,40,136]{2,1,0:T(8,128)S(1)} %slice_add_fusion, f32[14,38,134]{2,1,0:T(8,128)S(1)} %fusion.11, f32[16,40,136]{2,1,0:T(8,128)S(1)} %get-tuple-element.10, f32[16,40,136]{2,1,0:T(8,128)S(1)} %get-tuple-element.9, f32[16,40,136]{2,1,0:T(8,128)S(1)} %get-tuple-element.8, ...), kind=kLoop, calls=%fused_computation.59 | loop fusion | flops 1026432 | bytes 3650100 | tf_op jit(solution)/shard_map/jit(_where)/select_n | solution.py:192
  104.6 1.6 %fusion.33 = f32[10,34,130]{2,1,0:T(8,128)S(1)} fusion(f32[16,40,136]{2,1,0:T(8,128)S(1)} %slice_add_fusion, f32[12,36,132]{2,1,0:T(8,128)S(1)} %fusion.24, f32[16,40,136]{2,1,0:T(8,128)S(1)} %get-tuple-element.10, f32[16,40,136]{2,1,0:T(8,128)S(1)} %get-tuple-element.9, f32[16,40,136]{2,1,0:T(8,128)S(1)} %get-tuple-element.8, ...), kind=kLoop, calls=%fused_computation.76 | loop fusion | flops 795600 | bytes 2829270 | tf_op jit(solution)/shard_map/jit(_where)/select_n | solution.py:192
  106.2 1.8 %fusion.51 = (f32[]{:T(128)}, f32[8,32,128]{2,1,0:T(8,128)}) fusion(f32[16,40,136]{2,1,0:T(8,128)S(1)} %slice_add_fusion, f32[10,34,130]{2,1,0:T(8,128)S(1)} %fusion.33, f32[16,40,136]{2,1,0:T(8,128)S(1)} %get-tuple-element.10, f32[16,40,136]{2,1,0:T(8,128)S(1)} %get-tuple-element.9, f32[16,40,136]{2,1,0:T(8,128)S(1)} %get-tuple-element.8, ...), kind=kLoop, calls=%fused_computation.117 | loop fusion | flops 524287 | bytes 2097156 | tf_op jit(solution)/shard_map/reduce_sum | solution.py:200
  108.0 0.8 broadcast_in_dim.96
  108.8 30.0 %all_to_all.16 = f32[512,1,1]{2,1,0:T(1,128)S(1)} all-to-all(f32[512,1,1]{2,1,0:T(1,128)S(1)} %broadcast_in_dim.96), channel_id=1, replica_groups=mesh['gx'=16,'gy'=8,'gz'=4] {'gx','gy','gz'}, dimensions={0} | all-to-all | bytes 4096 | tf_op jit(solution)/shard_map/all_to_all | solution.py:202
  138.8 1.1 reduce_sum.49
  (49 shorter events, 0.4 us)
Async XLA Ops:
  0.6 24.8 %copy-start.12 = (f32[6]{0:T(128)S(1)}, f32[6]{0:T(128)}, u32[]{:S(2)}) copy-start(f32[6]{0:T(128)} %param.12) | copy-start | bytes 76
  0.6 24.8 %copy-start.13 = (s32[128]{0:T(128)S(1)}, s32[128]{0:T(128)}, u32[]{:S(2)}) copy-start(s32[128]{0:T(128)} %param.13) | copy-start | bytes 1540
  0.7 24.9 %copy-start.7 = (f32[8,32,128]{2,1,0:T(8,128)S(1)}, f32[8,32,128]{2,1,0:T(8,128)}, u32[]{:S(2)}) copy-start(f32[8,32,128]{2,1,0:T(8,128)} %param.11) | copy-start | bytes 393220
  0.7 24.9 %copy-start.3 = (f32[8,32,128]{2,1,0:T(8,128)S(1)}, f32[8,32,128]{2,1,0:T(8,128)}, u32[]{:S(2)}) copy-start(f32[8,32,128]{2,1,0:T(8,128)} %param.19) | copy-start | bytes 393220
  7.0 35.2 %all-to-all-start = ((f32[128,1,520]{2,1,0:T(1,128)}), f32[128,1,520]{2,1,0:T(1,128)S(1)}, u32[]{:S(2)}, u32[]{:S(2)}) async-start(f32[128,1,520]{2,1,0:T(1,128)} %all_to_all.13), calls=%async_computation | async-start | bytes 655360 | tf_op jit(solution)/shard_map/all_to_all | solution.py:127
  25.5 49.8 %copy-start.1 = (f32[1,8,32,128]{3,2,1,0:T(8,128)}, f32[1,8,32,128]{3,2,1,0:T(8,128)S(1)}, u32[]{:S(2)}) copy-start(f32[1,8,32,128]{3,2,1,0:T(8,128)S(1)} %multiply_bitcast_fusion) | copy-start | bytes 393220
  25.6 40.0 %collective-permute-start = (f32[2,5,32,128]{3,2,1,0:T(8,128)S(1)}, f32[2,5,32,128]{3,2,1,0:T(8,128)S(1)}, u32[]{:S(2)}, u32[]{:S(2)}) collective-permute-start(f32[2,5,32,128]{3,2,1,0:T(8,128)S(1)} %get-tuple-element.21), channel_id=1, source_target_pairs={{0,32},{32,64},{64,96},{96,128},{128,160},{160,192},{192,224},{224... | collective-permute-start | bytes 491528 | tf_op jit(solution)/shard_map/ppermute | solution.py:22
  32.8 32.8 %collective-permute-start.1 = (f32[2,5,32,128]{3,2,1,0:T(8,128)S(1)}, f32[2,5,32,128]{3,2,1,0:T(8,128)S(1)}, u32[]{:S(2)}, u32[]{:S(2)}) collective-permute-start(f32[2,5,32,128]{3,2,1,0:T(8,128)S(1)} %get-tuple-element.22), channel_id=1, source_target_pairs={{32,0},{64,32},{96,64},{128,96},{160,128},{192,160},{224,192},{256... | collective-permute-start | bytes 491528 | tf_op jit(solution)/shard_map/ppermute | solution.py:23
  43.0 1.3 copy-start.6
  44.3 5.7 %collective-permute-start.2 = (f32[2,4,32,128]{3,2,1,0:T(8,128)S(1)}, f32[2,4,32,128]{3,2,1,0:T(8,128)S(1)}, u32[]{:S(2)}, u32[]{:S(2)}) collective-permute-start(f32[2,4,32,128]{3,2,1,0:T(8,128)S(1)} %get-tuple-element.24), channel_id=1, source_target_pairs={{0,32},{32,64},{64,96},{96,128},{128,160},{160,192},{192,224},{224... | collective-permute-start | bytes 393224 | tf_op jit(solution)/shard_map/ppermute | solution.py:22
  47.5 18.1 %collective-permute-start.3 = (f32[2,4,32,128]{3,2,1,0:T(8,128)S(1)}, f32[2,4,32,128]{3,2,1,0:T(8,128)S(1)}, u32[]{:S(2)}, u32[]{:S(2)}) collective-permute-start(f32[2,4,32,128]{3,2,1,0:T(8,128)S(1)} %get-tuple-element.23), channel_id=1, source_target_pairs={{32,0},{64,32},{96,64},{128,96},{160,128},{192,160},{224,192},{256... | collective-permute-start | bytes 393224 | tf_op jit(solution)/shard_map/ppermute | solution.py:23
  65.6 9.7 %copy-start = (f32[2,18,32,128]{3,2,1,0:T(8,128)}, f32[2,18,32,128]{3,2,1,0:T(8,128)S(1)}, u32[]{:S(2)}) copy-start(f32[2,18,32,128]{3,2,1,0:T(8,128)S(1)} %broadcast_dynamic-update-slice_fusion.1) | copy-start | bytes 1769476
  65.6 9.7 %copy-start.4 = (f32[2,5,32,128]{3,2,1,0:T(8,128)}, f32[2,5,32,128]{3,2,1,0:T(8,128)S(1)}, u32[]{:S(2)}) copy-start(f32[2,5,32,128]{3,2,1,0:T(8,128)S(1)} %collective-permute-done) | copy-start | bytes 491524
  65.6 9.7 %copy-start.5 = (f32[2,5,32,128]{3,2,1,0:T(8,128)}, f32[2,5,32,128]{3,2,1,0:T(8,128)S(1)}, u32[]{:S(2)}) copy-start(f32[2,5,32,128]{3,2,1,0:T(8,128)S(1)} %collective-permute-done.1) | copy-start | bytes 491524
  65.7 4.5 %collective-permute-start.4 = (f32[360,128]{1,0:T(8,128)S(1)}, f32[360,128]{1,0:T(8,128)S(1)}, u32[]{:S(2)}, u32[]{:S(2)}) collective-permute-start(f32[360,128]{1,0:T(8,128)S(1)} %reshape.268), channel_id=1, source_target_pairs={{0,4},{4,8},{8,12},{12,16},{16,20},{20,24},{24,28},{1,5},{5,9},{9,... | collective-permute-start | bytes 552968 | tf_op jit(solution)/shard_map/ppermute | solution.py:22
  67.7 6.9 %collective-permute-start.5 = (f32[360,128]{1,0:T(8,128)S(1)}, f32[360,128]{1,0:T(8,128)S(1)}, u32[]{:S(2)}, u32[]{:S(2)}) collective-permute-start(f32[360,128]{1,0:T(8,128)S(1)} %reshape.270), channel_id=1, source_target_pairs={{4,0},{8,4},{12,8},{16,12},{20,16},{24,20},{28,24},{5,1},{9,5},{13... | collective-permute-start | bytes 552968 | tf_op jit(solution)/shard_map/ppermute | solution.py:23
  70.2 5.1 %copy-start.2 = (f32[4,18,5,128]{3,2,1,0:T(8,128)}, f32[4,18,5,128]{3,2,1,0:T(8,128)S(1)}, u32[]{:S(2)}) copy-start(f32[4,18,5,128]{3,2,1,0:T(8,128)S(1)} %reshape.269) | copy-start | bytes 552964
  79.8 6.1 %collective-permute-start.6 = (f32[20,756]{1,0:T(8,128)S(1)}, f32[20,756]{1,0:T(8,128)S(1)}, u32[]{:S(2)}, u32[]{:S(2)}) collective-permute-start(f32[20,756]{1,0:T(8,128)S(1)} %reshape.272), channel_id=1, source_target_pairs={{0,1},{1,2},{2,3},{4,5},{5,6},{6,7},{8,9},{9,10},{10,11},{12,13},{... | collective-permute-start | bytes 181448 | tf_op jit(solution)/shard_map/ppermute | solution.py:22
  83.9 5.1 %collective-permute-start.7 = (f32[20,756]{1,0:T(8,128)S(1)}, f32[20,756]{1,0:T(8,128)S(1)}, u32[]{:S(2)}, u32[]{:S(2)}) collective-permute-start(f32[20,756]{1,0:T(8,128)S(1)} %reshape.274), channel_id=1, source_target_pairs={{1,0},{2,1},{3,2},{5,4},{6,5},{7,6},{9,8},{10,9},{11,10},{13,12},{... | collective-permute-start | bytes 181448 | tf_op jit(solution)/shard_map/ppermute | solution.py:23
  96.4 0.7 copy-start.8
  99.7 0.7 copy-start.11
  100.4 2.2 %copy-start.9 = (pred[132]{0:T(512)(128)(4,1)S(1)}, pred[132]{0:T(512)(128)(4,1)}, u32[]{:S(2)}) copy-start(pred[132]{0:T(512)(128)(4,1)} %compare_and_fusion.6) | copy-start | bytes 400
  102.6 1.9 %copy-start.10 = (pred[130]{0:T(512)(128)(4,1)S(1)}, pred[130]{0:T(512)(128)(4,1)}, u32[]{:S(2)}) copy-start(pred[130]{0:T(512)(128)(4,1)} %compare_and_fusion.9) | copy-start | bytes 394

commit v3 on v2

--- a/solution.py
+++ b/solution.py
@@ -103,15 +103,36 @@
     peer_count = grid_x * grid_y
     block_count = block_dest.shape[0]
     capacity = max(2, 4 * block_count // peer_count)
-    slot_total = peer_count * capacity
     layer_eps = table_lookup(material_eps, layer_material)
     permittivity = texture * layer_eps[None, None, :]
 
+    halo = SWEEPS + 1
+    reach = halo - 1
+    early = jnp.stack([permittivity, initial, charge], axis=0)
+    early_prev, early_next = exchange_x(early, halo)
+    early_x = jnp.concatenate([early_prev, early, early_next], axis=1)
+
+    roles = 3
     same_dest = block_dest[:, None] == block_dest[None, :]
     order = jnp.arange(block_count, dtype=jnp.int32)
     earlier = order[None, :] < order[:, None]
     slot_rank = jnp.sum((same_dest & earlier).astype(jnp.int32), axis=1)
-    position = block_dest * capacity + slot_rank
+    owner_x = block_dest // grid_y
+    column_x = block_column // cells_y
+    slot_total = peer_count * roles * capacity
+    to_next = (column_x >= cells_x - reach) & (owner_x + 1 < grid_x)
+    to_prev = (column_x < reach) & (owner_x > 0)
+    position = jnp.concatenate(
+        [
+            block_dest * (roles * capacity) + slot_rank,
+            jnp.where(
+                to_next, (block_dest + grid_y) * (roles * capacity) + capacity + slot_rank, slot_total
+            ),
+            jnp.where(
+                to_prev, (block_dest - grid_y) * (roles * capacity) + 2 * capacity + slot_rank, slot_total
+            ),
+        ]
+    )
     block_volts = table_lookup(gate_volts, block_gate)
     rows = jnp.concatenate(
         [
@@ -121,39 +142,38 @@
         ],
         axis=1,
     )
+    rows = jnp.concatenate([rows, rows, rows], axis=0)
     width_row = cells_z + 2
-    send = jnp.zeros((slot_total, width_row), jnp.float32).at[position].set(rows)
-    send = send.reshape(peer_count, capacity * width_row)
+    send = jnp.zeros((slot_total, width_row), jnp.float32).at[position].set(rows, mode="drop")
+    send = send.reshape(peer_count, roles * capacity * width_row)
     recv = lax.all_to_all(send, ("gx", "gy"), split_axis=0, concat_axis=0, tiled=True)
     recv = recv.reshape(slot_total, width_row)
     cond_recv = recv[:, :cells_z]
     volt_recv = recv[:, cells_z]
     column_recv = recv[:, cells_z + 1].astype(jnp.int32)
     extra_recv = cond_recv * volt_recv[:, None]
-    columns = jnp.arange(cells_x * cells_y, dtype=jnp.int32)
-    one_hot = (columns[:, None] == column_recv[None, :]).astype(jnp.float32)
+    role_recv = (jnp.arange(slot_total, dtype=jnp.int32) // capacity) % roles
+    shift = jnp.where(role_recv == 1, -cells_x, jnp.where(role_recv == 2, cells_x, 0))
+    ext_x = column_recv // cells_y + shift + reach
+    ext_column = ext_x * cells_y + column_recv % cells_y
+    ext_cells = cells_x + 2 * reach
+    columns = jnp.arange(ext_cells * cells_y, dtype=jnp.int32)
+    one_hot = (columns[:, None] == ext_column[None, :]).astype(jnp.float32)
     summed = jnp.dot(
         one_hot,
         jnp.concatenate([cond_recv, extra_recv], axis=1),
         precision=lax.Precision.HIGHEST,
         preferred_element_type=jnp.float32,
     )
-    coupling = summed[:, :cells_z].reshape(cells_x, cells_y, cells_z)
-    injected = summed[:, cells_z:].reshape(cells_x, cells_y, cells_z)
-    forcing = charge + injected
-
-    halo = SWEEPS + 1
-    early = jnp.stack([permittivity, initial], axis=0)
-    early_prev, early_next = exchange_x(early, halo)
-    late = jnp.stack([forcing, coupling], axis=0)
-    late_prev, late_next = exchange_x(late, halo - 1)
-    pad = jnp.zeros((2, 1, cells_y, cells_z), jnp.float32)
-    late_prev = jnp.concatenate([pad, late_prev], axis=1)
-    late_next = jnp.concatenate([late_next, pad], axis=1)
+    coupling_x = summed[:, :cells_z].reshape(ext_cells, cells_y, cells_z)
+    injected_x = summed[:, cells_z:].reshape(ext_cells, cells_y, cells_z)
+    forcing_x = early_x[2, 1:-1] + injected_x
+    pad = jnp.zeros((1, cells_y, cells_z), jnp.float32)
     fields_x = jnp.concatenate(
         [
-            jnp.concatenate([early_prev, early, early_next], axis=1),
-            jnp.concatenate([late_prev, late, late_next], axis=1),
+            early_x[:2],
+            jnp.concatenate([pad, forcing_x, pad], axis=0)[None],
+            jnp.concatenate([pad, coupling_x, pad], axis=0)[None],
         ],
         axis=0,
     )

time: 142 us -> 164 us (1.15)
  local copies, waits for them, and re-layouts: 12.3 us -> 25.4 us
  blocking collectives: 30 us -> 33.5 us
  waiting for transfers between devices: 29.4 us -> 31.1 us
    ppermute x4 -> x3, waiting for transfers between devices: 1.21 us -> 26.7 us  [exchange(): from_prev = lax.ppermute(hi, axis, forward)]
    ppermute x4 -> x3, waiting for transfers between devices: 22.1 us -> 4.4 us  [exchange(): from_next = lax.ppermute(lo, axis, backward)]
    all_to_all x1, waiting for transfers between devices: 6.11 us -> 0.01 us  [on_device(): lax.all_to_all(send, ('gx', 'gy'), split_axis=0, concat_axis=0, tiled=True)]
    all_to_all x1, blocking collectives: 30 us -> 33.5 us  [on_device(): lax.all_to_all(jnp.full((device_count,), local_total), ('gx', 'gy', 'gz')...]
    transpose x3, local copies, waits for them, and re-layouts: 3.04 us -> 6.43 us  [pack(): return jnp.moveaxis(a, 3, 1).reshape(nf * width, nx * ny)]
    reshape x2, local copies, waits for them, and re-layouts: 0.96 us -> 3.42 us  [unpack(): return jnp.moveaxis(a.reshape(nf, width, nx, ny), 1, 3)]
    reshape x2, local copies, waits for them, and re-layouts: 1.19 us -> 3.39 us  [pack(): return jnp.moveaxis(a, 3, 1).reshape(nf * width, nx * ny)]
    transpose x2, local copies, waits for them, and re-layouts: 2.45 us -> 4.57 us  [unpack(): return jnp.moveaxis(a.reshape(nf, width, nx, ny), 1, 3)]
  transfers between devices with their start and end apart: 9 -> 7, of which waited for: 5 -> 3; matrix products, arithmetic and copies ran while one was open for 5% -> 6% of each run, Pallas kernels for 0% -> 0%
where the time goes in v3:
time: 164 us; the launch traced here: 163 us
  starting transfers between devices  40.7 us (25%)
  blocking collectives  33.5 us (20%)
  waiting for transfers between devices  31.1 us (19%)
  other arithmetic  27.7 us (17%)
  local copies, waits for them, and re-layouts  25.4 us (15%)
  between operations  2.92 us (2%)
  matrix products  1.78 us (1%)
    all_to_all x1, blocking collectives, on_device(): lax.all_to_all(jnp.full((device_count,), local_total), ('gx', 'gy', 'gz')...  33.5 us
    ppermute x3, waiting for transfers between devices, exchange(): from_prev = lax.ppermute(hi, axis, forward)  26.7 us
    all_to_all x1, starting transfers between devices, on_device(): lax.all_to_all(send, ('gx', 'gy'), split_axis=0, concat_axis=0, tiled=True)  18.4 us
    ppermute x3, starting transfers between devices, exchange(): from_prev = lax.ppermute(hi, axis, forward)  17.4 us
    select_n x4, other arithmetic, on_device(): updated = jnp.where(inside_mask(k), updated, 0.0)  8.47 us
    transpose x3, local copies, waits for them, and re-layouts, pack(): return jnp.moveaxis(a, 3, 1).reshape(nf * width, nx * ny)  6.43 us
    ppermute x3, starting transfers between devices, exchange(): from_next = lax.ppermute(lo, axis, backward)  4.89 us
    transpose x2, local copies, waits for them, and re-layouts, unpack(): return jnp.moveaxis(a.reshape(nf, width, nx, ny), 1, 3)  4.57 us
  transfers between devices with their start and end apart: 7, of which 3 were waited for; matrix products, arithmetic and copies ran while one was open for 6% of the time, Pallas kernels for 0%

profile of v3, /device:TPU:1, one launch (start us, length us, event | category | flops | bytes accessed | tf_op | source)
XLA Modules:
  0.0 163.2 jit_solution(16602890989053004853)
XLA Ops:
  0.6 0.9 convert_reduce_fusion
  1.5 0.7 fusion.91
  2.3 0.1 copy.35
  2.4 0.9 select_reduce_fusion
  3.3 0.1 copy.34
  3.4 0.7 add_bitcast_fusion
  4.1 2.7 %scatter_custom_fusion = f32[1536,130]{1,0:T(8,128)S(1)} fusion(s32[384]{0:T(512)S(1)} %fusion.90, f32[]{:T(128)} %constant.152.clone.1, f32[128,1]{1,0:T(8,128)S(1)} %copy.35, f32[]{:T(128)} %constant.179, f32[128,1]{1,0:T(8,128)S(1)} %copy.34, f32[128,128]{1,0:T(8,128)} %param.15), kind=kCustom, calls=%fused_computation.19 | custom fusion | flops 399360 | bytes 995336 | tf_op jit(solution)/shard_map/scatter | solution.py:147
  6.8 0.0 copy-start.11
  6.9 0.0 copy-start.12
  6.9 0.0 copy-start.6
  6.9 0.0 copy-start
  6.9 0.0 copy-start.1
  6.9 3.1 %all_to_all.13 = f32[128,1,1560]{2,1,0:T(1,128)} reshape(f32[1536,130]{1,0:T(8,128)S(1)} %scatter_custom_fusion) | data formatting | bytes 1597440 | tf_op jit(solution)/shard_map/all_to_all | solution.py:149
  10.0 18.4 %all-to-all-start = ((f32[128,1,1560]{2,1,0:T(1,128)}), f32[128,1,1560]{2,1,0:T(1,128)S(1)}, u32[]{:S(2)}, u32[]{:S(2)}) async-start(f32[128,1,1560]{2,1,0:T(1,128)} %all_to_all.13), calls=%async_computation | async-start | bytes 1703936 | tf_op jit(solution)/shard_map/all_to_all | solution.py:149
  28.4 0.1 select_reduce_fusion.1
  28.6 7.2 %collective-permute-start = (f32[3,5,32,128]{3,2,1,0:T(8,128)S(1)}, f32[3,5,32,128]{3,2,1,0:T(8,128)S(1)}, u32[]{:S(2)}, u32[]{:S(2)}) collective-permute-start(f32[3,5,32,128]{3,2,1,0:T(8,128)S(1)} %get-tuple-element.26), channel_id=1, source_target_pairs={{0,32},{32,64},{64,96},{96,128},{128,160},{160,192},{192,224},{224... | collective-permute-start | bytes 737288 | tf_op jit(solution)/shard_map/ppermute | solution.py:22
  35.8 1.5 collective-permute-start.1
  37.3 0.5 compare_and_fusion
  37.9 0.5 compare_and_fusion.3
  38.4 0.5 compare_and_fusion.6
  38.9 0.1 broadcast_and_fusion
  39.0 0.1 broadcast_and_fusion.1
  39.1 0.1 broadcast_and_fusion.2
  39.2 26.3 %collective-permute-done = f32[3,5,32,128]{3,2,1,0:T(8,128)S(1)} collective-permute-done((f32[3,5,32,128]{3,2,1,0:T(8,128)S(1)}, f32[3,5,32,128]{3,2,1,0:T(8,128)S(1)}, u32[]{:S(2)}, u32[]{:S(2)}) %collective-permute-start) | collective-permute-done | bytes 245792 | tf_op jit(solution)/shard_map/ppermute | solution.py:22
  65.5 0.7 copy-done.2
  66.2 0.7 copy-done.4
  66.9 0.1 pad_maximum_fusion.2
  67.0 2.0 %reduce.2 = f32[128,1560]{1,0:T(8,128)S(1)} reduce(f32[128,1,1560]{2,1,0:T(1,128)S(1)} %all-to-all-done, f32[]{:T(128)} %constant.176), dimensions={1}, to_apply=%all_to_all.11.reduce_sub_computation | reduce | bytes 1597444 | tf_op jit(solution)/shard_map/all_to_all | solution.py:149
  69.0 0.7 reshape.442
  69.7 0.3 slice_reduce_fusion
  70.0 0.5 fusion.5
  70.5 0.3 fusion.94
  70.8 1.8 %fusion = f32[512,256]{1,0:T(8,128)S(1)} fusion(f32[1536,128]{1,0:T(8,128)S(1)} %get-tuple-element.21, f32[1536,128]{1,0:T(8,128)S(1)} %get-tuple-element.20, s32[1536]{0:T(1024)S(1)} %fusion.78), kind=kOutput, calls=%fused_computation.3 | convolution fusion | flops 2417098752 | bytes 2103296 | tf_op jit(solution)/shard_map/dot_general | solution.py:162
  72.9 6.5 %collective-permute-start.2 = (f32[360,128]{1,0:T(8,128)S(1)}, f32[360,128]{1,0:T(8,128)S(1)}, u32[]{:S(2)}, u32[]{:S(2)}) collective-permute-start(f32[360,128]{1,0:T(8,128)S(1)} %reshape.445), channel_id=1, source_target_pairs={{0,4},{4,8},{8,12},{12,16},{16,20},{20,24},{24,28},{1,5},{5,9},{9,... | collective-permute-start | bytes 552968 | tf_op jit(solution)/shard_map/ppermute | solution.py:22
  79.4 1.9 %collective-permute-start.3 = (f32[360,128]{1,0:T(8,128)S(1)}, f32[360,128]{1,0:T(8,128)S(1)}, u32[]{:S(2)}, u32[]{:S(2)}) collective-permute-start(f32[360,128]{1,0:T(8,128)S(1)} %reshape.447), channel_id=1, source_target_pairs={{4,0},{8,4},{12,8},{16,12},{20,16},{24,20},{28,24},{5,1},{9,5},{13... | collective-permute-start | bytes 552968 | tf_op jit(solution)/shard_map/ppermute | solution.py:23
  81.3 0.1 broadcast_and_fusion.3
  81.4 0.4 collective-permute-done.2
  81.8 4.4 %collective-permute-done.3 = f32[360,128]{1,0:T(8,128)S(1)} collective-permute-done((f32[360,128]{1,0:T(8,128)S(1)}, f32[360,128]{1,0:T(8,128)S(1)}, u32[]{:S(2)}, u32[]{:S(2)}) %collective-permute-start.3) | collective-permute-done | bytes 184352 | tf_op jit(solution)/shard_map/ppermute | solution.py:23
  86.3 0.3 pad_maximum_fusion.1
  86.5 1.8 %slice_bitcast_fusion.1 = (f32[4,5,18,42]{1,3,2,0:T(8,128)}, f32[4,5,18,42]{1,3,2,0:T(8,128)S(1)}) fusion(f32[4,18,42,128]{3,2,1,0:T(8,128)S(1)} %pad_maximum_fusion.1), kind=kLoop, calls=%fused_computation.5 | loop fusion | bytes 241920 | tf_op jit(solution)/shard_map/transpose | solution.py:45
  88.4 3.1 %copy.37 = f32[4,5,18,42]{3,2,1,0:T(8,128)} copy(f32[4,5,18,42]{1,3,2,0:T(8,128)} %get-tuple-element.18) | data formatting | bytes 120960 | tf_op jit(solution)/shard_map/transpose | solution.py:45
  91.4 1.7 %reshape.449 = f32[20,756]{1,0:T(8,128)} reshape(f32[4,5,18,42]{3,2,1,0:T(8,128)} %copy.37) | data formatting | bytes 120960 | tf_op jit(solution)/shard_map/reshape | solution.py:45
  93.1 3.7 %collective-permute-start.4 = (f32[20,756]{1,0:T(8,128)}, f32[20,756]{1,0:T(8,128)}, u32[]{:S(2)}, u32[]{:S(2)}) collective-permute-start(f32[20,756]{1,0:T(8,128)} %reshape.449), channel_id=1, source_target_pairs={{0,1},{1,2},{2,3},{4,5},{5,6},{6,7},{8,9},{9,10},{10,11},{12,13},{... | collective-permute-start | bytes 181448 | tf_op jit(solution)/shard_map/ppermute | solution.py:22
  96.8 1.6 copy.38
  98.4 1.7 %reshape.451 = f32[20,756]{1,0:T(8,128)} reshape(f32[4,5,18,42]{3,2,1,0:T(8,128)} %copy.38) | data formatting | bytes 120960 | tf_op jit(solution)/shard_map/reshape | solution.py:45
  100.1 1.5 collective-permute-start.5
  101.6 0.6 compare_and_fusion.9
  102.2 1.7 %reshape.450 = f32[4,5,18,42]{3,2,1,0:T(8,128)} reshape(f32[20,756]{1,0:T(8,128)} %collective-permute-done.4) | data formatting | bytes 120960 | tf_op jit(solution)/shard_map/reshape | solution.py:48
  103.9 1.7 %copy.39 = f32[4,18,42,5]{3,2,1,0:T(8,128)S(1)} copy(f32[4,18,42,5]{2,1,3,0:T(8,128)} %bitcast.45) | data formatting | bytes 120960 | tf_op jit(solution)/shard_map/transpose | solution.py:48
  105.6 1.7 %reshape.452 = f32[4,5,18,42]{3,2,1,0:T(8,128)} reshape(f32[20,756]{1,0:T(8,128)} %collective-permute-done.5) | data formatting | bytes 120960 | tf_op jit(solution)/shard_map/reshape | solution.py:48
  107.3 2.9 %copy.40 = f32[4,18,42,5]{3,2,1,0:T(8,128)} copy(f32[4,18,42,5]{2,1,3,0:T(8,128)} %bitcast.46) | data formatting | bytes 120960 | tf_op jit(solution)/shard_map/transpose | solution.py:48
  110.2 4.1 %pad_maximum_fusion = f32[4,18,42,138]{3,2,1,0:T(8,128)S(1)} fusion(f32[4,18,42,5]{3,2,1,0:T(8,128)} %copy.40, f32[4,18,5,128]{3,2,1,0:T(8,128)S(1)} %reshape.448, f32[1,18,32,128]{3,2,1,0:T(8,128)S(1)} %get-tuple-element.29, f32[1,18,32,128]{3,2,1,0:T(8,128)S(1)} %get-tuple-element.28, f32[2,18,32,128]{3,2,1,0:T(8,128)S(1)} %slice.378, ...), kind=kLoop, calls=%fused_computation.1 | loop fusion | flops 2503872 | bytes 3338496 | tf_op jit(solution)/shard_map/concatenate | solution.py:51
  114.3 0.3 slice_bitcast_fusion.3
  114.6 0.4 copy-done.7
  115.0 2.7 %fusion.13 = (f32[16,40,136]{2,1,0:T(8,128)S(1)}, f32[16,40,136]{2,1,0:T(8,128)S(1)}, f32[16,40,136]{2,1,0:T(8,128)S(1)}, f32[16,40,136]{2,1,0:T(8,128)S(1)}, f3...) fusion(f32[18,42,138]{2,1,0:T(8,128)S(1)} %get-tuple-element.17, ...), kind=kLoop, calls=%fused_computation.28 | loop fusion | flops 3742720 | bytes 8008456 | tf_op jit(solution)/shard_map/jit(_where)/select_n | solution.py:212
  117.7 0.3 slice_add_fusion
  118.0 0.2 copy-done.10
  118.3 2.2 %fusion.19 = f32[14,38,134]{2,1,0:T(8,128)S(1)} fusion(f32[16,40,136]{2,1,0:T(8,128)S(1)} %slice_add_fusion, f32[16,40,136]{2,1,0:T(8,128)S(1)} %get-tuple-element.4, f32[16,40,136]{2,1,0:T(8,128)S(1)} %get-tuple-element.10, f32[16,40,136]{2,1,0:T(8,128)S(1)} %get-tuple-element.9, f32[16,40,136]{2,1,0:T(8,128)S(1)} %get-tuple-element.8, ...), kind=kLoop, calls=%fused_computation.47 | loop fusion | flops 1283184 | bytes 4563098 | tf_op jit(solution)/shard_map/jit(_where)/select_n | solution.py:212
  120.5 1.9 %fusion.28 = f32[12,36,132]{2,1,0:T(8,128)S(1)} fusion(f32[16,40,136]{2,1,0:T(8,128)S(1)} %slice_add_fusion, f32[14,38,134]{2,1,0:T(8,128)S(1)} %fusion.19, f32[16,40,136]{2,1,0:T(8,128)S(1)} %get-tuple-element.10, f32[16,40,136]{2,1,0:T(8,128)S(1)} %get-tuple-element.9, f32[16,40,136]{2,1,0:T(8,128)S(1)} %get-tuple-element.8, ...), kind=kLoop, calls=%fused_computation.66 | loop fusion | flops 1026432 | bytes 3650100 | tf_op jit(solution)/shard_map/jit(_where)/select_n | solution.py:212
  122.5 1.6 fusion.37
  124.1 1.8 %fusion.67 = (f32[]{:T(128)}, f32[8,32,128]{2,1,0:T(8,128)}) fusion(f32[16,40,136]{2,1,0:T(8,128)S(1)} %slice_add_fusion, f32[10,34,130]{2,1,0:T(8,128)S(1)} %fusion.37, f32[16,40,136]{2,1,0:T(8,128)S(1)} %get-tuple-element.10, f32[16,40,136]{2,1,0:T(8,128)S(1)} %get-tuple-element.9, f32[16,40,136]{2,1,0:T(8,128)S(1)} %get-tuple-element.8, ...), kind=kLoop, calls=%fused_computation.131 | loop fusion | flops 524287 | bytes 2097156 | tf_op jit(solution)/shard_map/reduce_sum | solution.py:220
  125.9 0.8 broadcast_in_dim.119
  126.7 33.5 %all_to_all.16 = f32[512,1,1]{2,1,0:T(1,128)S(1)} all-to-all(f32[512,1,1]{2,1,0:T(1,128)S(1)} %broadcast_in_dim.119), channel_id=1, replica_groups=mesh['gx'=16,'gy'=8,'gz'=4] {'gx','gy','gz'}, dimensions={0} | all-to-all | bytes 4096 | tf_op jit(solution)/shard_map/all_to_all | solution.py:222
  160.2 1.1 reduce_sum.49
  (44 shorter events, 0.5 us)
Async XLA Ops:
  6.8 21.6 %copy-start.11 = (f32[6]{0:T(128)S(1)}, f32[6]{0:T(128)}, u32[]{:S(2)}) copy-start(f32[6]{0:T(128)} %param.12) | copy-start | bytes 76
  6.9 21.6 %copy-start.12 = (s32[128]{0:T(128)S(1)}, s32[128]{0:T(128)}, u32[]{:S(2)}) copy-start(s32[128]{0:T(128)} %param.13) | copy-start | bytes 1540
  6.9 21.6 %copy-start.6 = (f32[8,32,128]{2,1,0:T(8,128)S(1)}, f32[8,32,128]{2,1,0:T(8,128)}, u32[]{:S(2)}) copy-start(f32[8,32,128]{2,1,0:T(8,128)} %param.11) | copy-start | bytes 393220
  6.9 21.6 %copy-start = (f32[8,32,128]{2,1,0:T(8,128)S(1)}, f32[8,32,128]{2,1,0:T(8,128)}, u32[]{:S(2)}) copy-start(f32[8,32,128]{2,1,0:T(8,128)} %param.10) | copy-start | bytes 393220
  6.9 21.6 %copy-start.1 = (f32[8,32,128]{2,1,0:T(8,128)S(1)}, f32[8,32,128]{2,1,0:T(8,128)}, u32[]{:S(2)}) copy-start(f32[8,32,128]{2,1,0:T(8,128)} %param.19) | copy-start | bytes 393220
  10.0 57.0 %all-to-all-start = ((f32[128,1,1560]{2,1,0:T(1,128)}), f32[128,1,1560]{2,1,0:T(1,128)S(1)}, u32[]{:S(2)}, u32[]{:S(2)}) async-start(f32[128,1,1560]{2,1,0:T(1,128)} %all_to_all.13), calls=%async_computation | async-start | bytes 1703936 | tf_op jit(solution)/shard_map/all_to_all | solution.py:149
  28.6 36.8 %collective-permute-start = (f32[3,5,32,128]{3,2,1,0:T(8,128)S(1)}, f32[3,5,32,128]{3,2,1,0:T(8,128)S(1)}, u32[]{:S(2)}, u32[]{:S(2)}) collective-permute-start(f32[3,5,32,128]{3,2,1,0:T(8,128)S(1)} %get-tuple-element.26), channel_id=1, source_target_pairs={{0,32},{32,64},{64,96},{96,128},{128,160},{160,192},{192,224},{224... | collective-permute-start | bytes 737288 | tf_op jit(solution)/shard_map/ppermute | solution.py:22
  35.8 29.7 %collective-permute-start.1 = (f32[3,5,32,128]{3,2,1,0:T(8,128)S(1)}, f32[3,5,32,128]{3,2,1,0:T(8,128)S(1)}, u32[]{:S(2)}, u32[]{:S(2)}) collective-permute-start(f32[3,5,32,128]{3,2,1,0:T(8,128)S(1)} %get-tuple-element.27), channel_id=1, source_target_pairs={{32,0},{64,32},{96,64},{128,96},{160,128},{192,160},{224,192},{256... | collective-permute-start | bytes 737288 | tf_op jit(solution)/shard_map/ppermute | solution.py:23
  65.5 0.7 copy-start.2
  66.2 0.7 copy-start.4
  70.8 1.9 %copy-start.3 = (f32[3,5,32,128]{3,2,1,0:T(8,128)S(1)}, f32[3,5,32,128]{3,2,1,0:T(8,128)}, u32[]{:S(2)}) copy-start(f32[3,5,32,128]{3,2,1,0:T(8,128)} %copy-done.2) | copy-start | bytes 737284
  70.8 1.9 %copy-start.5 = (f32[3,5,32,128]{3,2,1,0:T(8,128)S(1)}, f32[3,5,32,128]{3,2,1,0:T(8,128)}, u32[]{:S(2)}) copy-start(f32[3,5,32,128]{3,2,1,0:T(8,128)} %copy-done.4) | copy-start | bytes 737284
  72.9 8.9 %collective-permute-start.2 = (f32[360,128]{1,0:T(8,128)S(1)}, f32[360,128]{1,0:T(8,128)S(1)}, u32[]{:S(2)}, u32[]{:S(2)}) collective-permute-start(f32[360,128]{1,0:T(8,128)S(1)} %reshape.445), channel_id=1, source_target_pairs={{0,4},{4,8},{8,12},{12,16},{16,20},{20,24},{24,28},{1,5},{5,9},{9,... | collective-permute-start | bytes 552968 | tf_op jit(solution)/shard_map/ppermute | solution.py:22
  79.4 6.9 %collective-permute-start.3 = (f32[360,128]{1,0:T(8,128)S(1)}, f32[360,128]{1,0:T(8,128)S(1)}, u32[]{:S(2)}, u32[]{:S(2)}) collective-permute-start(f32[360,128]{1,0:T(8,128)S(1)} %reshape.447), channel_id=1, source_target_pairs={{4,0},{8,4},{12,8},{16,12},{20,16},{24,20},{28,24},{5,1},{9,5},{13... | collective-permute-start | bytes 552968 | tf_op jit(solution)/shard_map/ppermute | solution.py:23
  93.1 9.0 %collective-permute-start.4 = (f32[20,756]{1,0:T(8,128)}, f32[20,756]{1,0:T(8,128)}, u32[]{:S(2)}, u32[]{:S(2)}) collective-permute-start(f32[20,756]{1,0:T(8,128)} %reshape.449), channel_id=1, source_target_pairs={{0,1},{1,2},{2,3},{4,5},{5,6},{6,7},{8,9},{9,10},{10,11},{12,13},{... | collective-permute-start | bytes 181448 | tf_op jit(solution)/shard_map/ppermute | solution.py:22
  100.1 5.5 %collective-permute-start.5 = (f32[20,756]{1,0:T(8,128)}, f32[20,756]{1,0:T(8,128)}, u32[]{:S(2)}, u32[]{:S(2)}) collective-permute-start(f32[20,756]{1,0:T(8,128)} %reshape.451), channel_id=1, source_target_pairs={{1,0},{2,1},{3,2},{5,4},{6,5},{7,6},{9,8},{10,9},{11,10},{13,12},{... | collective-permute-start | bytes 181448 | tf_op jit(solution)/shard_map/ppermute | solution.py:23
  114.3 0.7 copy-start.7
  117.7 0.6 copy-start.10
  118.3 2.2 %copy-start.8 = (pred[132]{0:T(512)(128)(4,1)S(1)}, pred[132]{0:T(512)(128)(4,1)}, u32[]{:S(2)}) copy-start(pred[132]{0:T(512)(128)(4,1)} %compare_and_fusion.6) | copy-start | bytes 400
  120.5 1.9 %copy-start.9 = (pred[130]{0:T(512)(128)(4,1)S(1)}, pred[130]{0:T(512)(128)(4,1)}, u32[]{:S(2)}) copy-start(pred[130]{0:T(512)(128)(4,1)} %compare_and_fusion.9) | copy-start | bytes 394

commit v4 on v2

--- a/solution.py
+++ b/solution.py
@@ -29,6 +29,8 @@
 
 
 def with_wide_halo(fields, width):
+    prev, nxt = exchange(fields[:, :width], fields[:, -width:], "gx")
+    fields = jnp.concatenate([prev, fields, nxt], axis=1)
     nf, nx, ny, nz = fields.shape
 
     def pack_y(a):
@@ -143,30 +145,16 @@
     forcing = charge + injected
 
     halo = SWEEPS + 1
-    early = jnp.stack([permittivity, initial], axis=0)
-    early_prev, early_next = exchange_x(early, halo)
-    late = jnp.stack([forcing, coupling], axis=0)
-    late_prev, late_next = exchange_x(late, halo - 1)
-    pad = jnp.zeros((2, 1, cells_y, cells_z), jnp.float32)
-    late_prev = jnp.concatenate([pad, late_prev], axis=1)
-    late_next = jnp.concatenate([late_next, pad], axis=1)
-    fields_x = jnp.concatenate(
-        [
-            jnp.concatenate([early_prev, early, early_next], axis=1),
-            jnp.concatenate([late_prev, late, late_next], axis=1),
-        ],
-        axis=0,
-    )
-    wide = with_wide_halo(fields_x, halo)
-    eps_w, initial_w, forcing_w, coupling_w = wide[0], wide[1], wide[2], wide[3]
-    potential = initial_w
+    early = with_wide_halo(jnp.stack([permittivity, initial], axis=0), halo)
+    late = with_wide_halo(jnp.stack([forcing, coupling], axis=0), halo - 1)
+    eps_w, potential = early[0], early[1]
+    forcing_c, coupling_c = late[0], late[1]
 
     coefficients = face_coefficients(eps_w)
     diagonal_sum = coefficients[0]
     for index in range(1, 6):
         diagonal_sum = diagonal_sum + coefficients[index]
-    diagonal_sum = diagonal_sum + trim(coupling_w, 1)
-    forcing_c = trim(forcing_w, 1)
+    diagonal_sum = diagonal_sum + coupling_c
 
     def inside_mask(k):
         def axis_mask(axis, cells):

time: 142 us -> 147 us (1.035)
  starting transfers between devices: 40.2 us -> 54.1 us
  waiting for transfers between devices: 29.4 us -> 16.7 us
  other arithmetic: 26.4 us -> 29 us
    ppermute x4 -> x6, starting transfers between devices: 15.4 us -> 28.9 us  [exchange(): from_prev = lax.ppermute(hi, axis, forward)]
    ppermute x4 -> x6, waiting for transfers between devices: 22.1 us -> 11.6 us  [exchange(): from_next = lax.ppermute(lo, axis, backward)]
    all_to_all x1, waiting for transfers between devices: 6.11 us -> 2.62 us  [on_device(): lax.all_to_all(send, ('gx', 'gy'), split_axis=0, concat_axis=0, tiled=True)]
    ppermute x4 -> x6, starting transfers between devices: 6.47 us -> 9.83 us  [exchange(): from_next = lax.ppermute(lo, axis, backward)]
    all_to_all x1, starting transfers between devices: 18.4 us -> 15.4 us  [on_device(): lax.all_to_all(send, ('gx', 'gy'), split_axis=0, concat_axis=0, tiled=True)]
    another operation x4, other arithmetic: 0.08 us -> 2.66 us  [the longest x2 1.91 us: on_device(): early = with_wide_halo(jnp.stack([permittivity, initial], axis=0), halo)]
    reshape x2 -> x4, local copies, waits for them, and re-layouts: 0.96 us -> 2.53 us  [unpack(): return jnp.moveaxis(a.reshape(nf, width, nx, ny), 1, 3)]
    transpose x3 -> x6, local copies, waits for them, and re-layouts: 3.04 us -> 2.01 us  [pack(): return jnp.moveaxis(a, 3, 1).reshape(nf * width, nx * ny)]
  transfers between devices with their start and end apart: 9 -> 13, of which waited for: 5 -> 7; matrix products, arithmetic and copies ran while one was open for 5% -> 10% of each run, Pallas kernels for 0% -> 0%
where the time goes in v4:
time: 147 us; the launch traced here: 146 us
  starting transfers between devices  54.1 us (37%)
  blocking collectives  30.3 us (21%)
  other arithmetic  29 us (20%)
  waiting for transfers between devices  16.7 us (11%)
  local copies, waits for them, and re-layouts  12.6 us (9%)
  between operations  3.15 us (2%)
    all_to_all x1, blocking collectives, on_device(): lax.all_to_all(jnp.full((device_count,), local_total), ('gx', 'gy', 'gz')...  30.3 us
    ppermute x6, starting transfers between devices, exchange(): from_prev = lax.ppermute(hi, axis, forward)  28.9 us
    all_to_all x1, starting transfers between devices, on_device(): lax.all_to_all(send, ('gx', 'gy'), split_axis=0, concat_axis=0, tiled=True)  15.4 us
    ppermute x6, waiting for transfers between devices, exchange(): from_next = lax.ppermute(lo, axis, backward)  11.6 us
    ppermute x6, starting transfers between devices, exchange(): from_next = lax.ppermute(lo, axis, backward)  9.83 us
    select_n x4, other arithmetic, on_device(): updated = jnp.where(inside_mask(k), updated, 0.0)  8.12 us
    concatenate x2, other arithmetic, with_wide_halo(): return jnp.concatenate([unpack(prev), fields, unpack(nxt)], axis=3)  3.83 us
  transfers between devices with their start and end apart: 13, of which 7 were waited for; matrix products, arithmetic and copies ran while one was open for 10% of the time, Pallas kernels for 0%

profile of v4, /device:TPU:1, one launch (start us, length us, event | category | flops | bytes accessed | tf_op | source)
XLA Modules:
  0.0 146.4 jit_solution(5218871819830031265)
XLA Ops:
  0.6 0.8 select_reduce_fusion.1
  1.4 0.9 multiply_bitcast_fusion
  2.3 1.0 fusion.46
  3.3 11.6 %collective-permute-start = (f32[2,5,32,128]{3,2,1,0:T(8,128)S(1)}, f32[2,5,32,128]{3,2,1,0:T(8,128)S(1)}, u32[]{:S(2)}, u32[]{:S(2)}) collective-permute-start(f32[2,5,32,128]{3,2,1,0:T(8,128)S(1)} %get-tuple-element.23), channel_id=1, source_target_pairs={{0,32},{32,64},{64,96},{96,128},{128,160},{160,192},{192,224},{224... | collective-permute-start | bytes 491528 | tf_op jit(solution)/shard_map/ppermute | solution.py:22
  14.9 1.3 collective-permute-start.1
  16.2 0.9 select_reduce_fusion
  17.2 0.7 convert_bitcast_fusion
  18.0 0.9 convert_reduce_fusion
  18.9 0.7 compare_select_fusion
  19.6 1.5 %scatter_custom_fusion = f32[512,130]{1,0:T(8,128)S(1)} fusion(s32[128]{0:T(128)S(1)} %compare_select_fusion, f32[]{:T(128)} %constant.36.clone.1, f32[128,1]{1,0:T(8,128)S(1)} %copy.51, f32[]{:T(128)} %constant.49, f32[128,1]{1,0:T(8,128)S(1)} %copy.50, f32[128,128]{1,0:T(8,128)} %param.15), kind=kCustom, calls=%fused_computation.103 | custom fusion | flops 33280 | bytes 462856 | tf_op jit(solution)/shard_map/scatter | solution.py:127
  21.1 1.4 all_to_all.13
  22.5 15.4 %all-to-all-start = ((f32[128,1,520]{2,1,0:T(1,128)}), f32[128,1,520]{2,1,0:T(1,128)S(1)}, u32[]{:S(2)}, u32[]{:S(2)}) async-start(f32[128,1,520]{2,1,0:T(1,128)} %all_to_all.13), calls=%async_computation | async-start | bytes 655360 | tf_op jit(solution)/shard_map/all_to_all | solution.py:129
  38.4 0.5 compare_and_fusion
  38.9 0.6 compare_and_fusion.3
  39.6 3.5 %collective-permute-start.2 = (f32[180,128]{1,0:T(8,128)S(1)}, f32[180,128]{1,0:T(8,128)S(1)}, u32[]{:S(2)}, u32[]{:S(2)}) collective-permute-start(f32[180,128]{1,0:T(8,128)S(1)} %reshape.290), channel_id=1, source_target_pairs={{0,4},{4,8},{8,12},{12,16},{16,20},{20,24},{24,28},{1,5},{5,9},{9,... | collective-permute-start | bytes 276488 | tf_op jit(solution)/shard_map/ppermute | solution.py:22
  43.1 1.9 %collective-permute-start.3 = (f32[180,128]{1,0:T(8,128)S(1)}, f32[180,128]{1,0:T(8,128)S(1)}, u32[]{:S(2)}, u32[]{:S(2)}) collective-permute-start(f32[180,128]{1,0:T(8,128)S(1)} %reshape.292), channel_id=1, source_target_pairs={{4,0},{8,4},{12,8},{16,12},{20,16},{24,20},{28,24},{5,1},{9,5},{13... | collective-permute-start | bytes 276488 | tf_op jit(solution)/shard_map/ppermute | solution.py:23
  45.1 0.5 compare_and_fusion.6
  45.6 2.4 %collective-permute-done.2 = f32[180,128]{1,0:T(8,128)S(1)} collective-permute-done((f32[180,128]{1,0:T(8,128)S(1)}, f32[180,128]{1,0:T(8,128)S(1)}, u32[]{:S(2)}, u32[]{:S(2)}) %collective-permute-start.2) | collective-permute-done | bytes 92192 | tf_op jit(solution)/shard_map/ppermute | solution.py:22
  48.0 2.6 %collective-permute-done.3 = f32[180,128]{1,0:T(8,128)S(1)} collective-permute-done((f32[180,128]{1,0:T(8,128)S(1)}, f32[180,128]{1,0:T(8,128)S(1)}, u32[]{:S(2)}, u32[]{:S(2)}) %collective-permute-start.3) | collective-permute-done | bytes 92192 | tf_op jit(solution)/shard_map/ppermute | solution.py:23
  50.8 2.6 %all-to-all-done = f32[128,1,520]{2,1,0:T(1,128)S(1)} async-done(((f32[128,1,520]{2,1,0:T(1,128)}), f32[128,1,520]{2,1,0:T(1,128)S(1)}, u32[]{:S(2)}, u32[]{:S(2)}) %all-to-all-start) | async-done | bytes 266272 | tf_op jit(solution)/shard_map/all_to_all | solution.py:129
  53.5 0.8 reduce.1
  55.0 0.5 fusion.20
  55.6 0.7 fusion.47
  56.3 4.2 %collective-permute-start.6 = (f32[2,4,32,128]{3,2,1,0:T(8,128)}, f32[2,4,32,128]{3,2,1,0:T(8,128)S(1)}, u32[]{:S(2)}, u32[]{:S(2)}) collective-permute-start(f32[2,4,32,128]{3,2,1,0:T(8,128)} %get-tuple-element.25), channel_id=1, source_target_pairs={{0,32},{32,64},{64,96},{96,128},{128,160},{160,192},{192,224},{224... | collective-permute-start | bytes 393224 | tf_op jit(solution)/shard_map/ppermute | solution.py:22
  60.6 1.3 collective-permute-start.7
  61.9 0.3 slice_bitcast_fusion.3
  62.2 0.5 copy.46
  62.8 3.1 %collective-permute-start.4 = (f32[10,756]{1,0:T(8,128)S(1)}, f32[10,756]{1,0:T(8,128)S(1)}, u32[]{:S(2)}, u32[]{:S(2)}) collective-permute-start(f32[10,756]{1,0:T(8,128)S(1)} %reshape.294), channel_id=1, source_target_pairs={{0,1},{1,2},{2,3},{4,5},{5,6},{6,7},{8,9},{9,10},{10,11},{12,13},{... | collective-permute-start | bytes 90728 | tf_op jit(solution)/shard_map/ppermute | solution.py:22
  65.9 0.5 copy.47
  66.5 1.3 collective-permute-start.5
  67.8 0.6 compare_and_fusion.9
  68.5 0.4 copy.48
  68.9 2.4 %collective-permute-done.5 = f32[10,756]{1,0:T(8,128)S(1)} collective-permute-done((f32[10,756]{1,0:T(8,128)S(1)}, f32[10,756]{1,0:T(8,128)S(1)}, u32[]{:S(2)}, u32[]{:S(2)}) %collective-permute-start.5) | collective-permute-done | bytes 30272 | tf_op jit(solution)/shard_map/ppermute | solution.py:23
  71.4 0.4 copy.49
  71.9 3.7 %collective-permute-done.7 = f32[2,4,32,128]{3,2,1,0:T(8,128)} collective-permute-done((f32[2,4,32,128]{3,2,1,0:T(8,128)}, f32[2,4,32,128]{3,2,1,0:T(8,128)}, u32[]{:S(2)}, u32[]{:S(2)}) %collective-permute-start.7) | collective-permute-done | bytes 131104 | tf_op jit(solution)/shard_map/ppermute | solution.py:23
  75.6 0.8 pad_maximum_fusion.13
  76.4 2.7 %collective-permute-start.8 = (f32[128,128]{1,0:T(8,128)S(1)}, f32[128,128]{1,0:T(8,128)S(1)}, u32[]{:S(2)}, u32[]{:S(2)}) collective-permute-start(f32[128,128]{1,0:T(8,128)S(1)} %bitcast.62), channel_id=1, source_target_pairs={{0,4},{4,8},{8,12},{12,16},{16,20},{20,24},{24,28},{1,5},{5,9},{9,... | collective-permute-start | bytes 196616 | tf_op jit(solution)/shard_map/ppermute | solution.py:22
  79.1 2.6 %collective-permute-start.9 = (f32[128,128]{1,0:T(8,128)S(1)}, f32[128,128]{1,0:T(8,128)S(1)}, u32[]{:S(2)}, u32[]{:S(2)}) collective-permute-start(f32[128,128]{1,0:T(8,128)S(1)} %bitcast.61), channel_id=1, source_target_pairs={{4,0},{8,4},{12,8},{16,12},{20,16},{24,20},{28,24},{5,1},{9,5},{13... | collective-permute-start | bytes 196616 | tf_op jit(solution)/shard_map/ppermute | solution.py:23
  81.7 2.2 %pad_maximum_fusion = f32[2,18,42,138]{3,2,1,0:T(8,128)S(1)} fusion(f32[2,18,42,5]{3,2,1,0:T(8,128)S(1)} %copy.49, f32[2,18,5,128]{3,2,1,0:T(8,128)} %copy-done.12, f32[2,5,32,128]{3,2,1,0:T(8,128)} %copy-done.10, f32[1,8,32,128]{3,2,1,0:T(8,128)} %bitcast.49, f32[1,8,32,128]{3,2,1,0:T(8,128)} %copy-done.3, f32[2,5,32,128]{3,2,1,0:T(8,128)} %copy-done.9, ...), kind=kLoop, calls=%fused_computation.1 | loop fusion | flops 1460592 | bytes 1669248 | tf_op jit(solution)/shard_map/concatenate | solution.py:53
  83.9 0.9 collective-permute-done.9
  84.9 1.0 pad_maximum_fusion.3
  86.1 0.3 copy.53
  86.4 0.7 reshape.304
  87.1 3.7 %collective-permute-start.10 = (f32[8,640]{1,0:T(8,128)}, f32[8,640]{1,0:T(8,128)}, u32[]{:S(2)}, u32[]{:S(2)}) collective-permute-start(f32[8,640]{1,0:T(8,128)} %reshape.304), channel_id=1, source_target_pairs={{0,1},{1,2},{2,3},{4,5},{5,6},{6,7},{8,9},{9,10},{10,11},{12,13},{... | collective-permute-start | bytes 61448 | tf_op jit(solution)/shard_map/ppermute | solution.py:22
  90.8 0.3 copy.54
  91.1 0.7 reshape.306
  91.8 1.5 collective-permute-start.11
  93.5 0.9 reshape.305
  94.4 0.3 copy.55
  94.7 2.0 %collective-permute-done.11 = f32[8,640]{1,0:T(8,128)} collective-permute-done((f32[8,640]{1,0:T(8,128)}, f32[8,640]{1,0:T(8,128)}, u32[]{:S(2)}, u32[]{:S(2)}) %collective-permute-start.11) | collective-permute-done | bytes 20512 | tf_op jit(solution)/shard_map/ppermute | solution.py:23
  96.7 1.4 reshape.307
  98.1 1.1 copy.56
  99.3 1.7 %pad_maximum_fusion.1 = f32[2,16,40,136]{3,2,1,0:T(8,128)S(1)} fusion(f32[2,16,40,4]{3,2,1,0:T(8,128)S(1)} %copy.56, f32[2,16,4,128]{3,2,1,0:T(4,128)} %bitcast.58, f32[2,4,32,128]{3,2,1,0:T(8,128)} %collective-permute-done.7, f32[1,8,32,128]{3,2,1,0:T(8,128)S(1)} %bitcast.47, f32[1,8,32,128]{3,2,1,0:T(8,128)S(1)} %copy-done.2, ...), kind=kLoop, calls=%fused_computation.2 | loop fusion | flops 1218560 | bytes 1392640 | tf_op jit(solution)/shard_map/concatenate | solution.py:53
  101.0 0.6 copy-done.20
  101.6 2.4 %fusion.6 = (f32[16,40,136]{2,1,0:T(8,128)S(1)}, f32[16,40,136]{2,1,0:T(8,128)S(1)}, f32[16,40,136]{2,1,0:T(8,128)S(1)}, f32[16,40,136]{2,1,0:T(8,128)S(1)}, f32...) fusion(f32[18,42,138]{2,1,0:T(8,128)S(1)} %get-tuple-element.12, ...), kind=kLoop, calls=%fused_computation.16 | loop fusion | flops 3742720 | bytes 8008456 | tf_op jit(solution)/shard_map/jit(_where)/select_n | solution.py:180
  104.0 0.3 fusion
  104.3 0.4 copy-done.23
  104.6 2.2 %fusion.12 = f32[14,38,134]{2,1,0:T(8,128)S(1)} fusion(f32[16,40,136]{2,1,0:T(8,128)S(1)} %fusion, f32[16,40,136]{2,1,0:T(8,128)S(1)} %get-tuple-element.4, f32[16,40,136]{2,1,0:T(8,128)S(1)} %get-tuple-element.10, f32[16,40,136]{2,1,0:T(8,128)S(1)} %get-tuple-element.9, f32[16,40,136]{2,1,0:T(8,128)S(1)} %get-tuple-element.8, ...), kind=kLoop, calls=%fused_computation.39 | loop fusion | flops 1283184 | bytes 4563098 | tf_op jit(solution)/shard_map/jit(_where)/select_n | solution.py:180
  106.9 1.9 %fusion.25 = f32[12,36,132]{2,1,0:T(8,128)S(1)} fusion(f32[16,40,136]{2,1,0:T(8,128)S(1)} %fusion, f32[14,38,134]{2,1,0:T(8,128)S(1)} %fusion.12, f32[16,40,136]{2,1,0:T(8,128)S(1)} %get-tuple-element.10, f32[16,40,136]{2,1,0:T(8,128)S(1)} %get-tuple-element.9, f32[16,40,136]{2,1,0:T(8,128)S(1)} %get-tuple-element.8, ...), kind=kLoop, calls=%fused_computation.63 | loop fusion | flops 1026432 | bytes 3650100 | tf_op jit(solution)/shard_map/jit(_where)/select_n | solution.py:180
  108.8 1.6 %fusion.34 = f32[10,34,130]{2,1,0:T(8,128)S(1)} fusion(f32[16,40,136]{2,1,0:T(8,128)S(1)} %fusion, f32[12,36,132]{2,1,0:T(8,128)S(1)} %fusion.25, f32[16,40,136]{2,1,0:T(8,128)S(1)} %get-tuple-element.10, f32[16,40,136]{2,1,0:T(8,128)S(1)} %get-tuple-element.9, f32[16,40,136]{2,1,0:T(8,128)S(1)} %get-tuple-element.8, ...), kind=kLoop, calls=%fused_computation.80 | loop fusion | flops 795600 | bytes 2829270 | tf_op jit(solution)/shard_map/jit(_where)/select_n | solution.py:180
  110.4 1.8 %fusion.50 = (f32[]{:T(128)}, f32[8,32,128]{2,1,0:T(8,128)}) fusion(f32[16,40,136]{2,1,0:T(8,128)S(1)} %fusion, f32[10,34,130]{2,1,0:T(8,128)S(1)} %fusion.34, f32[16,40,136]{2,1,0:T(8,128)S(1)} %get-tuple-element.10, f32[16,40,136]{2,1,0:T(8,128)S(1)} %get-tuple-element.9, f32[16,40,136]{2,1,0:T(8,128)S(1)} %get-tuple-element.8, ...), kind=kLoop, calls=%fused_computation.115 | loop fusion | flops 524287 | bytes 2097156 | tf_op jit(solution)/shard_map/reduce_sum | solution.py:188
  112.3 0.8 broadcast_in_dim.92
  113.1 30.3 %all_to_all.16 = f32[512,1,1]{2,1,0:T(1,128)S(1)} all-to-all(f32[512,1,1]{2,1,0:T(1,128)S(1)} %broadcast_in_dim.92), channel_id=1, replica_groups=mesh['gx'=16,'gy'=8,'gz'=4] {'gx','gy','gz'}, dimensions={0} | all-to-all | bytes 4096 | tf_op jit(solution)/shard_map/all_to_all | solution.py:190
  143.4 1.1 reduce_sum.49
  (85 shorter events, 2.6 us)
Async XLA Ops:
  2.3 48.4 %copy-start.3 = (f32[1,8,32,128]{3,2,1,0:T(8,128)}, f32[1,8,32,128]{3,2,1,0:T(8,128)S(1)}, u32[]{:S(2)}) copy-start(f32[1,8,32,128]{3,2,1,0:T(8,128)S(1)} %multiply_bitcast_fusion) | copy-start | bytes 393220
  3.3 36.2 %copy-start.8 = (f32[8,32,128]{2,1,0:T(8,128)S(1)}, f32[8,32,128]{2,1,0:T(8,128)}, u32[]{:S(2)}) copy-start(f32[8,32,128]{2,1,0:T(8,128)} %param.19) | copy-start | bytes 393220
  3.3 36.1 %collective-permute-start = (f32[2,5,32,128]{3,2,1,0:T(8,128)S(1)}, f32[2,5,32,128]{3,2,1,0:T(8,128)S(1)}, u32[]{:S(2)}, u32[]{:S(2)}) collective-permute-start(f32[2,5,32,128]{3,2,1,0:T(8,128)S(1)} %get-tuple-element.23), channel_id=1, source_target_pairs={{0,32},{32,64},{64,96},{96,128},{128,160},{160,192},{192,224},{224... | collective-permute-start | bytes 491528 | tf_op jit(solution)/shard_map/ppermute | solution.py:22
  14.9 24.5 %collective-permute-start.1 = (f32[2,5,32,128]{3,2,1,0:T(8,128)S(1)}, f32[2,5,32,128]{3,2,1,0:T(8,128)S(1)}, u32[]{:S(2)}, u32[]{:S(2)}) collective-permute-start(f32[2,5,32,128]{3,2,1,0:T(8,128)S(1)} %get-tuple-element.24), channel_id=1, source_target_pairs={{32,0},{64,32},{96,64},{128,96},{160,128},{192,160},{224,192},{256... | collective-permute-start | bytes 491528 | tf_op jit(solution)/shard_map/ppermute | solution.py:23
  22.5 30.9 %all-to-all-start = ((f32[128,1,520]{2,1,0:T(1,128)}), f32[128,1,520]{2,1,0:T(1,128)S(1)}, u32[]{:S(2)}, u32[]{:S(2)}) async-start(f32[128,1,520]{2,1,0:T(1,128)} %all_to_all.13), calls=%async_computation | async-start | bytes 655360 | tf_op jit(solution)/shard_map/all_to_all | solution.py:129
  39.5 11.3 %copy-start.9 = (f32[2,5,32,128]{3,2,1,0:T(8,128)}, f32[2,5,32,128]{3,2,1,0:T(8,128)S(1)}, u32[]{:S(2)}) copy-start(f32[2,5,32,128]{3,2,1,0:T(8,128)S(1)} %collective-permute-done) | copy-start | bytes 491524
  39.5 11.3 %copy-start.10 = (f32[2,5,32,128]{3,2,1,0:T(8,128)}, f32[2,5,32,128]{3,2,1,0:T(8,128)S(1)}, u32[]{:S(2)}) copy-start(f32[2,5,32,128]{3,2,1,0:T(8,128)S(1)} %collective-permute-done.1) | copy-start | bytes 491524
  39.6 8.4 %collective-permute-start.2 = (f32[180,128]{1,0:T(8,128)S(1)}, f32[180,128]{1,0:T(8,128)S(1)}, u32[]{:S(2)}, u32[]{:S(2)}) collective-permute-start(f32[180,128]{1,0:T(8,128)S(1)} %reshape.290), channel_id=1, source_target_pairs={{0,4},{4,8},{8,12},{12,16},{16,20},{20,24},{24,28},{1,5},{5,9},{9,... | collective-permute-start | bytes 276488 | tf_op jit(solution)/shard_map/ppermute | solution.py:22
  43.1 7.5 %collective-permute-start.3 = (f32[180,128]{1,0:T(8,128)S(1)}, f32[180,128]{1,0:T(8,128)S(1)}, u32[]{:S(2)}, u32[]{:S(2)}) collective-permute-start(f32[180,128]{1,0:T(8,128)S(1)} %reshape.292), channel_id=1, source_target_pairs={{4,0},{8,4},{12,8},{16,12},{20,16},{24,20},{28,24},{5,1},{9,5},{13... | collective-permute-start | bytes 276488 | tf_op jit(solution)/shard_map/ppermute | solution.py:23
  48.0 5.4 %copy-start.11 = (f32[2,18,5,128]{3,2,1,0:T(8,128)}, f32[2,18,5,128]{3,2,1,0:T(8,128)S(1)}, u32[]{:S(2)}) copy-start(f32[2,18,5,128]{3,2,1,0:T(8,128)S(1)} %reshape.291) | copy-start | bytes 276484
  50.7 2.8 %copy-start.12 = (f32[2,18,5,128]{3,2,1,0:T(8,128)}, f32[2,18,5,128]{3,2,1,0:T(8,128)S(1)}, u32[]{:S(2)}) copy-start(f32[2,18,5,128]{3,2,1,0:T(8,128)S(1)} %reshape.293) | copy-start | bytes 276484
  54.5 1.0 copy-start.19
  55.5 5.0 %copy-start.4 = (f32[256,128]{1,0:T(8,128)}, f32[256,128]{1,0:T(8,128)S(1)}, u32[]{:S(2)}) copy-start(f32[256,128]{1,0:T(8,128)S(1)} %get-tuple-element.28) | copy-start | bytes 393220
  55.6 20.0 %copy-start = (f32[1,8,32,128]{3,2,1,0:T(8,128)}, f32[1,8,32,128]{3,2,1,0:T(8,128)S(1)}, u32[]{:S(2)}) copy-start(f32[1,8,32,128]{3,2,1,0:T(8,128)S(1)} %add_bitcast_fusion) | copy-start | bytes 393220
  56.3 15.5 %collective-permute-start.6 = (f32[2,4,32,128]{3,2,1,0:T(8,128)}, f32[2,4,32,128]{3,2,1,0:T(8,128)S(1)}, u32[]{:S(2)}, u32[]{:S(2)}) collective-permute-start(f32[2,4,32,128]{3,2,1,0:T(8,128)} %get-tuple-element.25), channel_id=1, source_target_pairs={{0,32},{32,64},{64,96},{96,128},{128,160},{160,192},{192,224},{224... | collective-permute-start | bytes 393224 | tf_op jit(solution)/shard_map/ppermute | solution.py:22
  60.6 15.0 %collective-permute-start.7 = (f32[2,4,32,128]{3,2,1,0:T(8,128)}, f32[2,4,32,128]{3,2,1,0:T(8,128)}, u32[]{:S(2)}, u32[]{:S(2)}) collective-permute-start(f32[2,4,32,128]{3,2,1,0:T(8,128)} %get-tuple-element.26), channel_id=1, source_target_pairs={{32,0},{64,32},{96,64},{128,96},{160,128},{192,160},{224,192},{256... | collective-permute-start | bytes 393224 | tf_op jit(solution)/shard_map/ppermute | solution.py:23
  62.8 5.6 %collective-permute-start.4 = (f32[10,756]{1,0:T(8,128)S(1)}, f32[10,756]{1,0:T(8,128)S(1)}, u32[]{:S(2)}, u32[]{:S(2)}) collective-permute-start(f32[10,756]{1,0:T(8,128)S(1)} %reshape.294), channel_id=1, source_target_pairs={{0,1},{1,2},{2,3},{4,5},{5,6},{6,7},{8,9},{9,10},{10,11},{12,13},{... | collective-permute-start | bytes 90728 | tf_op jit(solution)/shard_map/ppermute | solution.py:22
  66.3 9.2 %copy-start.5 = (f32[256,128]{1,0:T(8,128)S(1)}, f32[256,128]{1,0:T(8,128)}, u32[]{:S(2)}) copy-start(f32[256,128]{1,0:T(8,128)} %copy-done.4) | copy-start | bytes 393220
  66.5 4.8 %collective-permute-start.5 = (f32[10,756]{1,0:T(8,128)S(1)}, f32[10,756]{1,0:T(8,128)S(1)}, u32[]{:S(2)}, u32[]{:S(2)}) collective-permute-start(f32[10,756]{1,0:T(8,128)S(1)} %reshape.296), channel_id=1, source_target_pairs={{1,0},{2,1},{3,2},{5,4},{6,5},{7,6},{9,8},{10,9},{11,10},{13,12},{... | collective-permute-start | bytes 90728 | tf_op jit(solution)/shard_map/ppermute | solution.py:23
  71.9 7.3 %copy-start.13 = (f32[2,4,32,128]{3,2,1,0:T(8,128)}, f32[2,4,32,128]{3,2,1,0:T(8,128)S(1)}, u32[]{:S(2)}) copy-start(f32[2,4,32,128]{3,2,1,0:T(8,128)S(1)} %collective-permute-done.6) | copy-start | bytes 393220
  76.4 7.5 %collective-permute-start.8 = (f32[128,128]{1,0:T(8,128)S(1)}, f32[128,128]{1,0:T(8,128)S(1)}, u32[]{:S(2)}, u32[]{:S(2)}) collective-permute-start(f32[128,128]{1,0:T(8,128)S(1)} %bitcast.62), channel_id=1, source_target_pairs={{0,4},{4,8},{8,12},{12,16},{16,20},{20,24},{24,28},{1,5},{5,9},{9,... | collective-permute-start | bytes 196616 | tf_op jit(solution)/shard_map/ppermute | solution.py:22
  79.1 5.7 %copy-start.1 = (f32[1,8,32,128]{3,2,1,0:T(8,128)S(1)}, f32[1,8,32,128]{3,2,1,0:T(8,128)}, u32[]{:S(2)}) copy-start(f32[1,8,32,128]{3,2,1,0:T(8,128)} %copy-done) | copy-start | bytes 393220
  79.1 5.7 %copy-start.6 = (f32[256,128]{1,0:T(8,128)S(1)}, f32[256,128]{1,0:T(8,128)}, u32[]{:S(2)}) copy-start(f32[256,128]{1,0:T(8,128)} %copy-done.4) | copy-start | bytes 393220
  79.1 5.7 %collective-permute-start.9 = (f32[128,128]{1,0:T(8,128)S(1)}, f32[128,128]{1,0:T(8,128)S(1)}, u32[]{:S(2)}, u32[]{:S(2)}) collective-permute-start(f32[128,128]{1,0:T(8,128)S(1)} %bitcast.61), channel_id=1, source_target_pairs={{4,0},{8,4},{12,8},{16,12},{20,16},{24,20},{28,24},{5,1},{9,5},{13... | collective-permute-start | bytes 196616 | tf_op jit(solution)/shard_map/ppermute | solution.py:23
  81.7 3.1 %copy-start.14 = (f32[2,4,32,128]{3,2,1,0:T(8,128)S(1)}, f32[2,4,32,128]{3,2,1,0:T(8,128)}, u32[]{:S(2)}) copy-start(f32[2,4,32,128]{3,2,1,0:T(8,128)} %copy-done.13) | copy-start | bytes 393220
  83.9 2.2 %copy-start.16 = (f32[128,128]{1,0:T(8,128)}, f32[128,128]{1,0:T(8,128)S(1)}, u32[]{:S(2)}) copy-start(f32[128,128]{1,0:T(8,128)S(1)} %collective-permute-done.8) | copy-start | bytes 196612
  84.9 1.3 copy-start.18
  87.1 6.3 %collective-permute-start.10 = (f32[8,640]{1,0:T(8,128)}, f32[8,640]{1,0:T(8,128)}, u32[]{:S(2)}, u32[]{:S(2)}) collective-permute-start(f32[8,640]{1,0:T(8,128)} %reshape.304), channel_id=1, source_target_pairs={{0,1},{1,2},{2,3},{4,5},{5,6},{6,7},{8,9},{9,10},{10,11},{12,13},{... | collective-permute-start | bytes 61448 | tf_op jit(solution)/shard_map/ppermute | solution.py:22
  91.8 4.8 %collective-permute-start.11 = (f32[8,640]{1,0:T(8,128)}, f32[8,640]{1,0:T(8,128)}, u32[]{:S(2)}, u32[]{:S(2)}) collective-permute-start(f32[8,640]{1,0:T(8,128)} %reshape.306), channel_id=1, source_target_pairs={{1,0},{2,1},{3,2},{5,4},{6,5},{7,6},{9,8},{10,9},{11,10},{13,12},{... | collective-permute-start | bytes 61448 | tf_op jit(solution)/shard_map/ppermute | solution.py:23
  93.4 5.8 %copy-start.2 = (f32[1,8,32,128]{3,2,1,0:T(8,128)S(1)}, f32[1,8,32,128]{3,2,1,0:T(8,128)}, u32[]{:S(2)}) copy-start(f32[1,8,32,128]{3,2,1,0:T(8,128)} %copy-done) | copy-start | bytes 393220
  93.4 5.8 %copy-start.7 = (f32[256,128]{1,0:T(8,128)S(1)}, f32[256,128]{1,0:T(8,128)}, u32[]{:S(2)}) copy-start(f32[256,128]{1,0:T(8,128)} %copy-done.4) | copy-start | bytes 393220
  93.4 5.8 %copy-start.15 = (f32[2,4,32,128]{3,2,1,0:T(8,128)S(1)}, f32[2,4,32,128]{3,2,1,0:T(8,128)}, u32[]{:S(2)}) copy-start(f32[2,4,32,128]{3,2,1,0:T(8,128)} %copy-done.13) | copy-start | bytes 393220
  93.5 5.8 %copy-start.17 = (f32[128,128]{1,0:T(8,128)S(1)}, f32[128,128]{1,0:T(8,128)}, u32[]{:S(2)}) copy-start(f32[128,128]{1,0:T(8,128)} %copy-done.16) | copy-start | bytes 196612
  100.9 0.7 copy-start.20
  104.0 0.7 copy-start.23
  104.6 2.2 %copy-start.21 = (pred[132]{0:T(512)(128)(4,1)S(1)}, pred[132]{0:T(512)(128)(4,1)}, u32[]{:S(2)}) copy-start(pred[132]{0:T(512)(128)(4,1)} %compare_and_fusion.6) | copy-start | bytes 400
  106.9 1.9 %copy-start.22 = (pred[130]{0:T(512)(128)(4,1)S(1)}, pred[130]{0:T(512)(128)(4,1)}, u32[]{:S(2)}) copy-start(pred[130]{0:T(512)(128)(4,1)} %compare_and_fusion.9) | copy-start | bytes 394

commit v5 on v4

--- a/solution.py
+++ b/solution.py
@@ -2,6 +2,7 @@
 import jax.numpy as jnp
 from jax import lax
 from jax.sharding import PartitionSpec as P
+
 
 SWEEPS = 4
 
@@ -22,10 +23,6 @@
     from_prev = lax.ppermute(hi, axis, forward)
     from_next = lax.ppermute(lo, axis, backward)
     return from_prev, from_next
-
-
-def exchange_x(fields, width):
-    return exchange(fields[:, :width], fields[:, -width:], "gx")
 
 
 def with_wide_halo(fields, width):
@@ -86,7 +83,7 @@
     return a[k:-k, k:-k, k:-k]
 
 
-def on_device(
+def device_step(
     charge,
     texture,
     material_eps,
@@ -215,5 +212,5 @@
     )
     out_specs = (P("gx", "gy", "gz"), P())
     return jax.shard_map(
-        on_device, mesh=mesh, in_specs=in_specs, out_specs=out_specs, check_vma=False
-    )
+        device_step, mesh=mesh, in_specs=in_specs, out_specs=out_specs, check_vma=False
+    )

time: 147 us -> 147 us (level)
  no operation moved by 1% of the time
where the time goes in v5:
time: 147 us; the launch traced here: 146 us
  starting transfers between devices  54.1 us (37%)
  blocking collectives  30.3 us (21%)
  other arithmetic  29 us (20%)
  waiting for transfers between devices  16.7 us (11%)
  local copies, waits for them, and re-layouts  12.6 us (9%)
  between operations  3.15 us (2%)
    all_to_all x1, blocking collectives, device_step(): lax.all_to_all(jnp.full((device_count,), local_total), ('gx', 'gy', 'gz')...  30.3 us
    ppermute x6, starting transfers between devices, exchange(): from_prev = lax.ppermute(hi, axis, forward)  28.9 us
    all_to_all x1, starting transfers between devices, device_step(): lax.all_to_all(send, ('gx', 'gy'), split_axis=0, concat_axis=0, tiled=True)  15.4 us
    ppermute x6, waiting for transfers between devices, exchange(): from_next = lax.ppermute(lo, axis, backward)  11.6 us
    ppermute x6, starting transfers between devices, exchange(): from_next = lax.ppermute(lo, axis, backward)  9.83 us
    select_n x4, other arithmetic, device_step(): updated = jnp.where(inside_mask(k), updated, 0.0)  8.12 us
    concatenate x2, other arithmetic, with_wide_halo(): return jnp.concatenate([unpack(prev), fields, unpack(nxt)], axis=3)  3.83 us
  transfers between devices with their start and end apart: 13, of which 7 were waited for; matrix products, arithmetic and copies ran while one was open for 10% of the time, Pallas kernels for 0%

profile of v5, /device:TPU:1, one launch (start us, length us, event | category | flops | bytes accessed | tf_op | source)
XLA Modules:
  0.0 146.4 jit_solution(5218871819830031265)
XLA Ops:
  0.6 0.8 select_reduce_fusion.1
  1.4 0.9 multiply_bitcast_fusion
  2.3 1.0 fusion.46
  3.3 11.6 %collective-permute-start = (f32[2,5,32,128]{3,2,1,0:T(8,128)S(1)}, f32[2,5,32,128]{3,2,1,0:T(8,128)S(1)}, u32[]{:S(2)}, u32[]{:S(2)}) collective-permute-start(f32[2,5,32,128]{3,2,1,0:T(8,128)S(1)} %get-tuple-element.23), channel_id=1, source_target_pairs={{0,32},{32,64},{64,96},{96,128},{128,160},{160,192},{192,224},{224... | collective-permute-start | bytes 491528 | tf_op jit(solution)/shard_map/ppermute | solution.py:23
  14.9 1.3 collective-permute-start.1
  16.2 0.9 select_reduce_fusion
  17.2 0.7 convert_bitcast_fusion
  18.0 0.9 convert_reduce_fusion
  18.9 0.7 compare_select_fusion
  19.6 1.5 %scatter_custom_fusion = f32[512,130]{1,0:T(8,128)S(1)} fusion(s32[128]{0:T(128)S(1)} %compare_select_fusion, f32[]{:T(128)} %constant.36.clone.1, f32[128,1]{1,0:T(8,128)S(1)} %copy.51, f32[]{:T(128)} %constant.49, f32[128,1]{1,0:T(8,128)S(1)} %copy.50, f32[128,128]{1,0:T(8,128)} %param.15), kind=kCustom, calls=%fused_computation.103 | custom fusion | flops 33280 | bytes 462856 | tf_op jit(solution)/shard_map/scatter | solution.py:124
  21.1 1.4 all_to_all.13
  22.5 15.4 %all-to-all-start = ((f32[128,1,520]{2,1,0:T(1,128)}), f32[128,1,520]{2,1,0:T(1,128)S(1)}, u32[]{:S(2)}, u32[]{:S(2)}) async-start(f32[128,1,520]{2,1,0:T(1,128)} %all_to_all.13), calls=%async_computation | async-start | bytes 655360 | tf_op jit(solution)/shard_map/all_to_all | solution.py:126
  38.4 0.5 compare_and_fusion
  38.9 0.6 compare_and_fusion.3
  39.6 3.5 %collective-permute-start.2 = (f32[180,128]{1,0:T(8,128)S(1)}, f32[180,128]{1,0:T(8,128)S(1)}, u32[]{:S(2)}, u32[]{:S(2)}) collective-permute-start(f32[180,128]{1,0:T(8,128)S(1)} %reshape.290), channel_id=1, source_target_pairs={{0,4},{4,8},{8,12},{12,16},{16,20},{20,24},{24,28},{1,5},{5,9},{9,... | collective-permute-start | bytes 276488 | tf_op jit(solution)/shard_map/ppermute | solution.py:23
  43.1 1.9 %collective-permute-start.3 = (f32[180,128]{1,0:T(8,128)S(1)}, f32[180,128]{1,0:T(8,128)S(1)}, u32[]{:S(2)}, u32[]{:S(2)}) collective-permute-start(f32[180,128]{1,0:T(8,128)S(1)} %reshape.292), channel_id=1, source_target_pairs={{4,0},{8,4},{12,8},{16,12},{20,16},{24,20},{28,24},{5,1},{9,5},{13... | collective-permute-start | bytes 276488 | tf_op jit(solution)/shard_map/ppermute | solution.py:24
  45.1 0.5 compare_and_fusion.6
  45.6 2.4 %collective-permute-done.2 = f32[180,128]{1,0:T(8,128)S(1)} collective-permute-done((f32[180,128]{1,0:T(8,128)S(1)}, f32[180,128]{1,0:T(8,128)S(1)}, u32[]{:S(2)}, u32[]{:S(2)}) %collective-permute-start.2) | collective-permute-done | bytes 92192 | tf_op jit(solution)/shard_map/ppermute | solution.py:23
  48.0 2.6 %collective-permute-done.3 = f32[180,128]{1,0:T(8,128)S(1)} collective-permute-done((f32[180,128]{1,0:T(8,128)S(1)}, f32[180,128]{1,0:T(8,128)S(1)}, u32[]{:S(2)}, u32[]{:S(2)}) %collective-permute-start.3) | collective-permute-done | bytes 92192 | tf_op jit(solution)/shard_map/ppermute | solution.py:24
  50.8 2.6 %all-to-all-done = f32[128,1,520]{2,1,0:T(1,128)S(1)} async-done(((f32[128,1,520]{2,1,0:T(1,128)}), f32[128,1,520]{2,1,0:T(1,128)S(1)}, u32[]{:S(2)}, u32[]{:S(2)}) %all-to-all-start) | async-done | bytes 266272 | tf_op jit(solution)/shard_map/all_to_all | solution.py:126
  53.5 0.8 reduce.1
  55.0 0.5 fusion.20
  55.6 0.7 fusion.47
  56.3 4.2 %collective-permute-start.6 = (f32[2,4,32,128]{3,2,1,0:T(8,128)}, f32[2,4,32,128]{3,2,1,0:T(8,128)S(1)}, u32[]{:S(2)}, u32[]{:S(2)}) collective-permute-start(f32[2,4,32,128]{3,2,1,0:T(8,128)} %get-tuple-element.25), channel_id=1, source_target_pairs={{0,32},{32,64},{64,96},{96,128},{128,160},{160,192},{192,224},{224... | collective-permute-start | bytes 393224 | tf_op jit(solution)/shard_map/ppermute | solution.py:23
  60.6 1.3 collective-permute-start.7
  61.9 0.3 slice_bitcast_fusion.3
  62.2 0.5 copy.46
  62.8 3.1 %collective-permute-start.4 = (f32[10,756]{1,0:T(8,128)S(1)}, f32[10,756]{1,0:T(8,128)S(1)}, u32[]{:S(2)}, u32[]{:S(2)}) collective-permute-start(f32[10,756]{1,0:T(8,128)S(1)} %reshape.294), channel_id=1, source_target_pairs={{0,1},{1,2},{2,3},{4,5},{5,6},{6,7},{8,9},{9,10},{10,11},{12,13},{... | collective-permute-start | bytes 90728 | tf_op jit(solution)/shard_map/ppermute | solution.py:23
  65.9 0.5 copy.47
  66.5 1.3 collective-permute-start.5
  67.8 0.6 compare_and_fusion.9
  68.5 0.4 copy.48
  68.9 2.4 %collective-permute-done.5 = f32[10,756]{1,0:T(8,128)S(1)} collective-permute-done((f32[10,756]{1,0:T(8,128)S(1)}, f32[10,756]{1,0:T(8,128)S(1)}, u32[]{:S(2)}, u32[]{:S(2)}) %collective-permute-start.5) | collective-permute-done | bytes 30272 | tf_op jit(solution)/shard_map/ppermute | solution.py:24
  71.4 0.4 copy.49
  71.9 3.7 %collective-permute-done.7 = f32[2,4,32,128]{3,2,1,0:T(8,128)} collective-permute-done((f32[2,4,32,128]{3,2,1,0:T(8,128)}, f32[2,4,32,128]{3,2,1,0:T(8,128)}, u32[]{:S(2)}, u32[]{:S(2)}) %collective-permute-start.7) | collective-permute-done | bytes 131104 | tf_op jit(solution)/shard_map/ppermute | solution.py:24
  75.6 0.8 pad_maximum_fusion.13
  76.4 2.7 %collective-permute-start.8 = (f32[128,128]{1,0:T(8,128)S(1)}, f32[128,128]{1,0:T(8,128)S(1)}, u32[]{:S(2)}, u32[]{:S(2)}) collective-permute-start(f32[128,128]{1,0:T(8,128)S(1)} %bitcast.62), channel_id=1, source_target_pairs={{0,4},{4,8},{8,12},{12,16},{16,20},{20,24},{24,28},{1,5},{5,9},{9,... | collective-permute-start | bytes 196616 | tf_op jit(solution)/shard_map/ppermute | solution.py:23
  79.1 2.6 %collective-permute-start.9 = (f32[128,128]{1,0:T(8,128)S(1)}, f32[128,128]{1,0:T(8,128)S(1)}, u32[]{:S(2)}, u32[]{:S(2)}) collective-permute-start(f32[128,128]{1,0:T(8,128)S(1)} %bitcast.61), channel_id=1, source_target_pairs={{4,0},{8,4},{12,8},{16,12},{20,16},{24,20},{28,24},{5,1},{9,5},{13... | collective-permute-start | bytes 196616 | tf_op jit(solution)/shard_map/ppermute | solution.py:24
  81.7 2.2 %pad_maximum_fusion = f32[2,18,42,138]{3,2,1,0:T(8,128)S(1)} fusion(f32[2,18,42,5]{3,2,1,0:T(8,128)S(1)} %copy.49, f32[2,18,5,128]{3,2,1,0:T(8,128)} %copy-done.12, f32[2,5,32,128]{3,2,1,0:T(8,128)} %copy-done.10, f32[1,8,32,128]{3,2,1,0:T(8,128)} %bitcast.49, f32[1,8,32,128]{3,2,1,0:T(8,128)} %copy-done.3, f32[2,5,32,128]{3,2,1,0:T(8,128)} %copy-done.9, ...), kind=kLoop, calls=%fused_computation.1 | loop fusion | flops 1460592 | bytes 1669248 | tf_op jit(solution)/shard_map/concatenate | solution.py:50
  83.9 0.9 collective-permute-done.9
  84.9 1.0 pad_maximum_fusion.3
  86.1 0.3 copy.53
  86.4 0.7 reshape.304
  87.1 3.7 %collective-permute-start.10 = (f32[8,640]{1,0:T(8,128)}, f32[8,640]{1,0:T(8,128)}, u32[]{:S(2)}, u32[]{:S(2)}) collective-permute-start(f32[8,640]{1,0:T(8,128)} %reshape.304), channel_id=1, source_target_pairs={{0,1},{1,2},{2,3},{4,5},{5,6},{6,7},{8,9},{9,10},{10,11},{12,13},{... | collective-permute-start | bytes 61448 | tf_op jit(solution)/shard_map/ppermute | solution.py:23
  90.8 0.3 copy.54
  91.1 0.7 reshape.306
  91.8 1.5 collective-permute-start.11
  93.5 0.9 reshape.305
  94.4 0.3 copy.55
  94.7 2.0 %collective-permute-done.11 = f32[8,640]{1,0:T(8,128)} collective-permute-done((f32[8,640]{1,0:T(8,128)}, f32[8,640]{1,0:T(8,128)}, u32[]{:S(2)}, u32[]{:S(2)}) %collective-permute-start.11) | collective-permute-done | bytes 20512 | tf_op jit(solution)/shard_map/ppermute | solution.py:24
  96.7 1.4 reshape.307
  98.1 1.1 copy.56
  99.3 1.7 %pad_maximum_fusion.1 = f32[2,16,40,136]{3,2,1,0:T(8,128)S(1)} fusion(f32[2,16,40,4]{3,2,1,0:T(8,128)S(1)} %copy.56, f32[2,16,4,128]{3,2,1,0:T(4,128)} %bitcast.58, f32[2,4,32,128]{3,2,1,0:T(8,128)} %collective-permute-done.7, f32[1,8,32,128]{3,2,1,0:T(8,128)S(1)} %bitcast.47, f32[1,8,32,128]{3,2,1,0:T(8,128)S(1)} %copy-done.2, ...), kind=kLoop, calls=%fused_computation.2 | loop fusion | flops 1218560 | bytes 1392640 | tf_op jit(solution)/shard_map/concatenate | solution.py:50
  101.0 0.6 copy-done.20
  101.6 2.4 %fusion.6 = (f32[16,40,136]{2,1,0:T(8,128)S(1)}, f32[16,40,136]{2,1,0:T(8,128)S(1)}, f32[16,40,136]{2,1,0:T(8,128)S(1)}, f32[16,40,136]{2,1,0:T(8,128)S(1)}, f32...) fusion(f32[18,42,138]{2,1,0:T(8,128)S(1)} %get-tuple-element.12, ...), kind=kLoop, calls=%fused_computation.16 | loop fusion | flops 3742720 | bytes 8008456 | tf_op jit(solution)/shard_map/jit(_where)/select_n | solution.py:177
  104.0 0.3 fusion
  104.3 0.4 copy-done.23
  104.6 2.2 %fusion.12 = f32[14,38,134]{2,1,0:T(8,128)S(1)} fusion(f32[16,40,136]{2,1,0:T(8,128)S(1)} %fusion, f32[16,40,136]{2,1,0:T(8,128)S(1)} %get-tuple-element.4, f32[16,40,136]{2,1,0:T(8,128)S(1)} %get-tuple-element.10, f32[16,40,136]{2,1,0:T(8,128)S(1)} %get-tuple-element.9, f32[16,40,136]{2,1,0:T(8,128)S(1)} %get-tuple-element.8, ...), kind=kLoop, calls=%fused_computation.39 | loop fusion | flops 1283184 | bytes 4563098 | tf_op jit(solution)/shard_map/jit(_where)/select_n | solution.py:177
  106.9 1.9 %fusion.25 = f32[12,36,132]{2,1,0:T(8,128)S(1)} fusion(f32[16,40,136]{2,1,0:T(8,128)S(1)} %fusion, f32[14,38,134]{2,1,0:T(8,128)S(1)} %fusion.12, f32[16,40,136]{2,1,0:T(8,128)S(1)} %get-tuple-element.10, f32[16,40,136]{2,1,0:T(8,128)S(1)} %get-tuple-element.9, f32[16,40,136]{2,1,0:T(8,128)S(1)} %get-tuple-element.8, ...), kind=kLoop, calls=%fused_computation.63 | loop fusion | flops 1026432 | bytes 3650100 | tf_op jit(solution)/shard_map/jit(_where)/select_n | solution.py:177
  108.8 1.6 %fusion.34 = f32[10,34,130]{2,1,0:T(8,128)S(1)} fusion(f32[16,40,136]{2,1,0:T(8,128)S(1)} %fusion, f32[12,36,132]{2,1,0:T(8,128)S(1)} %fusion.25, f32[16,40,136]{2,1,0:T(8,128)S(1)} %get-tuple-element.10, f32[16,40,136]{2,1,0:T(8,128)S(1)} %get-tuple-element.9, f32[16,40,136]{2,1,0:T(8,128)S(1)} %get-tuple-element.8, ...), kind=kLoop, calls=%fused_computation.80 | loop fusion | flops 795600 | bytes 2829270 | tf_op jit(solution)/shard_map/jit(_where)/select_n | solution.py:177
  110.4 1.8 %fusion.50 = (f32[]{:T(128)}, f32[8,32,128]{2,1,0:T(8,128)}) fusion(f32[16,40,136]{2,1,0:T(8,128)S(1)} %fusion, f32[10,34,130]{2,1,0:T(8,128)S(1)} %fusion.34, f32[16,40,136]{2,1,0:T(8,128)S(1)} %get-tuple-element.10, f32[16,40,136]{2,1,0:T(8,128)S(1)} %get-tuple-element.9, f32[16,40,136]{2,1,0:T(8,128)S(1)} %get-tuple-element.8, ...), kind=kLoop, calls=%fused_computation.115 | loop fusion | flops 524287 | bytes 2097156 | tf_op jit(solution)/shard_map/reduce_sum | solution.py:185
  112.3 0.8 broadcast_in_dim.92
  113.1 30.3 %all_to_all.16 = f32[512,1,1]{2,1,0:T(1,128)S(1)} all-to-all(f32[512,1,1]{2,1,0:T(1,128)S(1)} %broadcast_in_dim.92), channel_id=1, replica_groups=mesh['gx'=16,'gy'=8,'gz'=4] {'gx','gy','gz'}, dimensions={0} | all-to-all | bytes 4096 | tf_op jit(solution)/shard_map/all_to_all | solution.py:187
  143.4 1.1 reduce_sum.49
  (85 shorter events, 2.6 us)
Async XLA Ops:
  2.3 48.4 %copy-start.3 = (f32[1,8,32,128]{3,2,1,0:T(8,128)}, f32[1,8,32,128]{3,2,1,0:T(8,128)S(1)}, u32[]{:S(2)}) copy-start(f32[1,8,32,128]{3,2,1,0:T(8,128)S(1)} %multiply_bitcast_fusion) | copy-start | bytes 393220
  3.3 36.2 %copy-start.8 = (f32[8,32,128]{2,1,0:T(8,128)S(1)}, f32[8,32,128]{2,1,0:T(8,128)}, u32[]{:S(2)}) copy-start(f32[8,32,128]{2,1,0:T(8,128)} %param.19) | copy-start | bytes 393220
  3.3 36.1 %collective-permute-start = (f32[2,5,32,128]{3,2,1,0:T(8,128)S(1)}, f32[2,5,32,128]{3,2,1,0:T(8,128)S(1)}, u32[]{:S(2)}, u32[]{:S(2)}) collective-permute-start(f32[2,5,32,128]{3,2,1,0:T(8,128)S(1)} %get-tuple-element.23), channel_id=1, source_target_pairs={{0,32},{32,64},{64,96},{96,128},{128,160},{160,192},{192,224},{224... | collective-permute-start | bytes 491528 | tf_op jit(solution)/shard_map/ppermute | solution.py:23
  14.9 24.5 %collective-permute-start.1 = (f32[2,5,32,128]{3,2,1,0:T(8,128)S(1)}, f32[2,5,32,128]{3,2,1,0:T(8,128)S(1)}, u32[]{:S(2)}, u32[]{:S(2)}) collective-permute-start(f32[2,5,32,128]{3,2,1,0:T(8,128)S(1)} %get-tuple-element.24), channel_id=1, source_target_pairs={{32,0},{64,32},{96,64},{128,96},{160,128},{192,160},{224,192},{256... | collective-permute-start | bytes 491528 | tf_op jit(solution)/shard_map/ppermute | solution.py:24
  22.5 30.9 %all-to-all-start = ((f32[128,1,520]{2,1,0:T(1,128)}), f32[128,1,520]{2,1,0:T(1,128)S(1)}, u32[]{:S(2)}, u32[]{:S(2)}) async-start(f32[128,1,520]{2,1,0:T(1,128)} %all_to_all.13), calls=%async_computation | async-start | bytes 655360 | tf_op jit(solution)/shard_map/all_to_all | solution.py:126
  39.5 11.3 %copy-start.9 = (f32[2,5,32,128]{3,2,1,0:T(8,128)}, f32[2,5,32,128]{3,2,1,0:T(8,128)S(1)}, u32[]{:S(2)}) copy-start(f32[2,5,32,128]{3,2,1,0:T(8,128)S(1)} %collective-permute-done) | copy-start | bytes 491524
  39.5 11.3 %copy-start.10 = (f32[2,5,32,128]{3,2,1,0:T(8,128)}, f32[2,5,32,128]{3,2,1,0:T(8,128)S(1)}, u32[]{:S(2)}) copy-start(f32[2,5,32,128]{3,2,1,0:T(8,128)S(1)} %collective-permute-done.1) | copy-start | bytes 491524
  39.6 8.4 %collective-permute-start.2 = (f32[180,128]{1,0:T(8,128)S(1)}, f32[180,128]{1,0:T(8,128)S(1)}, u32[]{:S(2)}, u32[]{:S(2)}) collective-permute-start(f32[180,128]{1,0:T(8,128)S(1)} %reshape.290), channel_id=1, source_target_pairs={{0,4},{4,8},{8,12},{12,16},{16,20},{20,24},{24,28},{1,5},{5,9},{9,... | collective-permute-start | bytes 276488 | tf_op jit(solution)/shard_map/ppermute | solution.py:23
  43.1 7.5 %collective-permute-start.3 = (f32[180,128]{1,0:T(8,128)S(1)}, f32[180,128]{1,0:T(8,128)S(1)}, u32[]{:S(2)}, u32[]{:S(2)}) collective-permute-start(f32[180,128]{1,0:T(8,128)S(1)} %reshape.292), channel_id=1, source_target_pairs={{4,0},{8,4},{12,8},{16,12},{20,16},{24,20},{28,24},{5,1},{9,5},{13... | collective-permute-start | bytes 276488 | tf_op jit(solution)/shard_map/ppermute | solution.py:24
  48.0 5.4 %copy-start.11 = (f32[2,18,5,128]{3,2,1,0:T(8,128)}, f32[2,18,5,128]{3,2,1,0:T(8,128)S(1)}, u32[]{:S(2)}) copy-start(f32[2,18,5,128]{3,2,1,0:T(8,128)S(1)} %reshape.291) | copy-start | bytes 276484
  50.7 2.8 %copy-start.12 = (f32[2,18,5,128]{3,2,1,0:T(8,128)}, f32[2,18,5,128]{3,2,1,0:T(8,128)S(1)}, u32[]{:S(2)}) copy-start(f32[2,18,5,128]{3,2,1,0:T(8,128)S(1)} %reshape.293) | copy-start | bytes 276484
  54.5 1.0 copy-start.19
  55.5 5.0 %copy-start.4 = (f32[256,128]{1,0:T(8,128)}, f32[256,128]{1,0:T(8,128)S(1)}, u32[]{:S(2)}) copy-start(f32[256,128]{1,0:T(8,128)S(1)} %get-tuple-element.28) | copy-start | bytes 393220
  55.6 20.0 %copy-start = (f32[1,8,32,128]{3,2,1,0:T(8,128)}, f32[1,8,32,128]{3,2,1,0:T(8,128)S(1)}, u32[]{:S(2)}) copy-start(f32[1,8,32,128]{3,2,1,0:T(8,128)S(1)} %add_bitcast_fusion) | copy-start | bytes 393220
  56.3 15.5 %collective-permute-start.6 = (f32[2,4,32,128]{3,2,1,0:T(8,128)}, f32[2,4,32,128]{3,2,1,0:T(8,128)S(1)}, u32[]{:S(2)}, u32[]{:S(2)}) collective-permute-start(f32[2,4,32,128]{3,2,1,0:T(8,128)} %get-tuple-element.25), channel_id=1, source_target_pairs={{0,32},{32,64},{64,96},{96,128},{128,160},{160,192},{192,224},{224... | collective-permute-start | bytes 393224 | tf_op jit(solution)/shard_map/ppermute | solution.py:23
  60.6 15.0 %collective-permute-start.7 = (f32[2,4,32,128]{3,2,1,0:T(8,128)}, f32[2,4,32,128]{3,2,1,0:T(8,128)}, u32[]{:S(2)}, u32[]{:S(2)}) collective-permute-start(f32[2,4,32,128]{3,2,1,0:T(8,128)} %get-tuple-element.26), channel_id=1, source_target_pairs={{32,0},{64,32},{96,64},{128,96},{160,128},{192,160},{224,192},{256... | collective-permute-start | bytes 393224 | tf_op jit(solution)/shard_map/ppermute | solution.py:24
  62.8 5.6 %collective-permute-start.4 = (f32[10,756]{1,0:T(8,128)S(1)}, f32[10,756]{1,0:T(8,128)S(1)}, u32[]{:S(2)}, u32[]{:S(2)}) collective-permute-start(f32[10,756]{1,0:T(8,128)S(1)} %reshape.294), channel_id=1, source_target_pairs={{0,1},{1,2},{2,3},{4,5},{5,6},{6,7},{8,9},{9,10},{10,11},{12,13},{... | collective-permute-start | bytes 90728 | tf_op jit(solution)/shard_map/ppermute | solution.py:23
  66.3 9.2 %copy-start.5 = (f32[256,128]{1,0:T(8,128)S(1)}, f32[256,128]{1,0:T(8,128)}, u32[]{:S(2)}) copy-start(f32[256,128]{1,0:T(8,128)} %copy-done.4) | copy-start | bytes 393220
  66.5 4.8 %collective-permute-start.5 = (f32[10,756]{1,0:T(8,128)S(1)}, f32[10,756]{1,0:T(8,128)S(1)}, u32[]{:S(2)}, u32[]{:S(2)}) collective-permute-start(f32[10,756]{1,0:T(8,128)S(1)} %reshape.296), channel_id=1, source_target_pairs={{1,0},{2,1},{3,2},{5,4},{6,5},{7,6},{9,8},{10,9},{11,10},{13,12},{... | collective-permute-start | bytes 90728 | tf_op jit(solution)/shard_map/ppermute | solution.py:24
  71.9 7.3 %copy-start.13 = (f32[2,4,32,128]{3,2,1,0:T(8,128)}, f32[2,4,32,128]{3,2,1,0:T(8,128)S(1)}, u32[]{:S(2)}) copy-start(f32[2,4,32,128]{3,2,1,0:T(8,128)S(1)} %collective-permute-done.6) | copy-start | bytes 393220
  76.4 7.5 %collective-permute-start.8 = (f32[128,128]{1,0:T(8,128)S(1)}, f32[128,128]{1,0:T(8,128)S(1)}, u32[]{:S(2)}, u32[]{:S(2)}) collective-permute-start(f32[128,128]{1,0:T(8,128)S(1)} %bitcast.62), channel_id=1, source_target_pairs={{0,4},{4,8},{8,12},{12,16},{16,20},{20,24},{24,28},{1,5},{5,9},{9,... | collective-permute-start | bytes 196616 | tf_op jit(solution)/shard_map/ppermute | solution.py:23
  79.1 5.7 %copy-start.1 = (f32[1,8,32,128]{3,2,1,0:T(8,128)S(1)}, f32[1,8,32,128]{3,2,1,0:T(8,128)}, u32[]{:S(2)}) copy-start(f32[1,8,32,128]{3,2,1,0:T(8,128)} %copy-done) | copy-start | bytes 393220
  79.1 5.7 %copy-start.6 = (f32[256,128]{1,0:T(8,128)S(1)}, f32[256,128]{1,0:T(8,128)}, u32[]{:S(2)}) copy-start(f32[256,128]{1,0:T(8,128)} %copy-done.4) | copy-start | bytes 393220
  79.1 5.7 %collective-permute-start.9 = (f32[128,128]{1,0:T(8,128)S(1)}, f32[128,128]{1,0:T(8,128)S(1)}, u32[]{:S(2)}, u32[]{:S(2)}) collective-permute-start(f32[128,128]{1,0:T(8,128)S(1)} %bitcast.61), channel_id=1, source_target_pairs={{4,0},{8,4},{12,8},{16,12},{20,16},{24,20},{28,24},{5,1},{9,5},{13... | collective-permute-start | bytes 196616 | tf_op jit(solution)/shard_map/ppermute | solution.py:24
  81.7 3.1 %copy-start.14 = (f32[2,4,32,128]{3,2,1,0:T(8,128)S(1)}, f32[2,4,32,128]{3,2,1,0:T(8,128)}, u32[]{:S(2)}) copy-start(f32[2,4,32,128]{3,2,1,0:T(8,128)} %copy-done.13) | copy-start | bytes 393220
  83.9 2.2 %copy-start.16 = (f32[128,128]{1,0:T(8,128)}, f32[128,128]{1,0:T(8,128)S(1)}, u32[]{:S(2)}) copy-start(f32[128,128]{1,0:T(8,128)S(1)} %collective-permute-done.8) | copy-start | bytes 196612
  84.9 1.3 copy-start.18
  87.1 6.3 %collective-permute-start.10 = (f32[8,640]{1,0:T(8,128)}, f32[8,640]{1,0:T(8,128)}, u32[]{:S(2)}, u32[]{:S(2)}) collective-permute-start(f32[8,640]{1,0:T(8,128)} %reshape.304), channel_id=1, source_target_pairs={{0,1},{1,2},{2,3},{4,5},{5,6},{6,7},{8,9},{9,10},{10,11},{12,13},{... | collective-permute-start | bytes 61448 | tf_op jit(solution)/shard_map/ppermute | solution.py:23
  91.8 4.8 %collective-permute-start.11 = (f32[8,640]{1,0:T(8,128)}, f32[8,640]{1,0:T(8,128)}, u32[]{:S(2)}, u32[]{:S(2)}) collective-permute-start(f32[8,640]{1,0:T(8,128)} %reshape.306), channel_id=1, source_target_pairs={{1,0},{2,1},{3,2},{5,4},{6,5},{7,6},{9,8},{10,9},{11,10},{13,12},{... | collective-permute-start | bytes 61448 | tf_op jit(solution)/shard_map/ppermute | solution.py:24
  93.4 5.8 %copy-start.2 = (f32[1,8,32,128]{3,2,1,0:T(8,128)S(1)}, f32[1,8,32,128]{3,2,1,0:T(8,128)}, u32[]{:S(2)}) copy-start(f32[1,8,32,128]{3,2,1,0:T(8,128)} %copy-done) | copy-start | bytes 393220
  93.4 5.8 %copy-start.7 = (f32[256,128]{1,0:T(8,128)S(1)}, f32[256,128]{1,0:T(8,128)}, u32[]{:S(2)}) copy-start(f32[256,128]{1,0:T(8,128)} %copy-done.4) | copy-start | bytes 393220
  93.4 5.8 %copy-start.15 = (f32[2,4,32,128]{3,2,1,0:T(8,128)S(1)}, f32[2,4,32,128]{3,2,1,0:T(8,128)}, u32[]{:S(2)}) copy-start(f32[2,4,32,128]{3,2,1,0:T(8,128)} %copy-done.13) | copy-start | bytes 393220
  93.5 5.8 %copy-start.17 = (f32[128,128]{1,0:T(8,128)S(1)}, f32[128,128]{1,0:T(8,128)}, u32[]{:S(2)}) copy-start(f32[128,128]{1,0:T(8,128)} %copy-done.16) | copy-start | bytes 196612
  100.9 0.7 copy-start.20
  104.0 0.7 copy-start.23
  104.6 2.2 %copy-start.21 = (pred[132]{0:T(512)(128)(4,1)S(1)}, pred[132]{0:T(512)(128)(4,1)}, u32[]{:S(2)}) copy-start(pred[132]{0:T(512)(128)(4,1)} %compare_and_fusion.6) | copy-start | bytes 400
  106.9 1.9 %copy-start.22 = (pred[130]{0:T(512)(128)(4,1)S(1)}, pred[130]{0:T(512)(128)(4,1)}, u32[]{:S(2)}) copy-start(pred[130]{0:T(512)(128)(4,1)} %compare_and_fusion.9) | copy-start | bytes 394

commit v6 on v2

--- a/solution.py
+++ b/solution.py
@@ -143,23 +143,43 @@
     forcing = charge + injected
 
     halo = SWEEPS + 1
+    lo, hx, hy, hz = halo, halo + cells_x, halo + cells_y, halo + cells_z
+    buffer = jnp.zeros(
+        (4, cells_x + 2 * halo, cells_y + 2 * halo, cells_z + 2 * halo), jnp.float32
+    )
     early = jnp.stack([permittivity, initial], axis=0)
     early_prev, early_next = exchange_x(early, halo)
     late = jnp.stack([forcing, coupling], axis=0)
     late_prev, late_next = exchange_x(late, halo - 1)
-    pad = jnp.zeros((2, 1, cells_y, cells_z), jnp.float32)
-    late_prev = jnp.concatenate([pad, late_prev], axis=1)
-    late_next = jnp.concatenate([late_next, pad], axis=1)
-    fields_x = jnp.concatenate(
-        [
-            jnp.concatenate([early_prev, early, early_next], axis=1),
-            jnp.concatenate([late_prev, late, late_next], axis=1),
-        ],
-        axis=0,
-    )
-    wide = with_wide_halo(fields_x, halo)
-    eps_w, initial_w, forcing_w, coupling_w = wide[0], wide[1], wide[2], wide[3]
-    potential = initial_w
+    buffer = buffer.at[0:2, lo:hx, lo:hy, lo:hz].set(early)
+    buffer = buffer.at[2:4, lo:hx, lo:hy, lo:hz].set(late)
+    buffer = buffer.at[0:2, 0:lo, lo:hy, lo:hz].set(early_prev)
+    buffer = buffer.at[0:2, hx:, lo:hy, lo:hz].set(early_next)
+    buffer = buffer.at[2:4, 1:lo, lo:hy, lo:hz].set(late_prev)
+    buffer = buffer.at[2:4, hx:hx + halo - 1, lo:hy, lo:hz].set(late_next)
+
+    nf, nx, ny, nz = buffer.shape
+    slab_y = (nf * nx * halo, cells_z)
+    prev, nxt = exchange(
+        buffer[:, :, lo:lo + halo, lo:hz].reshape(slab_y),
+        buffer[:, :, hy - halo:hy, lo:hz].reshape(slab_y),
+        "gy",
+    )
+    buffer = buffer.at[:, :, 0:lo, lo:hz].set(prev.reshape(nf, nx, halo, cells_z))
+    buffer = buffer.at[:, :, hy:, lo:hz].set(nxt.reshape(nf, nx, halo, cells_z))
+
+    def pack(a):
+        return jnp.moveaxis(a, 3, 1).reshape(nf * halo, nx * ny)
+
+    def unpack(a):
+        return jnp.moveaxis(a.reshape(nf, halo, nx, ny), 1, 3)
+
+    prev, nxt = exchange(
+        pack(buffer[..., lo:lo + halo]), pack(buffer[..., hz - halo:hz]), "gz"
+    )
+    buffer = buffer.at[..., 0:lo].set(unpack(prev))
+    buffer = buffer.at[..., hz:].set(unpack(nxt))
+    eps_w, potential, forcing_w, coupling_w = buffer[0], buffer[1], buffer[2], buffer[3]
 
     coefficients = face_coefficients(eps_w)
     diagonal_sum = coefficients[0]

time: 142 us -> 282 us (1.99)
  local copies, waits for them, and re-layouts: 12.3 us -> 149 us
  waiting for transfers between devices: 29.4 us -> 12.1 us
  starting transfers between devices: 40.2 us -> 51.3 us
  other arithmetic: 26.4 us -> 34.3 us
    scatter x0 -> x10, local copies, waits for them, and re-layouts: none -> 116 us  [the longest x1 23.9 us: on_device(): buffer = buffer.at[..., hz:].set(unpack(nxt))]
    ppermute x4, waiting for transfers between devices: 22.1 us -> 0.01 us  [exchange(): from_next = lax.ppermute(lo, axis, backward)]
    ppermute x4, starting transfers between devices: 15.4 us -> 30.4 us  [exchange(): from_prev = lax.ppermute(hi, axis, forward)]
    reshape x8, local copies, waits for them, and re-layouts: 2.99 us -> 15.9 us  [the longest x4 9.16 us: unpack(): return jnp.moveaxis(a.reshape(nf, halo, nx, ny), 1, 3)]
    concatenate x2 -> x0, other arithmetic: 6.02 us -> none  [the longest x1 4.81 us: with_wide_halo(): return jnp.concatenate([unpack(prev), fields, unpack(nxt)], axis=3)]
    another operation x2 -> x3, other arithmetic: 0.04 us -> 4.25 us  [on_device(): early = jnp.stack([permittivity, initial], axis=0)]
    another operation x0 -> x3, local copies, waits for them, and re-layouts: none -> 3.89 us
    slice x1, other arithmetic: 0.04 us -> 3.9 us  [on_device(): buffer[:, :, lo:lo + halo, lo:hz].reshape(slab_y)]
  transfers between devices with their start and end apart: 9 -> 9, of which waited for: 5 -> 3; matrix products, arithmetic and copies ran while one was open for 5% -> 33% of each run, Pallas kernels for 0% -> 0%
where the time goes in v6:
time: 282 us; the launch traced here: 281 us
  local copies, waits for them, and re-layouts  149 us (53%)
  starting transfers between devices  51.3 us (18%)
  other arithmetic  34.3 us (12%)
  blocking collectives  30.8 us (11%)
  waiting for transfers between devices  12.1 us (4%)
  between operations  2.87 us (1%)
    all_to_all x1, blocking collectives, on_device(): lax.all_to_all(jnp.full((device_count,), local_total), ('gx', 'gy', 'gz')...  30.8 us
    ppermute x4, starting transfers between devices, exchange(): from_prev = lax.ppermute(hi, axis, forward)  30.4 us
    scatter x1, local copies, waits for them, and re-layouts, on_device(): buffer = buffer.at[..., hz:].set(unpack(nxt))  23.9 us
    scatter x1, local copies, waits for them, and re-layouts, on_device(): buffer.at[:, :, 0:lo, lo:hz].set(prev.reshape(nf, nx, halo, cells_z))  23.3 us
    scatter x1, local copies, waits for them, and re-layouts, on_device(): buffer = buffer.at[:, :, hy:, lo:hz].set(nxt.reshape(nf, nx, halo, cells_z))  22.1 us
    scatter x1, local copies, waits for them, and re-layouts, on_device(): buffer = buffer.at[..., 0:lo].set(unpack(prev))  20.8 us
    all_to_all x1, starting transfers between devices, on_device(): lax.all_to_all(send, ('gx', 'gy'), split_axis=0, concat_axis=0, tiled=True)  15 us
    all_to_all x1, waiting for transfers between devices, on_device(): lax.all_to_all(send, ('gx', 'gy'), split_axis=0, concat_axis=0, tiled=True)  9.48 us
  transfers between devices with their start and end apart: 9, of which 3 were waited for; matrix products, arithmetic and copies ran while one was open for 33% of the time, Pallas kernels for 0%

profile of v6, /device:TPU:1, one launch (start us, length us, event | category | flops | bytes accessed | tf_op | source)
XLA Modules:
  0.0 280.9 jit_solution(9020235119059640719)
XLA Ops:
  0.6 0.8 select_reduce_fusion.1
  1.4 0.9 multiply_bitcast_fusion
  2.3 1.7 fusion.46
  4.0 1.3 collective-permute-start.1
  5.3 12.8 %collective-permute-start = (f32[2,5,32,128]{3,2,1,0:T(8,128)}, f32[2,5,32,128]{3,2,1,0:T(8,128)}, u32[]{:S(2)}, u32[]{:S(2)}) collective-permute-start(f32[2,5,32,128]{3,2,1,0:T(8,128)} %get-tuple-element.144), channel_id=1, source_target_pairs={{0,32},{32,64},{64,96},{96,128},{128,160},{160,192},{192,224},{224... | collective-permute-start | bytes 491528 | tf_op jit(solution)/shard_map/ppermute | solution.py:22
  18.1 0.7 convert_bitcast_fusion
  18.7 0.9 convert_reduce_fusion
  19.6 0.7 compare_select_fusion
  20.4 0.9 select_reduce_fusion
  21.5 1.5 scatter_custom_fusion
  23.0 1.4 all_to_all.13
  24.4 15.0 %all-to-all-start = ((f32[128,1,520]{2,1,0:T(1,128)}), f32[128,1,520]{2,1,0:T(1,128)S(1)}, u32[]{:S(2)}, u32[]{:S(2)}) async-start(f32[128,1,520]{2,1,0:T(1,128)} %all_to_all.13), calls=%async_computation | async-start | bytes 655360 | tf_op jit(solution)/shard_map/all_to_all | solution.py:127
  39.4 1.6 pad_maximum_fusion
  41.6 0.6 compare_and_fusion.10
  42.2 0.6 compare_and_fusion.7
  43.9 0.8 and_reduce_fusion
  44.7 0.6 compare_and_fusion.6
  45.5 9.5 %all-to-all-done = f32[128,1,520]{2,1,0:T(1,128)S(1)} async-done(((f32[128,1,520]{2,1,0:T(1,128)}), f32[128,1,520]{2,1,0:T(1,128)S(1)}, u32[]{:S(2)}, u32[]{:S(2)}) %all-to-all-start) | async-done | bytes 266272 | tf_op jit(solution)/shard_map/all_to_all | solution.py:127
  54.9 0.8 reduce.26
  57.1 0.6 copy-done
  57.7 0.7 fusion.48
  58.4 1.3 collective-permute-start.3
  59.7 8.6 %collective-permute-start.2 = (f32[2,4,32,128]{3,2,1,0:T(8,128)}, f32[2,4,32,128]{3,2,1,0:T(8,128)}, u32[]{:S(2)}, u32[]{:S(2)}) collective-permute-start(f32[2,4,32,128]{3,2,1,0:T(8,128)} %get-tuple-element.142), channel_id=1, source_target_pairs={{0,32},{32,64},{64,96},{96,128},{128,160},{160,192},{192,224},{224... | collective-permute-start | bytes 393224 | tf_op jit(solution)/shard_map/ppermute | solution.py:22
  68.8 1.5 scatter.40
  70.3 0.7 pad_maximum_fusion.1
  71.1 6.6 %scatter.44 = f32[4,18,42,138]{3,2,1,0:T(8,128)S(1)} dynamic-update-slice(f32[4,18,42,138]{3,2,1,0:T(8,128)S(1)} %scatter.40, f32[2,8,32,128]{3,2,1,0:T(8,128)} %pad_maximum_fusion.1, s32[]{:T(128)} %constant.381.clone.1, s32[]{:T(128)} %constant.382.clone.1, s32[]{:T(128)} %constant.382.clone.1, s32[]{:T(128)} %constant.382.clone.1) | dynamic-update-slice | bytes 524292 | tf_op jit(solution)/shard_map/scatter | solution.py:155
  77.6 4.6 %scatter.45 = f32[4,18,42,138]{3,2,1,0:T(8,128)S(1)} dynamic-update-slice(f32[4,18,42,138]{3,2,1,0:T(8,128)S(1)} %scatter.44, f32[2,5,32,128]{3,2,1,0:T(8,128)} %collective-permute-done, s32[]{:T(128)} %constant.368.clone.1, s32[]{:T(128)} %constant.368.clone.1, s32[]{:T(128)} %constant.382.clone.1, s32[]{:T(128)} %constant.382.clone.1) | dynamic-update-slice | bytes 327684 | tf_op jit(solution)/shard_map/scatter | solution.py:156
  82.3 4.6 %scatter.46 = f32[4,18,42,138]{3,2,1,0:T(8,128)S(1)} dynamic-update-slice(f32[4,18,42,138]{3,2,1,0:T(8,128)S(1)} %scatter.45, f32[2,5,32,128]{3,2,1,0:T(8,128)} %collective-permute-done.1, s32[]{:T(128)} %constant.368.clone.1, s32[]{:T(128)} %constant.383.clone.1, s32[]{:T(128)} %constant.382.clone.1, s32[]{:T(128)} %constant.382.clone.1) | dynamic-update-slice | bytes 327684 | tf_op jit(solution)/shard_map/scatter | solution.py:157
  87.0 4.0 %scatter.49 = f32[4,18,42,138]{3,2,1,0:T(8,128)S(1)} dynamic-update-slice(f32[4,18,42,138]{3,2,1,0:T(8,128)S(1)} %scatter.46, f32[2,4,32,128]{3,2,1,0:T(8,128)} %collective-permute-done.2, s32[]{:T(128)} %constant.381.clone.1, s32[]{:T(128)} %constant.384.clone.1, s32[]{:T(128)} %constant.382.clone.1, s32[]{:T(128)} %constant.382.clone.1) | dynamic-update-slice | bytes 262148 | tf_op jit(solution)/shard_map/scatter | solution.py:158
  91.0 4.0 %scatter.50 = f32[4,18,42,138]{3,2,1,0:T(8,128)S(1)} dynamic-update-slice(f32[4,18,42,138]{3,2,1,0:T(8,128)S(1)} %scatter.49, f32[2,4,32,128]{3,2,1,0:T(8,128)} %collective-permute-done.3, s32[]{:T(128)} %constant.381.clone.1, s32[]{:T(128)} %constant.383.clone.1, s32[]{:T(128)} %constant.382.clone.1, s32[]{:T(128)} %constant.382.clone.1) | dynamic-update-slice | bytes 262148 | tf_op jit(solution)/shard_map/scatter | solution.py:159
  95.0 0.8 slice.741
  95.9 1.7 reshape.657
  97.5 4.5 %collective-permute-start.4 = (f32[360,128]{1,0:T(8,128)}, f32[360,128]{1,0:T(8,128)}, u32[]{:S(2)}, u32[]{:S(2)}) collective-permute-start(f32[360,128]{1,0:T(8,128)} %reshape.657), channel_id=1, source_target_pairs={{0,4},{4,8},{8,12},{12,16},{16,20},{20,24},{24,28},{1,5},{5,9},{9,... | collective-permute-start | bytes 552968 | tf_op jit(solution)/shard_map/ppermute | solution.py:22
  102.0 0.8 broadcast_and_fusion.2
  102.8 2.0 collective-permute-done.4
  104.8 1.7 reshape.658
  106.5 3.9 %fusion.65 = (f32[4,18,5,128]{3,2,1,0:T(8,128)}, f32[4,18,5,128]{3,2,1,0:T(8,128)}) fusion(f32[4,18,42,138]{3,2,1,0:T(8,128)S(1)} %scatter.50, f32[4,18,5,128]{3,2,1,0:T(8,128)} %reshape.658, s32[]{:T(128)} %bitcast.7, s32[]{:T(128)} %bitcast.8, pred[]{:T(512)} %and_reduce_fusion), kind=kLoop, calls=%fused_computation.160 | loop fusion | flops 46080 | bytes 921609 | tf_op jit(solution)/shard_map/slice | solution.py:164
  110.3 1.7 reshape.661
  112.0 2.1 collective-permute-start.5
  114.1 0.8 broadcast_and_fusion.3
  114.9 23.3 %scatter.51 = f32[4,18,42,138]{3,2,1,0:T(8,128)S(1)} dynamic-update-slice(f32[4,18,42,138]{3,2,1,0:T(8,128)S(1)} %scatter.50, f32[4,18,5,128]{3,2,1,0:T(8,128)} %get-tuple-element.138, s32[]{:T(128)} %constant.368.clone.1, s32[]{:T(128)} %constant.368.clone.1, s32[]{:T(128)} %bitcast.7, s32[]{:T(128)} %bitcast.8) | dynamic-update-slice | bytes 368644 | tf_op jit(solution)/shard_map/scatter | solution.py:168
  138.2 1.7 reshape.662
  139.9 22.1 %scatter.54 = f32[4,18,42,138]{3,2,1,0:T(8,128)S(1)} dynamic-update-slice(f32[4,18,42,138]{3,2,1,0:T(8,128)S(1)} %scatter.51, f32[4,18,5,128]{3,2,1,0:T(8,128)} %reshape.662, s32[]{:T(128)} %constant.368.clone.1, s32[]{:T(128)} %constant.368.clone.1, s32[]{:T(128)} %constant.388.clone.1, s32[]{:T(128)} %constant.382.clone.1) | dynamic-update-slice | bytes 368644 | tf_op jit(solution)/shard_map/scatter | solution.py:169
  162.0 2.3 slice_bitcast_fusion
  164.3 3.0 %copy.39 = f32[4,5,18,42]{3,2,1,0:T(8,128)} copy(f32[4,5,18,42]{1,3,2,0:T(8,128)} %get-tuple-element.135) | data formatting | bytes 120960 | tf_op jit(solution)/shard_map/transpose | solution.py:172
  167.4 1.7 reshape.665
  169.1 1.3 collective-permute-start.7
  170.3 3.1 %copy.37 = f32[4,5,18,42]{3,2,1,0:T(8,128)} copy(f32[4,5,18,42]{1,3,2,0:T(8,128)} %get-tuple-element.136) | data formatting | bytes 120960 | tf_op jit(solution)/shard_map/transpose | solution.py:172
  173.4 1.7 reshape.663
  175.1 4.6 %collective-permute-start.6 = (f32[20,756]{1,0:T(8,128)}, f32[20,756]{1,0:T(8,128)}, u32[]{:S(2)}, u32[]{:S(2)}) collective-permute-start(f32[20,756]{1,0:T(8,128)} %reshape.663), channel_id=1, source_target_pairs={{0,1},{1,2},{2,3},{4,5},{5,6},{6,7},{8,9},{9,10},{10,11},{12,13},{... | collective-permute-start | bytes 181448 | tf_op jit(solution)/shard_map/ppermute | solution.py:22
  180.8 1.7 reshape.664
  182.5 2.9 %copy.38 = f32[4,5,18,42]{1,3,2,0:T(8,128)} copy(f32[4,5,18,42]{3,2,1,0:T(8,128)} %reshape.664) | data formatting | bytes 120960 | tf_op jit(solution)/shard_map/reshape | solution.py:175
  185.4 20.8 %scatter.66 = f32[4,18,42,138]{3,2,1,0:T(8,128)S(1)} dynamic-update-slice(f32[4,18,42,138]{3,2,1,0:T(8,128)S(1)} %scatter.54, f32[4,18,42,5]{3,2,1,0:T(8,128)} %bitcast.28, s32[]{:T(128)} %constant.368.clone.1, s32[]{:T(128)} %constant.368.clone.1, s32[]{:T(128)} %constant.368.clone.1, s32[]{:T(128)} %constant.368.clone.1) | dynamic-update-slice | bytes 120964 | tf_op jit(solution)/shard_map/scatter | solution.py:180
  206.2 1.7 reshape.666
  207.9 2.9 %copy.40 = f32[4,5,18,42]{1,3,2,0:T(8,128)} copy(f32[4,5,18,42]{3,2,1,0:T(8,128)} %reshape.666) | data formatting | bytes 120960 | tf_op jit(solution)/shard_map/reshape | solution.py:175
  210.8 23.9 %scatter.67 = f32[4,18,42,138]{3,2,1,0:T(8,128)S(1)} dynamic-update-slice(f32[4,18,42,138]{3,2,1,0:T(8,128)S(1)} %scatter.66, f32[4,18,42,5]{3,2,1,0:T(8,128)} %bitcast.27, s32[]{:T(128)} %constant.368.clone.1, s32[]{:T(128)} %constant.368.clone.1, s32[]{:T(128)} %constant.368.clone.1, s32[]{:T(128)} %constant.389.clone.1) | dynamic-update-slice | bytes 120964 | tf_op jit(solution)/shard_map/scatter | solution.py:181
  235.4 2.7 fusion.5
  238.7 2.2 fusion.11
  241.0 1.9 fusion.24
  242.9 1.6 fusion.33
  244.5 1.8 fusion.51
  246.3 0.8 broadcast_in_dim.93
  247.1 30.8 %all_to_all.16 = f32[512,1,1]{2,1,0:T(1,128)S(1)} all-to-all(f32[512,1,1]{2,1,0:T(1,128)S(1)} %broadcast_in_dim.93), channel_id=1, replica_groups=mesh['gx'=16,'gy'=8,'gz'=4] {'gx','gy','gz'}, dimensions={0} | all-to-all | bytes 4096 | tf_op jit(solution)/shard_map/all_to_all | solution.py:222
  277.9 1.1 reduce_sum.49
  (50 shorter events, 6.2 us)
Async XLA Ops:
  0.6 43.3 %copy-start.8 = (s32[4]{0:T(128)S(1)}, s32[4]{0:T(128)}, u32[]{:S(2)}) copy-start(s32[4]{0:T(128)} %constant.386.clone.1) | copy-start | bytes 52
  4.0 78.3 %collective-permute-start.1 = (f32[2,5,32,128]{3,2,1,0:T(8,128)}, f32[2,5,32,128]{3,2,1,0:T(8,128)}, u32[]{:S(2)}, u32[]{:S(2)}) collective-permute-start(f32[2,5,32,128]{3,2,1,0:T(8,128)} %get-tuple-element.143), channel_id=1, source_target_pairs={{32,0},{64,32},{96,64},{128,96},{160,128},{192,160},{224,192},{256... | collective-permute-start | bytes 491528 | tf_op jit(solution)/shard_map/ppermute | solution.py:23
  5.3 72.3 %collective-permute-start = (f32[2,5,32,128]{3,2,1,0:T(8,128)}, f32[2,5,32,128]{3,2,1,0:T(8,128)}, u32[]{:S(2)}, u32[]{:S(2)}) collective-permute-start(f32[2,5,32,128]{3,2,1,0:T(8,128)} %get-tuple-element.144), channel_id=1, source_target_pairs={{0,32},{32,64},{64,96},{96,128},{128,160},{160,192},{192,224},{224... | collective-permute-start | bytes 491528 | tf_op jit(solution)/shard_map/ppermute | solution.py:22
  20.4 36.6 %copy-start.4 = (f32[8,32,128]{2,1,0:T(8,128)S(1)}, f32[8,32,128]{2,1,0:T(8,128)}, u32[]{:S(2)}) copy-start(f32[8,32,128]{2,1,0:T(8,128)} %param.30) | copy-start | bytes 393220
  24.4 30.6 %all-to-all-start = ((f32[128,1,520]{2,1,0:T(1,128)}), f32[128,1,520]{2,1,0:T(1,128)S(1)}, u32[]{:S(2)}, u32[]{:S(2)}) async-start(f32[128,1,520]{2,1,0:T(1,128)} %all_to_all.13), calls=%async_computation | async-start | bytes 655360 | tf_op jit(solution)/shard_map/all_to_all | solution.py:127
  57.0 1.4 copy-start.2
  57.1 0.6 copy-start
  58.4 32.6 %collective-permute-start.3 = (f32[2,4,32,128]{3,2,1,0:T(8,128)}, f32[2,4,32,128]{3,2,1,0:T(8,128)}, u32[]{:S(2)}, u32[]{:S(2)}) collective-permute-start(f32[2,4,32,128]{3,2,1,0:T(8,128)} %get-tuple-element.141), channel_id=1, source_target_pairs={{32,0},{64,32},{96,64},{128,96},{160,128},{192,160},{224,192},{256... | collective-permute-start | bytes 393224 | tf_op jit(solution)/shard_map/ppermute | solution.py:23
  59.7 27.3 %collective-permute-start.2 = (f32[2,4,32,128]{3,2,1,0:T(8,128)}, f32[2,4,32,128]{3,2,1,0:T(8,128)}, u32[]{:S(2)}, u32[]{:S(2)}) collective-permute-start(f32[2,4,32,128]{3,2,1,0:T(8,128)} %get-tuple-element.142), channel_id=1, source_target_pairs={{0,32},{32,64},{64,96},{96,128},{128,160},{160,192},{192,224},{224... | collective-permute-start | bytes 393224 | tf_op jit(solution)/shard_map/ppermute | solution.py:22
  68.8 1.5 copy-start.1
  68.8 1.6 copy-start.3
  97.5 7.3 %collective-permute-start.4 = (f32[360,128]{1,0:T(8,128)}, f32[360,128]{1,0:T(8,128)}, u32[]{:S(2)}, u32[]{:S(2)}) collective-permute-start(f32[360,128]{1,0:T(8,128)} %reshape.657), channel_id=1, source_target_pairs={{0,4},{4,8},{8,12},{12,16},{16,20},{20,24},{24,28},{1,5},{5,9},{9,... | collective-permute-start | bytes 552968 | tf_op jit(solution)/shard_map/ppermute | solution.py:22
  112.0 26.2 %collective-permute-start.5 = (f32[360,128]{1,0:T(8,128)}, f32[360,128]{1,0:T(8,128)}, u32[]{:S(2)}, u32[]{:S(2)}) collective-permute-start(f32[360,128]{1,0:T(8,128)} %reshape.661), channel_id=1, source_target_pairs={{4,0},{8,4},{12,8},{16,12},{20,16},{24,20},{28,24},{5,1},{9,5},{13... | collective-permute-start | bytes 552968 | tf_op jit(solution)/shard_map/ppermute | solution.py:23
  169.1 37.1 %collective-permute-start.7 = (f32[20,756]{1,0:T(8,128)}, f32[20,756]{1,0:T(8,128)}, u32[]{:S(2)}, u32[]{:S(2)}) collective-permute-start(f32[20,756]{1,0:T(8,128)} %reshape.665), channel_id=1, source_target_pairs={{1,0},{2,1},{3,2},{5,4},{6,5},{7,6},{9,8},{10,9},{11,10},{13,12},{... | collective-permute-start | bytes 181448 | tf_op jit(solution)/shard_map/ppermute | solution.py:23
  175.1 5.7 %collective-permute-start.6 = (f32[20,756]{1,0:T(8,128)}, f32[20,756]{1,0:T(8,128)}, u32[]{:S(2)}, u32[]{:S(2)}) collective-permute-start(f32[20,756]{1,0:T(8,128)} %reshape.663), channel_id=1, source_target_pairs={{0,1},{1,2},{2,3},{4,5},{5,6},{6,7},{8,9},{9,10},{10,11},{12,13},{... | collective-permute-start | bytes 181448 | tf_op jit(solution)/shard_map/ppermute | solution.py:22
  234.7 0.7 copy-start.5
  238.1 0.6 copy-start.9
  238.7 2.2 copy-start.7
  240.9 1.9 copy-start.6

commit v7 on v2

--- a/solution.py
+++ b/solution.py
@@ -48,7 +48,10 @@
         return jnp.moveaxis(a.reshape(nf, width, nx, ny), 1, 3)
 
     prev, nxt = exchange(pack(fields[..., :width]), pack(fields[..., -width:]), "gz")
-    return jnp.concatenate([unpack(prev), fields, unpack(nxt)], axis=3)
+    nz = fields.shape[3]
+    wide = jnp.pad(fields, ((0, 0), (0, 0), (0, 0), (width, width)))
+    wide = lax.dynamic_update_slice(wide, unpack(prev), (0, 0, 0, 0))
+    return lax.dynamic_update_slice(wide, unpack(nxt), (0, 0, 0, nz + width))
 
 
 def shifted(padded):

time: 142 us -> 202 us (1.42)
  local copies, waits for them, and re-layouts: 12.3 us -> 69.1 us
  starting transfers between devices: 40.2 us -> 44.7 us
  other arithmetic: 26.4 us -> 23.2 us
    dynamic_update_slice x0 -> x2, local copies, waits for them, and re-layouts: none -> 44.9 us  [the longest x1 24 us: with_wide_halo(): return lax.dynamic_update_slice(wide, unpack(nxt), (0, 0, 0, nz + width))]
    all_to_all x1, waiting for transfers between devices: 6.11 us -> 14 us  [on_device(): lax.all_to_all(send, ('gx', 'gy'), split_axis=0, concat_axis=0, tiled=True)]
    ppermute x4, starting transfers between devices: 15.4 us -> 22.8 us  [exchange(): from_prev = lax.ppermute(hi, axis, forward)]
    ppermute x4, waiting for transfers between devices: 22.1 us -> 15.1 us  [exchange(): from_next = lax.ppermute(lo, axis, backward)]
    concatenate x1 -> x0, other arithmetic: 4.81 us -> none  [with_wide_halo(): return jnp.concatenate([unpack(prev), fields, unpack(nxt)], axis=3)]
    transpose x2, local copies, waits for them, and re-layouts: 2.45 us -> 5.91 us  [unpack(): return jnp.moveaxis(a.reshape(nf, width, nx, ny), 1, 3)]
    transpose x3, local copies, waits for them, and re-layouts: 3.04 us -> 6.42 us  [pack(): return jnp.moveaxis(a, 3, 1).reshape(nf * width, nx * ny)]
    all_to_all x1, starting transfers between devices: 18.4 us -> 15.4 us  [on_device(): lax.all_to_all(send, ('gx', 'gy'), split_axis=0, concat_axis=0, tiled=True)]
  transfers between devices with their start and end apart: 9 -> 9, of which waited for: 5 -> 5; matrix products, arithmetic and copies ran while one was open for 5% -> 9% of each run, Pallas kernels for 0% -> 0%
where the time goes in v7:
time: 202 us; the launch traced here: 201 us
  local copies, waits for them, and re-layouts  69.1 us (34%)
  starting transfers between devices  44.7 us (22%)
  waiting for transfers between devices  31 us (15%)
  blocking collectives  29.9 us (15%)
  other arithmetic  23.2 us (11%)
  between operations  2.89 us (1%)
    all_to_all x1, blocking collectives, on_device(): lax.all_to_all(jnp.full((device_count,), local_total), ('gx', 'gy', 'gz')...  29.9 us
    dynamic_update_slice x1, local copies, waits for them, and re-layouts, with_wide_halo(): return lax.dynamic_update_slice(wide, unpack(nxt), (0, 0, 0, nz + width))  24 us
    ppermute x4, starting transfers between devices, exchange(): from_prev = lax.ppermute(hi, axis, forward)  22.8 us
    dynamic_update_slice x1, local copies, waits for them, and re-layouts, with_wide_halo(): wide = lax.dynamic_update_slice(wide, unpack(prev), (0, 0, 0, 0))  20.8 us
    all_to_all x1, starting transfers between devices, on_device(): lax.all_to_all(send, ('gx', 'gy'), split_axis=0, concat_axis=0, tiled=True)  15.4 us
    ppermute x4, waiting for transfers between devices, exchange(): from_next = lax.ppermute(lo, axis, backward)  15.1 us
    all_to_all x1, waiting for transfers between devices, on_device(): lax.all_to_all(send, ('gx', 'gy'), split_axis=0, concat_axis=0, tiled=True)  14 us
    select_n x4, other arithmetic, on_device(): updated = jnp.where(inside_mask(k), updated, 0.0)  8.47 us
  transfers between devices with their start and end apart: 9, of which 5 were waited for; matrix products, arithmetic and copies ran while one was open for 9% of the time, Pallas kernels for 0%

profile of v7, /device:TPU:1, one launch (start us, length us, event | category | flops | bytes accessed | tf_op | source)
XLA Modules:
  0.0 201.2 jit_solution(4436519747013223096)
XLA Ops:
  0.6 0.8 select_reduce_fusion.1
  1.4 0.9 multiply_bitcast_fusion
  2.3 1.0 fusion.46
  3.3 11.5 %collective-permute-start = (f32[2,5,32,128]{3,2,1,0:T(8,128)S(1)}, f32[2,5,32,128]{3,2,1,0:T(8,128)S(1)}, u32[]{:S(2)}, u32[]{:S(2)}) collective-permute-start(f32[2,5,32,128]{3,2,1,0:T(8,128)S(1)} %get-tuple-element.21), channel_id=1, source_target_pairs={{0,32},{32,64},{64,96},{96,128},{128,160},{160,192},{192,224},{224... | collective-permute-start | bytes 491528 | tf_op jit(solution)/shard_map/ppermute | solution.py:22
  14.8 1.3 collective-permute-start.1
  16.1 0.7 convert_bitcast_fusion
  16.7 0.9 convert_reduce_fusion
  17.6 0.7 compare_select_fusion
  18.3 0.1 copy.35
  18.4 0.9 select_reduce_fusion
  19.3 0.1 copy.34
  19.4 1.5 scatter_custom_fusion
  21.0 1.4 all_to_all.13
  22.3 15.4 %all-to-all-start = ((f32[128,1,520]{2,1,0:T(1,128)}), f32[128,1,520]{2,1,0:T(1,128)S(1)}, u32[]{:S(2)}, u32[]{:S(2)}) async-start(f32[128,1,520]{2,1,0:T(1,128)} %all_to_all.13), calls=%async_computation | async-start | bytes 655360 | tf_op jit(solution)/shard_map/all_to_all | solution.py:130
  37.9 0.6 compare_and_fusion.9
  38.5 0.1 broadcast_and_fusion
  38.6 0.5 compare_and_fusion.6
  39.1 0.1 broadcast_and_fusion.1
  39.2 0.1 broadcast_and_fusion.2
  39.2 14.0 %all-to-all-done = f32[128,1,520]{2,1,0:T(1,128)S(1)} async-done(((f32[128,1,520]{2,1,0:T(1,128)}), f32[128,1,520]{2,1,0:T(1,128)S(1)}, u32[]{:S(2)}, u32[]{:S(2)}) %all-to-all-start) | async-done | bytes 266272 | tf_op jit(solution)/shard_map/all_to_all | solution.py:130
  53.3 0.8 reduce.1
  54.1 0.3 reshape.266
  54.3 0.1 slice_reduce_fusion
  54.5 0.2 fusion.42
  54.7 0.1 fusion.65
  54.9 0.5 fusion.19
  55.4 4.3 %collective-permute-start.2 = (f32[2,4,32,128]{3,2,1,0:T(8,128)S(1)}, f32[2,4,32,128]{3,2,1,0:T(8,128)S(1)}, u32[]{:S(2)}, u32[]{:S(2)}) collective-permute-start(f32[2,4,32,128]{3,2,1,0:T(8,128)S(1)} %get-tuple-element.24), channel_id=1, source_target_pairs={{0,32},{32,64},{64,96},{96,128},{128,160},{160,192},{192,224},{224... | collective-permute-start | bytes 393224 | tf_op jit(solution)/shard_map/ppermute | solution.py:22
  59.7 0.6 compare_and_fusion.3
  60.2 1.3 collective-permute-start.3
  61.5 0.6 collective-permute-done.2
  62.2 13.9 %collective-permute-done.3 = f32[2,4,32,128]{3,2,1,0:T(8,128)S(1)} collective-permute-done((f32[2,4,32,128]{3,2,1,0:T(8,128)S(1)}, f32[2,4,32,128]{3,2,1,0:T(8,128)S(1)}, u32[]{:S(2)}, u32[]{:S(2)}) %collective-permute-start.3) | collective-permute-done | bytes 131104 | tf_op jit(solution)/shard_map/ppermute | solution.py:23
  76.3 2.7 %collective-permute-start.5 = (f32[360,128]{1,0:T(8,128)S(1)}, f32[360,128]{1,0:T(8,128)S(1)}, u32[]{:S(2)}, u32[]{:S(2)}) collective-permute-start(f32[360,128]{1,0:T(8,128)S(1)} %reshape.270), channel_id=1, source_target_pairs={{4,0},{8,4},{12,8},{16,12},{20,16},{24,20},{28,24},{5,1},{9,5},{13... | collective-permute-start | bytes 552968 | tf_op jit(solution)/shard_map/ppermute | solution.py:23
  79.0 2.9 %collective-permute-start.4 = (f32[360,128]{1,0:T(8,128)S(1)}, f32[360,128]{1,0:T(8,128)S(1)}, u32[]{:S(2)}, u32[]{:S(2)}) collective-permute-start(f32[360,128]{1,0:T(8,128)S(1)} %reshape.268), channel_id=1, source_target_pairs={{0,4},{4,8},{8,12},{12,16},{16,20},{20,24},{24,28},{1,5},{5,9},{9,... | collective-permute-start | bytes 552968 | tf_op jit(solution)/shard_map/ppermute | solution.py:22
  81.9 0.1 broadcast_and_fusion.3
  82.0 1.2 collective-permute-done.5
  83.2 1.1 collective-permute-done.4
  84.4 0.3 pad_maximum_fusion
  84.7 1.8 slice_bitcast_fusion
  86.5 3.0 %copy.39 = f32[4,5,18,42]{3,2,1,0:T(8,128)} copy(f32[4,5,18,42]{1,3,2,0:T(8,128)} %get-tuple-element.15) | data formatting | bytes 120960 | tf_op jit(solution)/shard_map/transpose | solution.py:45
  89.5 1.7 reshape.274
  91.2 1.3 collective-permute-start.7
  92.5 1.6 copy.37
  94.1 1.1 reshape.272
  95.1 4.2 %collective-permute-start.6 = (f32[20,756]{1,0:T(8,128)S(1)}, f32[20,756]{1,0:T(8,128)S(1)}, u32[]{:S(2)}, u32[]{:S(2)}) collective-permute-start(f32[20,756]{1,0:T(8,128)S(1)} %reshape.272), channel_id=1, source_target_pairs={{0,1},{1,2},{2,3},{4,5},{5,6},{6,7},{8,9},{9,10},{10,11},{12,13},{... | collective-permute-start | bytes 181448 | tf_op jit(solution)/shard_map/ppermute | solution.py:22
  99.3 0.5 compare_and_fusion
  99.8 2.7 %pad.4 = f32[4,18,42,138]{3,2,1,0:T(8,128)} pad(f32[4,18,42,128]{3,2,1,0:T(8,128)S(1)} %pad_maximum_fusion, f32[]{:T(128)} %constant.37.clone.1), padding=0_0x0_0x0_0x5_5 | pad | bytes 3217540 | tf_op jit(solution)/shard_map/jit(_pad)/pad | solution.py:52
  102.6 0.8 reshape.273
  103.4 3.0 %copy.38 = f32[4,18,42,5]{3,2,1,0:T(8,128)} copy(f32[4,18,42,5]{2,1,3,0:T(8,128)} %bitcast.30) | data formatting | bytes 120960 | tf_op jit(solution)/shard_map/transpose | solution.py:48
  106.4 1.7 reshape.275
  108.1 2.9 %copy.40 = f32[4,18,42,5]{3,2,1,0:T(8,128)} copy(f32[4,18,42,5]{2,1,3,0:T(8,128)} %bitcast.31) | data formatting | bytes 120960 | tf_op jit(solution)/shard_map/transpose | solution.py:48
  111.0 20.8 %dynamic_update_slice.6 = f32[4,18,42,138]{3,2,1,0:T(8,128)S(1)} dynamic-update-slice(f32[4,18,42,138]{3,2,1,0:T(8,128)S(1)} %copy-done, f32[4,18,42,5]{3,2,1,0:T(8,128)} %copy.38, s32[]{:T(128)} %constant.26.clone.1, s32[]{:T(128)} %constant.26.clone.1, s32[]{:T(128)} %constant.26.clone.1, s32[]{:T(128)} %constant.26.clone.1) | dynamic-update-slice | bytes 120964 | tf_op jit(solution)/shard_map/dynamic_update_slice | solution.py:53
  131.9 24.0 %dynamic_update_slice.7 = f32[4,18,42,138]{3,2,1,0:T(8,128)S(1)} dynamic-update-slice(f32[4,18,42,138]{3,2,1,0:T(8,128)S(1)} %dynamic_update_slice.6, f32[4,18,42,5]{3,2,1,0:T(8,128)} %copy.40, s32[]{:T(128)} %constant.26.clone.1, s32[]{:T(128)} %constant.26.clone.1, s32[]{:T(128)} %constant.26.clone.1, s32[]{:T(128)} %constant.39.clone.1) | dynamic-update-slice | bytes 120964 | tf_op jit(solution)/shard_map/dynamic_update_slice | solution.py:54
  155.9 0.4 slice_bitcast_fusion.3
  156.3 0.3 copy-done.3
  156.6 2.7 %fusion.5 = (f32[16,40,136]{2,1,0:T(8,128)S(1)}, f32[16,40,136]{2,1,0:T(8,128)S(1)}, f32[16,40,136]{2,1,0:T(8,128)S(1)}, f32[16,40,136]{2,1,0:T(8,128)S(1)}, f32...) fusion(f32[18,42,138]{2,1,0:T(8,128)S(1)} %get-tuple-element.14, ...), kind=kLoop, calls=%fused_computation.15 | loop fusion | flops 3742720 | bytes 8008456 | tf_op jit(solution)/shard_map/jit(_where)/select_n | solution.py:195
  159.3 0.3 slice_add_fusion
  159.6 0.3 copy-done.6
  159.9 2.2 %fusion.11 = f32[14,38,134]{2,1,0:T(8,128)S(1)} fusion(f32[16,40,136]{2,1,0:T(8,128)S(1)} %slice_add_fusion, f32[16,40,136]{2,1,0:T(8,128)S(1)} %get-tuple-element.4, f32[16,40,136]{2,1,0:T(8,128)S(1)} %get-tuple-element.10, f32[16,40,136]{2,1,0:T(8,128)S(1)} %get-tuple-element.9, f32[16,40,136]{2,1,0:T(8,128)S(1)} %get-tuple-element.8, ...), kind=kLoop, calls=%fused_computation.34 | loop fusion | flops 1283184 | bytes 4563098 | tf_op jit(solution)/shard_map/jit(_where)/select_n | solution.py:195
  162.2 1.9 fusion.24
  164.1 1.6 fusion.33
  165.7 1.8 fusion.51
  167.6 0.8 broadcast_in_dim.96
  168.3 29.9 %all_to_all.16 = f32[512,1,1]{2,1,0:T(1,128)S(1)} all-to-all(f32[512,1,1]{2,1,0:T(1,128)S(1)} %broadcast_in_dim.96), channel_id=1, replica_groups=mesh['gx'=16,'gy'=8,'gz'=4] {'gx','gy','gz'}, dimensions={0} | all-to-all | bytes 4096 | tf_op jit(solution)/shard_map/all_to_all | solution.py:205
  198.2 1.1 reduce_sum.49
  (37 shorter events, 0.4 us)
Async XLA Ops:
  3.3 72.9 %collective-permute-start = (f32[2,5,32,128]{3,2,1,0:T(8,128)S(1)}, f32[2,5,32,128]{3,2,1,0:T(8,128)S(1)}, u32[]{:S(2)}, u32[]{:S(2)}) collective-permute-start(f32[2,5,32,128]{3,2,1,0:T(8,128)S(1)} %get-tuple-element.21), channel_id=1, source_target_pairs={{0,32},{32,64},{64,96},{96,128},{128,160},{160,192},{192,224},{224... | collective-permute-start | bytes 491528 | tf_op jit(solution)/shard_map/ppermute | solution.py:22
  14.8 61.4 %collective-permute-start.1 = (f32[2,5,32,128]{3,2,1,0:T(8,128)S(1)}, f32[2,5,32,128]{3,2,1,0:T(8,128)S(1)}, u32[]{:S(2)}, u32[]{:S(2)}) collective-permute-start(f32[2,5,32,128]{3,2,1,0:T(8,128)S(1)} %get-tuple-element.22), channel_id=1, source_target_pairs={{32,0},{64,32},{96,64},{128,96},{160,128},{192,160},{224,192},{256... | collective-permute-start | bytes 491528 | tf_op jit(solution)/shard_map/ppermute | solution.py:23
  22.3 30.9 %all-to-all-start = ((f32[128,1,520]{2,1,0:T(1,128)}), f32[128,1,520]{2,1,0:T(1,128)S(1)}, u32[]{:S(2)}, u32[]{:S(2)}) async-start(f32[128,1,520]{2,1,0:T(1,128)} %all_to_all.13), calls=%async_computation | async-start | bytes 655360 | tf_op jit(solution)/shard_map/all_to_all | solution.py:130
  54.1 1.3 copy-start.2
  54.9 21.3 %copy-start.1 = (f32[8,32,128]{2,1,0:T(8,128)S(1)}, f32[8,32,128]{2,1,0:T(8,128)}, u32[]{:S(2)}) copy-start(f32[8,32,128]{2,1,0:T(8,128)} %param.19) | copy-start | bytes 393220
  55.4 6.7 %collective-permute-start.2 = (f32[2,4,32,128]{3,2,1,0:T(8,128)S(1)}, f32[2,4,32,128]{3,2,1,0:T(8,128)S(1)}, u32[]{:S(2)}, u32[]{:S(2)}) collective-permute-start(f32[2,4,32,128]{3,2,1,0:T(8,128)S(1)} %get-tuple-element.24), channel_id=1, source_target_pairs={{0,32},{32,64},{64,96},{96,128},{128,160},{160,192},{192,224},{224... | collective-permute-start | bytes 393224 | tf_op jit(solution)/shard_map/ppermute | solution.py:22
  60.2 15.9 %collective-permute-start.3 = (f32[2,4,32,128]{3,2,1,0:T(8,128)S(1)}, f32[2,4,32,128]{3,2,1,0:T(8,128)S(1)}, u32[]{:S(2)}, u32[]{:S(2)}) collective-permute-start(f32[2,4,32,128]{3,2,1,0:T(8,128)S(1)} %get-tuple-element.23), channel_id=1, source_target_pairs={{32,0},{64,32},{96,64},{128,96},{160,128},{192,160},{224,192},{256... | collective-permute-start | bytes 393224 | tf_op jit(solution)/shard_map/ppermute | solution.py:23
  76.3 6.9 %collective-permute-start.5 = (f32[360,128]{1,0:T(8,128)S(1)}, f32[360,128]{1,0:T(8,128)S(1)}, u32[]{:S(2)}, u32[]{:S(2)}) collective-permute-start(f32[360,128]{1,0:T(8,128)S(1)} %reshape.270), channel_id=1, source_target_pairs={{4,0},{8,4},{12,8},{16,12},{20,16},{24,20},{28,24},{5,1},{9,5},{13... | collective-permute-start | bytes 552968 | tf_op jit(solution)/shard_map/ppermute | solution.py:23
  79.0 5.4 %collective-permute-start.4 = (f32[360,128]{1,0:T(8,128)S(1)}, f32[360,128]{1,0:T(8,128)S(1)}, u32[]{:S(2)}, u32[]{:S(2)}) collective-permute-start(f32[360,128]{1,0:T(8,128)S(1)} %reshape.268), channel_id=1, source_target_pairs={{0,4},{4,8},{8,12},{12,16},{16,20},{20,24},{24,28},{1,5},{5,9},{9,... | collective-permute-start | bytes 552968 | tf_op jit(solution)/shard_map/ppermute | solution.py:22
  91.2 15.2 %collective-permute-start.7 = (f32[20,756]{1,0:T(8,128)}, f32[20,756]{1,0:T(8,128)}, u32[]{:S(2)}, u32[]{:S(2)}) collective-permute-start(f32[20,756]{1,0:T(8,128)} %reshape.274), channel_id=1, source_target_pairs={{1,0},{2,1},{3,2},{5,4},{6,5},{7,6},{9,8},{10,9},{11,10},{13,12},{... | collective-permute-start | bytes 181448 | tf_op jit(solution)/shard_map/ppermute | solution.py:23
  95.1 7.4 %collective-permute-start.6 = (f32[20,756]{1,0:T(8,128)S(1)}, f32[20,756]{1,0:T(8,128)S(1)}, u32[]{:S(2)}, u32[]{:S(2)}) collective-permute-start(f32[20,756]{1,0:T(8,128)S(1)} %reshape.272), channel_id=1, source_target_pairs={{0,1},{1,2},{2,3},{4,5},{5,6},{6,7},{8,9},{9,10},{10,11},{12,13},{... | collective-permute-start | bytes 181448 | tf_op jit(solution)/shard_map/ppermute | solution.py:22
  103.4 7.6 %copy-start = (f32[4,18,42,138]{3,2,1,0:T(8,128)S(1)}, f32[4,18,42,138]{3,2,1,0:T(8,128)}, u32[]{:S(2)}) copy-start(f32[4,18,42,138]{3,2,1,0:T(8,128)} %pad.4) | copy-start | bytes 5007748
  155.9 0.7 copy-start.3
  159.3 0.6 copy-start.6
  159.9 2.2 %copy-start.5 = (pred[132]{0:T(512)(128)(4,1)S(1)}, pred[132]{0:T(512)(128)(4,1)}, u32[]{:S(2)}) copy-start(pred[132]{0:T(512)(128)(4,1)} %compare_and_fusion.6) | copy-start | bytes 400
  162.2 1.9 copy-start.4

commit v8 on v2

--- a/solution.py
+++ b/solution.py
@@ -122,7 +122,11 @@
         axis=1,
     )
     width_row = cells_z + 2
-    send = jnp.zeros((slot_total, width_row), jnp.float32).at[position].set(rows)
+    slots = jnp.arange(slot_total, dtype=jnp.int32)
+    placement = (slots[:, None] == position[None, :]).astype(jnp.float32)
+    send = jnp.dot(
+        placement, rows, precision=lax.Precision.HIGHEST, preferred_element_type=jnp.float32
+    )
     send = send.reshape(peer_count, capacity * width_row)
     recv = lax.all_to_all(send, ("gx", "gy"), split_axis=0, concat_axis=0, tiled=True)
     recv = recv.reshape(slot_total, width_row)

time: 142 us -> 142 us (level)
  other arithmetic: 26.4 us -> 24.8 us
    scatter x1 -> x0, other arithmetic: 1.53 us -> none  [on_device(): jnp.zeros((slot_total, width_row), jnp.float32).at[position].set(rows)]
where the time goes in v8:
time: 142 us; the launch traced here: 141 us
  starting transfers between devices  40.2 us (28%)
  blocking collectives  29.8 us (21%)
  waiting for transfers between devices  29.4 us (21%)
  other arithmetic  24.8 us (17%)
  local copies, waits for them, and re-layouts  12.2 us (9%)
  between operations  2.98 us (2%)
  matrix products  1.74 us (1%)
    all_to_all x1, blocking collectives, on_device(): lax.all_to_all(jnp.full((device_count,), local_total), ('gx', 'gy', 'gz')...  29.8 us
    ppermute x4, waiting for transfers between devices, exchange(): from_next = lax.ppermute(lo, axis, backward)  22 us
    all_to_all x1, starting transfers between devices, on_device(): lax.all_to_all(send, ('gx', 'gy'), split_axis=0, concat_axis=0, tiled=True)  18.4 us
    ppermute x4, starting transfers between devices, exchange(): from_prev = lax.ppermute(hi, axis, forward)  15.4 us
    select_n x4, other arithmetic, on_device(): updated = jnp.where(inside_mask(k), updated, 0.0)  8.47 us
    ppermute x4, starting transfers between devices, exchange(): from_next = lax.ppermute(lo, axis, backward)  6.47 us
    all_to_all x1, waiting for transfers between devices, on_device(): lax.all_to_all(send, ('gx', 'gy'), split_axis=0, concat_axis=0, tiled=True)  6.26 us
    concatenate x1, other arithmetic, with_wide_halo(): return jnp.concatenate([unpack(prev), fields, unpack(nxt)], axis=3)  4.81 us
  transfers between devices with their start and end apart: 9, of which 5 were waited for; matrix products, arithmetic and copies ran while one was open for 5% of the time, Pallas kernels for 0%

profile of v8, /device:TPU:1, one launch (start us, length us, event | category | flops | bytes accessed | tf_op | source)
XLA Modules:
  0.0 141.2 jit_solution(15541944419839731901)
XLA Ops:
  0.7 0.0 copy-start.3
  0.7 0.9 select_reduce_fusion
  1.6 0.1 copy.37
  1.7 0.7 convert_bitcast_fusion
  2.4 0.1 copy.38
  2.5 0.9 convert_reduce_fusion
  3.4 0.7 multiply_add_fusion
  4.1 1.3 fusion.44
  5.4 1.4 all_to_all.13
  6.7 18.4 %all-to-all-start = ((f32[128,1,520]{2,1,0:T(1,128)}), f32[128,1,520]{2,1,0:T(1,128)S(1)}, u32[]{:S(2)}, u32[]{:S(2)}) async-start(f32[128,1,520]{2,1,0:T(1,128)} %all_to_all.13), calls=%async_computation | async-start | bytes 655360 | tf_op jit(solution)/shard_map/all_to_all | solution.py:131
  25.2 0.1 select_reduce_fusion.1
  25.3 0.0 copy-start.1
  25.3 7.2 %collective-permute-start = (f32[2,5,32,128]{3,2,1,0:T(8,128)S(1)}, f32[2,5,32,128]{3,2,1,0:T(8,128)S(1)}, u32[]{:S(2)}, u32[]{:S(2)}) collective-permute-start(f32[2,5,32,128]{3,2,1,0:T(8,128)S(1)} %get-tuple-element.21), channel_id=1, source_target_pairs={{0,32},{32,64},{64,96},{96,128},{128,160},{160,192},{192,224},{224... | collective-permute-start | bytes 491528 | tf_op jit(solution)/shard_map/ppermute | solution.py:22
  32.5 1.3 collective-permute-start.1
  33.9 0.5 compare_and_fusion
  34.4 0.5 compare_and_fusion.3
  34.9 0.5 compare_and_fusion.6
  35.4 0.1 broadcast_and_fusion
  35.5 0.1 broadcast_and_fusion.1
  35.6 0.1 broadcast_and_fusion.2
  35.7 6.3 %all-to-all-done = f32[128,1,520]{2,1,0:T(1,128)S(1)} async-done(((f32[128,1,520]{2,1,0:T(1,128)}), f32[128,1,520]{2,1,0:T(1,128)S(1)}, u32[]{:S(2)}, u32[]{:S(2)}) %all-to-all-start) | async-done | bytes 266272 | tf_op jit(solution)/shard_map/all_to_all | solution.py:131
  41.9 0.8 reduce.1
  42.7 0.3 reshape.267
  43.0 0.1 slice_reduce_fusion
  43.1 0.2 fusion.42
  43.4 0.1 fusion.66
  43.5 0.5 fusion.19
  44.1 3.1 %collective-permute-start.2 = (f32[2,4,32,128]{3,2,1,0:T(8,128)S(1)}, f32[2,4,32,128]{3,2,1,0:T(8,128)S(1)}, u32[]{:S(2)}, u32[]{:S(2)}) collective-permute-start(f32[2,4,32,128]{3,2,1,0:T(8,128)S(1)} %get-tuple-element.24), channel_id=1, source_target_pairs={{0,32},{32,64},{64,96},{96,128},{128,160},{160,192},{192,224},{224... | collective-permute-start | bytes 393224 | tf_op jit(solution)/shard_map/ppermute | solution.py:22
  47.2 1.3 collective-permute-start.3
  48.5 1.2 collective-permute-done.2
  49.8 15.5 %collective-permute-done.3 = f32[2,4,32,128]{3,2,1,0:T(8,128)S(1)} collective-permute-done((f32[2,4,32,128]{3,2,1,0:T(8,128)S(1)}, f32[2,4,32,128]{3,2,1,0:T(8,128)S(1)}, u32[]{:S(2)}, u32[]{:S(2)}) %collective-permute-start.3) | collective-permute-done | bytes 131104 | tf_op jit(solution)/shard_map/ppermute | solution.py:23
  65.5 1.9 %collective-permute-start.4 = (f32[360,128]{1,0:T(8,128)S(1)}, f32[360,128]{1,0:T(8,128)S(1)}, u32[]{:S(2)}, u32[]{:S(2)}) collective-permute-start(f32[360,128]{1,0:T(8,128)S(1)} %reshape.269), channel_id=1, source_target_pairs={{0,4},{4,8},{8,12},{12,16},{16,20},{20,24},{24,28},{1,5},{5,9},{9,... | collective-permute-start | bytes 552968 | tf_op jit(solution)/shard_map/ppermute | solution.py:22
  67.4 2.4 %collective-permute-start.5 = (f32[360,128]{1,0:T(8,128)S(1)}, f32[360,128]{1,0:T(8,128)S(1)}, u32[]{:S(2)}, u32[]{:S(2)}) collective-permute-start(f32[360,128]{1,0:T(8,128)S(1)} %reshape.271), channel_id=1, source_target_pairs={{4,0},{8,4},{12,8},{16,12},{20,16},{24,20},{28,24},{5,1},{9,5},{13... | collective-permute-start | bytes 552968 | tf_op jit(solution)/shard_map/ppermute | solution.py:23
  69.8 0.1 broadcast_and_fusion.3
  70.0 4.3 %collective-permute-done.5 = f32[360,128]{1,0:T(8,128)S(1)} collective-permute-done((f32[360,128]{1,0:T(8,128)S(1)}, f32[360,128]{1,0:T(8,128)S(1)}, u32[]{:S(2)}, u32[]{:S(2)}) %collective-permute-start.5) | collective-permute-done | bytes 184352 | tf_op jit(solution)/shard_map/ppermute | solution.py:23
  74.3 0.8 reshape.272
  75.1 1.2 pad_maximum_fusion.1
  76.3 0.6 slice_bitcast_fusion.1
  76.9 1.6 %copy.41 = f32[4,5,18,42]{3,2,1,0:T(8,128)} copy(f32[4,5,18,42]{1,3,2,0:T(8,128)S(1)} %get-tuple-element.15) | data formatting | bytes 120960 | tf_op jit(solution)/shard_map/transpose | solution.py:45
  78.5 1.1 reshape.273
  79.5 3.1 %collective-permute-start.6 = (f32[20,756]{1,0:T(8,128)S(1)}, f32[20,756]{1,0:T(8,128)S(1)}, u32[]{:S(2)}, u32[]{:S(2)}) collective-permute-start(f32[20,756]{1,0:T(8,128)S(1)} %reshape.273), channel_id=1, source_target_pairs={{0,1},{1,2},{2,3},{4,5},{5,6},{6,7},{8,9},{9,10},{10,11},{12,13},{... | collective-permute-start | bytes 181448 | tf_op jit(solution)/shard_map/ppermute | solution.py:22
  82.7 0.9 copy.42
  83.5 0.1 reshape.275
  83.7 1.5 %collective-permute-start.7 = (f32[20,756]{1,0:T(8,128)S(1)}, f32[20,756]{1,0:T(8,128)S(1)}, u32[]{:S(2)}, u32[]{:S(2)}) collective-permute-start(f32[20,756]{1,0:T(8,128)S(1)} %reshape.275), channel_id=1, source_target_pairs={{1,0},{2,1},{3,2},{5,4},{6,5},{7,6},{9,8},{10,9},{11,10},{13,12},{... | collective-permute-start | bytes 181448 | tf_op jit(solution)/shard_map/ppermute | solution.py:23
  85.1 0.6 compare_and_fusion.9
  85.7 0.1 reshape.274
  85.9 0.8 copy.43
  86.6 2.1 %collective-permute-done.7 = f32[20,756]{1,0:T(8,128)S(1)} collective-permute-done((f32[20,756]{1,0:T(8,128)S(1)}, f32[20,756]{1,0:T(8,128)S(1)}, u32[]{:S(2)}, u32[]{:S(2)}) %collective-permute-start.7) | collective-permute-done | bytes 60512 | tf_op jit(solution)/shard_map/ppermute | solution.py:23
  88.8 0.8 reshape.276
  89.6 1.7 %copy.44 = f32[4,18,42,5]{3,2,1,0:T(8,128)S(1)} copy(f32[4,18,42,5]{2,1,3,0:T(8,128)} %bitcast.31) | data formatting | bytes 120960 | tf_op jit(solution)/shard_map/transpose | solution.py:48
  91.3 4.8 %pad_maximum_fusion = f32[4,18,42,138]{3,2,1,0:T(8,128)S(1)} fusion(f32[4,18,42,5]{3,2,1,0:T(8,128)S(1)} %copy.44, f32[4,18,5,128]{3,2,1,0:T(8,128)} %reshape.272, f32[2,18,32,128]{3,2,1,0:T(8,128)} %copy-done, f32[2,5,32,128]{3,2,1,0:T(8,128)} %copy-done.5, f32[1,8,32,128]{3,2,1,0:T(8,128)} %bitcast.24, f32[1,8,32,128]{3,2,1,0:T(8,128)} %copy-done.1, ...), kind=kLoop, calls=%fused_computation | loop fusion | flops 3338496 | bytes 3338496 | tf_op jit(solution)/shard_map/concatenate | solution.py:51
  96.1 0.0 copy-start.8
  96.1 0.3 slice_bitcast_fusion.3
  96.5 0.3 copy-done.8
  96.8 2.7 %fusion.5 = (f32[16,40,136]{2,1,0:T(8,128)S(1)}, f32[16,40,136]{2,1,0:T(8,128)S(1)}, f32[16,40,136]{2,1,0:T(8,128)S(1)}, f32[16,40,136]{2,1,0:T(8,128)S(1)}, f32...) fusion(f32[18,42,138]{2,1,0:T(8,128)S(1)} %get-tuple-element.14, ...), kind=kLoop, calls=%fused_computation.15 | loop fusion | flops 3742720 | bytes 8008456 | tf_op jit(solution)/shard_map/jit(_where)/select_n | solution.py:196
  99.5 0.3 slice_add_fusion
  99.8 0.2 copy-done.11
  100.1 2.2 %fusion.11 = f32[14,38,134]{2,1,0:T(8,128)S(1)} fusion(f32[16,40,136]{2,1,0:T(8,128)S(1)} %slice_add_fusion, f32[16,40,136]{2,1,0:T(8,128)S(1)} %get-tuple-element.4, f32[16,40,136]{2,1,0:T(8,128)S(1)} %get-tuple-element.10, f32[16,40,136]{2,1,0:T(8,128)S(1)} %get-tuple-element.9, f32[16,40,136]{2,1,0:T(8,128)S(1)} %get-tuple-element.8, ...), kind=kLoop, calls=%fused_computation.34 | loop fusion | flops 1283184 | bytes 4563098 | tf_op jit(solution)/shard_map/jit(_where)/select_n | solution.py:196
  102.3 1.9 %fusion.24 = f32[12,36,132]{2,1,0:T(8,128)S(1)} fusion(f32[16,40,136]{2,1,0:T(8,128)S(1)} %slice_add_fusion, f32[14,38,134]{2,1,0:T(8,128)S(1)} %fusion.11, f32[16,40,136]{2,1,0:T(8,128)S(1)} %get-tuple-element.10, f32[16,40,136]{2,1,0:T(8,128)S(1)} %get-tuple-element.9, f32[16,40,136]{2,1,0:T(8,128)S(1)} %get-tuple-element.8, ...), kind=kLoop, calls=%fused_computation.58 | loop fusion | flops 1026432 | bytes 3650100 | tf_op jit(solution)/shard_map/jit(_where)/select_n | solution.py:196
  104.3 1.6 %fusion.33 = f32[10,34,130]{2,1,0:T(8,128)S(1)} fusion(f32[16,40,136]{2,1,0:T(8,128)S(1)} %slice_add_fusion, f32[12,36,132]{2,1,0:T(8,128)S(1)} %fusion.24, f32[16,40,136]{2,1,0:T(8,128)S(1)} %get-tuple-element.10, f32[16,40,136]{2,1,0:T(8,128)S(1)} %get-tuple-element.9, f32[16,40,136]{2,1,0:T(8,128)S(1)} %get-tuple-element.8, ...), kind=kLoop, calls=%fused_computation.75 | loop fusion | flops 795600 | bytes 2829270 | tf_op jit(solution)/shard_map/jit(_where)/select_n | solution.py:196
  105.9 1.8 %fusion.50 = (f32[]{:T(128)}, f32[8,32,128]{2,1,0:T(8,128)}) fusion(f32[16,40,136]{2,1,0:T(8,128)S(1)} %slice_add_fusion, f32[10,34,130]{2,1,0:T(8,128)S(1)} %fusion.33, f32[16,40,136]{2,1,0:T(8,128)S(1)} %get-tuple-element.10, f32[16,40,136]{2,1,0:T(8,128)S(1)} %get-tuple-element.9, f32[16,40,136]{2,1,0:T(8,128)S(1)} %get-tuple-element.8, ...), kind=kLoop, calls=%fused_computation.116 | loop fusion | flops 524287 | bytes 2097156 | tf_op jit(solution)/shard_map/reduce_sum | solution.py:204
  107.7 0.8 broadcast_in_dim.90
  108.5 29.8 %all_to_all.16 = f32[512,1,1]{2,1,0:T(1,128)S(1)} all-to-all(f32[512,1,1]{2,1,0:T(1,128)S(1)} %broadcast_in_dim.90), channel_id=1, replica_groups=mesh['gx'=16,'gy'=8,'gz'=4] {'gx','gy','gz'}, dimensions={0} | all-to-all | bytes 4096 | tf_op jit(solution)/shard_map/all_to_all | solution.py:206
  138.3 1.1 reduce_sum.49
  (49 shorter events, 0.4 us)
Async XLA Ops:
  0.6 24.5 %copy-start.12 = (f32[6]{0:T(128)S(1)}, f32[6]{0:T(128)}, u32[]{:S(2)}) copy-start(f32[6]{0:T(128)} %param.12) | copy-start | bytes 76
  0.6 24.5 %copy-start.13 = (s32[128]{0:T(128)S(1)}, s32[128]{0:T(128)}, u32[]{:S(2)}) copy-start(s32[128]{0:T(128)} %param.13) | copy-start | bytes 1540
  0.7 24.6 %copy-start.7 = (f32[8,32,128]{2,1,0:T(8,128)S(1)}, f32[8,32,128]{2,1,0:T(8,128)}, u32[]{:S(2)}) copy-start(f32[8,32,128]{2,1,0:T(8,128)} %param.11) | copy-start | bytes 393220
  0.7 24.6 %copy-start.3 = (f32[8,32,128]{2,1,0:T(8,128)S(1)}, f32[8,32,128]{2,1,0:T(8,128)}, u32[]{:S(2)}) copy-start(f32[8,32,128]{2,1,0:T(8,128)} %param.19) | copy-start | bytes 393220
  6.7 35.2 %all-to-all-start = ((f32[128,1,520]{2,1,0:T(1,128)}), f32[128,1,520]{2,1,0:T(1,128)S(1)}, u32[]{:S(2)}, u32[]{:S(2)}) async-start(f32[128,1,520]{2,1,0:T(1,128)} %all_to_all.13), calls=%async_computation | async-start | bytes 655360 | tf_op jit(solution)/shard_map/all_to_all | solution.py:131
  25.3 49.8 %copy-start.1 = (f32[1,8,32,128]{3,2,1,0:T(8,128)}, f32[1,8,32,128]{3,2,1,0:T(8,128)S(1)}, u32[]{:S(2)}) copy-start(f32[1,8,32,128]{3,2,1,0:T(8,128)S(1)} %multiply_bitcast_fusion) | copy-start | bytes 393220
  25.3 40.0 %collective-permute-start = (f32[2,5,32,128]{3,2,1,0:T(8,128)S(1)}, f32[2,5,32,128]{3,2,1,0:T(8,128)S(1)}, u32[]{:S(2)}, u32[]{:S(2)}) collective-permute-start(f32[2,5,32,128]{3,2,1,0:T(8,128)S(1)} %get-tuple-element.21), channel_id=1, source_target_pairs={{0,32},{32,64},{64,96},{96,128},{128,160},{160,192},{192,224},{224... | collective-permute-start | bytes 491528 | tf_op jit(solution)/shard_map/ppermute | solution.py:22
  32.5 32.8 %collective-permute-start.1 = (f32[2,5,32,128]{3,2,1,0:T(8,128)S(1)}, f32[2,5,32,128]{3,2,1,0:T(8,128)S(1)}, u32[]{:S(2)}, u32[]{:S(2)}) collective-permute-start(f32[2,5,32,128]{3,2,1,0:T(8,128)S(1)} %get-tuple-element.22), channel_id=1, source_target_pairs={{32,0},{64,32},{96,64},{128,96},{160,128},{192,160},{224,192},{256... | collective-permute-start | bytes 491528 | tf_op jit(solution)/shard_map/ppermute | solution.py:23
  42.7 1.3 copy-start.6
  44.1 5.7 %collective-permute-start.2 = (f32[2,4,32,128]{3,2,1,0:T(8,128)S(1)}, f32[2,4,32,128]{3,2,1,0:T(8,128)S(1)}, u32[]{:S(2)}, u32[]{:S(2)}) collective-permute-start(f32[2,4,32,128]{3,2,1,0:T(8,128)S(1)} %get-tuple-element.24), channel_id=1, source_target_pairs={{0,32},{32,64},{64,96},{96,128},{128,160},{160,192},{192,224},{224... | collective-permute-start | bytes 393224 | tf_op jit(solution)/shard_map/ppermute | solution.py:22
  47.2 18.1 %collective-permute-start.3 = (f32[2,4,32,128]{3,2,1,0:T(8,128)S(1)}, f32[2,4,32,128]{3,2,1,0:T(8,128)S(1)}, u32[]{:S(2)}, u32[]{:S(2)}) collective-permute-start(f32[2,4,32,128]{3,2,1,0:T(8,128)S(1)} %get-tuple-element.23), channel_id=1, source_target_pairs={{32,0},{64,32},{96,64},{128,96},{160,128},{192,160},{224,192},{256... | collective-permute-start | bytes 393224 | tf_op jit(solution)/shard_map/ppermute | solution.py:23
  65.3 9.7 %copy-start = (f32[2,18,32,128]{3,2,1,0:T(8,128)}, f32[2,18,32,128]{3,2,1,0:T(8,128)S(1)}, u32[]{:S(2)}) copy-start(f32[2,18,32,128]{3,2,1,0:T(8,128)S(1)} %broadcast_dynamic-update-slice_fusion.1) | copy-start | bytes 1769476
  65.3 9.7 %copy-start.4 = (f32[2,5,32,128]{3,2,1,0:T(8,128)}, f32[2,5,32,128]{3,2,1,0:T(8,128)S(1)}, u32[]{:S(2)}) copy-start(f32[2,5,32,128]{3,2,1,0:T(8,128)S(1)} %collective-permute-done) | copy-start | bytes 491524
  65.4 9.7 %copy-start.5 = (f32[2,5,32,128]{3,2,1,0:T(8,128)}, f32[2,5,32,128]{3,2,1,0:T(8,128)S(1)}, u32[]{:S(2)}) copy-start(f32[2,5,32,128]{3,2,1,0:T(8,128)S(1)} %collective-permute-done.1) | copy-start | bytes 491524
  65.5 4.5 %collective-permute-start.4 = (f32[360,128]{1,0:T(8,128)S(1)}, f32[360,128]{1,0:T(8,128)S(1)}, u32[]{:S(2)}, u32[]{:S(2)}) collective-permute-start(f32[360,128]{1,0:T(8,128)S(1)} %reshape.269), channel_id=1, source_target_pairs={{0,4},{4,8},{8,12},{12,16},{16,20},{20,24},{24,28},{1,5},{5,9},{9,... | collective-permute-start | bytes 552968 | tf_op jit(solution)/shard_map/ppermute | solution.py:22
  67.4 6.9 %collective-permute-start.5 = (f32[360,128]{1,0:T(8,128)S(1)}, f32[360,128]{1,0:T(8,128)S(1)}, u32[]{:S(2)}, u32[]{:S(2)}) collective-permute-start(f32[360,128]{1,0:T(8,128)S(1)} %reshape.271), channel_id=1, source_target_pairs={{4,0},{8,4},{12,8},{16,12},{20,16},{24,20},{28,24},{5,1},{9,5},{13... | collective-permute-start | bytes 552968 | tf_op jit(solution)/shard_map/ppermute | solution.py:23
  70.0 5.1 %copy-start.2 = (f32[4,18,5,128]{3,2,1,0:T(8,128)}, f32[4,18,5,128]{3,2,1,0:T(8,128)S(1)}, u32[]{:S(2)}) copy-start(f32[4,18,5,128]{3,2,1,0:T(8,128)S(1)} %reshape.270) | copy-start | bytes 552964
  79.5 6.2 %collective-permute-start.6 = (f32[20,756]{1,0:T(8,128)S(1)}, f32[20,756]{1,0:T(8,128)S(1)}, u32[]{:S(2)}, u32[]{:S(2)}) collective-permute-start(f32[20,756]{1,0:T(8,128)S(1)} %reshape.273), channel_id=1, source_target_pairs={{0,1},{1,2},{2,3},{4,5},{5,6},{6,7},{8,9},{9,10},{10,11},{12,13},{... | collective-permute-start | bytes 181448 | tf_op jit(solution)/shard_map/ppermute | solution.py:22
  83.7 5.1 %collective-permute-start.7 = (f32[20,756]{1,0:T(8,128)S(1)}, f32[20,756]{1,0:T(8,128)S(1)}, u32[]{:S(2)}, u32[]{:S(2)}) collective-permute-start(f32[20,756]{1,0:T(8,128)S(1)} %reshape.275), channel_id=1, source_target_pairs={{1,0},{2,1},{3,2},{5,4},{6,5},{7,6},{9,8},{10,9},{11,10},{13,12},{... | collective-permute-start | bytes 181448 | tf_op jit(solution)/shard_map/ppermute | solution.py:23
  96.1 0.7 copy-start.8
  99.5 0.6 copy-start.11
  100.1 2.2 %copy-start.9 = (pred[132]{0:T(512)(128)(4,1)S(1)}, pred[132]{0:T(512)(128)(4,1)}, u32[]{:S(2)}) copy-start(pred[132]{0:T(512)(128)(4,1)} %compare_and_fusion.6) | copy-start | bytes 400
  102.3 1.9 %copy-start.10 = (pred[130]{0:T(512)(128)(4,1)S(1)}, pred[130]{0:T(512)(128)(4,1)}, u32[]{:S(2)}) copy-start(pred[130]{0:T(512)(128)(4,1)} %compare_and_fusion.9) | copy-start | bytes 394

commit v9 on v2

--- a/solution.py
+++ b/solution.py
@@ -111,24 +111,31 @@
     order = jnp.arange(block_count, dtype=jnp.int32)
     earlier = order[None, :] < order[:, None]
     slot_rank = jnp.sum((same_dest & earlier).astype(jnp.int32), axis=1)
-    position = block_dest * capacity + slot_rank
     block_volts = table_lookup(gate_volts, block_gate)
-    rows = jnp.concatenate(
-        [
-            block_cond,
-            block_volts[:, None],
-            block_column.astype(jnp.float32)[:, None],
-        ],
-        axis=1,
-    )
-    width_row = cells_z + 2
-    send = jnp.zeros((slot_total, width_row), jnp.float32).at[position].set(rows)
-    send = send.reshape(peer_count, capacity * width_row)
+    meta = jnp.stack([block_volts, block_column.astype(jnp.float32)], axis=1)
+    peers = jnp.arange(peer_count, dtype=jnp.int32)
+    to_peer = peers[:, None] == block_dest[None, :]
+    cond_parts, meta_parts = [], []
+    for slot in range(capacity):
+        pick = (to_peer & (slot_rank[None, :] == slot)).astype(jnp.float32)
+        cond_parts.append(
+            jnp.dot(pick, block_cond, precision=lax.Precision.HIGHEST, preferred_element_type=jnp.float32)
+        )
+        meta_parts.append(
+            jnp.dot(pick, meta, precision=lax.Precision.HIGHEST, preferred_element_type=jnp.float32)
+        )
+    send = jnp.concatenate(cond_parts + meta_parts, axis=1)
     recv = lax.all_to_all(send, ("gx", "gy"), split_axis=0, concat_axis=0, tiled=True)
-    recv = recv.reshape(slot_total, width_row)
-    cond_recv = recv[:, :cells_z]
-    volt_recv = recv[:, cells_z]
-    column_recv = recv[:, cells_z + 1].astype(jnp.int32)
+    cond_recv = jnp.concatenate(
+        [recv[:, slot * cells_z:(slot + 1) * cells_z] for slot in range(capacity)], axis=0
+    )
+    meta_base = capacity * cells_z
+    volt_recv = jnp.concatenate(
+        [recv[:, meta_base + 2 * slot] for slot in range(capacity)], axis=0
+    )
+    column_recv = jnp.concatenate(
+        [recv[:, meta_base + 2 * slot + 1] for slot in range(capacity)], axis=0
+    ).astype(jnp.int32)
     extra_recv = cond_recv * volt_recv[:, None]
     columns = jnp.arange(cells_x * cells_y, dtype=jnp.int32)
     one_hot = (columns[:, None] == column_recv[None, :]).astype(jnp.float32)

time: 142 us -> 155 us (1.092)
  local copies, waits for them, and re-layouts: 12.3 us -> 19.6 us
  matrix products: 0.46 us -> 7.45 us
  other arithmetic: 26.4 us -> 20 us
  blocking collectives: 30 us -> 32.6 us
    dot_general x0 -> x8, matrix products: none -> 6.99 us  [the longest x4 3.8 us: on_device(): jnp.dot(pick, block_cond, precision=lax.Precision.HIGHEST, preferred_elem...]
    transpose x3, local copies, waits for them, and re-layouts: 3.04 us -> 6.44 us  [pack(): return jnp.moveaxis(a, 3, 1).reshape(nf * width, nx * ny)]
    all_to_all x1, blocking collectives: 30 us -> 32.6 us  [on_device(): lax.all_to_all(jnp.full((device_count,), local_total), ('gx', 'gy', 'gz')...]
    reshape x2, local copies, waits for them, and re-layouts: 0.96 us -> 3.41 us  [unpack(): return jnp.moveaxis(a.reshape(nf, width, nx, ny), 1, 3)]
    transpose x2, local copies, waits for them, and re-layouts: 2.45 us -> 4.57 us  [unpack(): return jnp.moveaxis(a.reshape(nf, width, nx, ny), 1, 3)]
    and x12, other arithmetic: 2.23 us -> 0.12 us  [axis_mask(): return (idx >= 0) & (idx < cells * lax.axis_size(axis))]
    all_to_all x1, waiting for transfers between devices: 6.11 us -> 7.72 us  [on_device(): lax.all_to_all(send, ('gx', 'gy'), split_axis=0, concat_axis=0, tiled=True)]
    reshape x2, local copies, waits for them, and re-layouts: 1.19 us -> 2.76 us  [pack(): return jnp.moveaxis(a, 3, 1).reshape(nf * width, nx * ny)]
where the time goes in v9:
time: 155 us; the launch traced here: 154 us
  starting transfers between devices  40.8 us (26%)
  blocking collectives  32.6 us (21%)
  waiting for transfers between devices  30.5 us (20%)
  other arithmetic  20 us (13%)
  local copies, waits for them, and re-layouts  19.6 us (13%)
  matrix products  7.45 us (5%)
  between operations  2.97 us (2%)
    all_to_all x1, blocking collectives, on_device(): lax.all_to_all(jnp.full((device_count,), local_total), ('gx', 'gy', 'gz')...  32.6 us
    ppermute x4, waiting for transfers between devices, exchange(): from_next = lax.ppermute(lo, axis, backward)  21.6 us
    all_to_all x1, starting transfers between devices, on_device(): lax.all_to_all(send, ('gx', 'gy'), split_axis=0, concat_axis=0, tiled=True)  18.4 us
    ppermute x4, starting transfers between devices, exchange(): from_prev = lax.ppermute(hi, axis, forward)  16 us
    select_n x4, other arithmetic, on_device(): updated = jnp.where(inside_mask(k), updated, 0.0)  8.5 us
    all_to_all x1, waiting for transfers between devices, on_device(): lax.all_to_all(send, ('gx', 'gy'), split_axis=0, concat_axis=0, tiled=True)  7.72 us
    ppermute x4, starting transfers between devices, exchange(): from_next = lax.ppermute(lo, axis, backward)  6.46 us
    transpose x3, local copies, waits for them, and re-layouts, pack(): return jnp.moveaxis(a, 3, 1).reshape(nf * width, nx * ny)  6.44 us
  transfers between devices with their start and end apart: 9, of which 5 were waited for; matrix products, arithmetic and copies ran while one was open for 5% of the time, Pallas kernels for 0%

profile of v9, /device:TPU:1, one launch (start us, length us, event | category | flops | bytes accessed | tf_op | source)
XLA Modules:
  0.0 154.0 jit_solution(1558640932941001346)
XLA Ops:
  0.6 0.0 copy-start
  0.6 0.0 copy-start.5
  0.7 0.0 copy-start.6
  0.7 0.0 copy-start.4
  0.7 0.9 convert_reduce_fusion
  1.6 0.7 convert_bitcast_fusion
  2.3 0.9 select_reduce_fusion
  3.2 0.8 fusion.65
  4.0 0.8 fusion.69
  4.8 1.0 fusion.67
  5.8 0.9 fusion.71
  6.7 0.8 fusion.73
  7.5 1.0 fusion.75
  8.4 0.8 fusion.77
  9.2 1.0 fusion.79
  10.2 0.9 copy.33
  11.1 18.4 %all-to-all-start = ((f32[128,1,520]{2,1,0:T(1,128)}), f32[128,1,520]{2,1,0:T(1,128)S(1)}, u32[]{:S(2)}, u32[]{:S(2)}) async-start(f32[128,1,520]{2,1,0:T(1,128)} %copy.33), calls=%async_computation | async-start | bytes 655360 | tf_op jit(solution)/shard_map/all_to_all | solution.py:128
  29.6 0.1 select_reduce_fusion.1
  29.7 7.2 %collective-permute-start = (f32[2,5,32,128]{3,2,1,0:T(8,128)S(1)}, f32[2,5,32,128]{3,2,1,0:T(8,128)S(1)}, u32[]{:S(2)}, u32[]{:S(2)}) collective-permute-start(f32[2,5,32,128]{3,2,1,0:T(8,128)S(1)} %get-tuple-element.31), channel_id=1, source_target_pairs={{0,32},{32,64},{64,96},{96,128},{128,160},{160,192},{192,224},{224... | collective-permute-start | bytes 491528 | tf_op jit(solution)/shard_map/ppermute | solution.py:22
  36.9 1.3 collective-permute-start.1
  38.3 0.1 broadcast_and_fusion
  38.4 0.1 broadcast_and_fusion.1
  38.5 0.1 broadcast_and_fusion.2
  38.6 7.7 %all-to-all-done = f32[128,1,520]{2,1,0:T(1,128)S(1)} async-done(((f32[128,1,520]{2,1,0:T(1,128)}), f32[128,1,520]{2,1,0:T(1,128)S(1)}, u32[]{:S(2)}, u32[]{:S(2)}) %all-to-all-start) | async-done | bytes 266272 | tf_op jit(solution)/shard_map/all_to_all | solution.py:128
  46.3 0.2 copy.34
  46.6 0.5 fusion.19
  47.1 0.0 copy-done.3
  47.1 3.1 %collective-permute-start.2 = (f32[2,4,32,128]{3,2,1,0:T(8,128)S(1)}, f32[2,4,32,128]{3,2,1,0:T(8,128)S(1)}, u32[]{:S(2)}, u32[]{:S(2)}) collective-permute-start(f32[2,4,32,128]{3,2,1,0:T(8,128)S(1)} %get-tuple-element.34), channel_id=1, source_target_pairs={{0,32},{32,64},{64,96},{96,128},{128,160},{160,192},{192,224},{224... | collective-permute-start | bytes 393224 | tf_op jit(solution)/shard_map/ppermute | solution.py:22
  50.3 1.3 collective-permute-start.3
  51.6 1.2 collective-permute-done.2
  52.9 16.8 %collective-permute-done.3 = f32[2,4,32,128]{3,2,1,0:T(8,128)S(1)} collective-permute-done((f32[2,4,32,128]{3,2,1,0:T(8,128)S(1)}, f32[2,4,32,128]{3,2,1,0:T(8,128)S(1)}, u32[]{:S(2)}, u32[]{:S(2)}) %collective-permute-start.3) | collective-permute-done | bytes 131104 | tf_op jit(solution)/shard_map/ppermute | solution.py:23
  69.6 0.0 collective-permute-done
  69.6 0.0 collective-permute-done.1
  69.8 1.9 %collective-permute-start.4 = (f32[360,128]{1,0:T(8,128)S(1)}, f32[360,128]{1,0:T(8,128)S(1)}, u32[]{:S(2)}, u32[]{:S(2)}) collective-permute-start(f32[360,128]{1,0:T(8,128)S(1)} %reshape.305), channel_id=1, source_target_pairs={{0,4},{4,8},{8,12},{12,16},{16,20},{20,24},{24,28},{1,5},{5,9},{9,... | collective-permute-start | bytes 552968 | tf_op jit(solution)/shard_map/ppermute | solution.py:22
  71.7 2.4 %collective-permute-start.5 = (f32[360,128]{1,0:T(8,128)S(1)}, f32[360,128]{1,0:T(8,128)S(1)}, u32[]{:S(2)}, u32[]{:S(2)}) collective-permute-start(f32[360,128]{1,0:T(8,128)S(1)} %reshape.307), channel_id=1, source_target_pairs={{4,0},{8,4},{12,8},{16,12},{20,16},{24,20},{28,24},{5,1},{9,5},{13... | collective-permute-start | bytes 552968 | tf_op jit(solution)/shard_map/ppermute | solution.py:23
  74.1 0.1 broadcast_and_fusion.3
  74.2 0.0 collective-permute-done.4
  74.3 4.3 %collective-permute-done.5 = f32[360,128]{1,0:T(8,128)S(1)} collective-permute-done((f32[360,128]{1,0:T(8,128)S(1)}, f32[360,128]{1,0:T(8,128)S(1)}, u32[]{:S(2)}, u32[]{:S(2)}) %collective-permute-start.5) | collective-permute-done | bytes 184352 | tf_op jit(solution)/shard_map/ppermute | solution.py:23
  78.6 0.0 copy-done.2
  78.6 0.3 pad_maximum_fusion.1
  78.9 1.8 %slice_bitcast_fusion.1 = (f32[4,5,18,42]{1,3,2,0:T(8,128)}, f32[4,5,18,42]{1,3,2,0:T(8,128)S(1)}) fusion(f32[4,18,42,128]{3,2,1,0:T(8,128)S(1)} %pad_maximum_fusion.1), kind=kLoop, calls=%fused_computation.2 | loop fusion | bytes 241920 | tf_op jit(solution)/shard_map/transpose | solution.py:45
  80.7 3.0 %copy.35 = f32[4,5,18,42]{3,2,1,0:T(8,128)} copy(f32[4,5,18,42]{1,3,2,0:T(8,128)} %get-tuple-element.15) | data formatting | bytes 120960 | tf_op jit(solution)/shard_map/transpose | solution.py:45
  83.8 1.1 reshape.309
  84.8 3.7 %collective-permute-start.6 = (f32[20,756]{1,0:T(8,128)S(1)}, f32[20,756]{1,0:T(8,128)}, u32[]{:S(2)}, u32[]{:S(2)}) collective-permute-start(f32[20,756]{1,0:T(8,128)S(1)} %reshape.309), channel_id=1, source_target_pairs={{0,1},{1,2},{2,3},{4,5},{5,6},{6,7},{8,9},{9,10},{10,11},{12,13},{... | collective-permute-start | bytes 181448 | tf_op jit(solution)/shard_map/ppermute | solution.py:22
  88.6 1.6 %copy.36 = f32[4,5,18,42]{3,2,1,0:T(8,128)} copy(f32[4,5,18,42]{1,3,2,0:T(8,128)S(1)} %get-tuple-element.16) | data formatting | bytes 120960 | tf_op jit(solution)/shard_map/transpose | solution.py:45
  90.1 1.7 %reshape.311 = f32[20,756]{1,0:T(8,128)} reshape(f32[4,5,18,42]{3,2,1,0:T(8,128)} %copy.36) | data formatting | bytes 120960 | tf_op jit(solution)/shard_map/reshape | solution.py:45
  91.8 1.5 collective-permute-start.7
  93.3 0.0 collective-permute-done.6
  93.3 1.7 %reshape.310 = f32[4,5,18,42]{3,2,1,0:T(8,128)} reshape(f32[20,756]{1,0:T(8,128)} %collective-permute-done.6) | data formatting | bytes 120960 | tf_op jit(solution)/shard_map/reshape | solution.py:48
  95.0 1.7 %copy.37 = f32[4,18,42,5]{3,2,1,0:T(8,128)S(1)} copy(f32[4,18,42,5]{2,1,3,0:T(8,128)} %bitcast.55) | data formatting | bytes 120960 | tf_op jit(solution)/shard_map/transpose | solution.py:48
  96.7 0.5 collective-permute-done.7
  97.2 1.7 %reshape.312 = f32[4,5,18,42]{3,2,1,0:T(8,128)} reshape(f32[20,756]{1,0:T(8,128)} %collective-permute-done.7) | data formatting | bytes 120960 | tf_op jit(solution)/shard_map/reshape | solution.py:48
  99.0 2.9 %copy.38 = f32[4,18,42,5]{3,2,1,0:T(8,128)} copy(f32[4,18,42,5]{2,1,3,0:T(8,128)} %bitcast.56) | data formatting | bytes 120960 | tf_op jit(solution)/shard_map/transpose | solution.py:48
  101.8 4.8 %pad_maximum_fusion = f32[4,18,42,138]{3,2,1,0:T(8,128)S(1)} fusion(f32[4,18,42,5]{3,2,1,0:T(8,128)} %copy.38, f32[4,18,5,128]{3,2,1,0:T(8,128)S(1)} %reshape.308, f32[2,18,32,128]{3,2,1,0:T(8,128)S(1)} %broadcast_dynamic-update-slice_fusion.1, f32[2,5,32,128]{3,2,1,0:T(8,128)} %copy-done.2, f32[1,8,32,128]{3,2,1,0:T(8,128)S(1)} %bitcast.49, ...), kind=kLoop, calls=%fused_computation | loop fusion | flops 3338496 | bytes 3338496 | tf_op jit(solution)/shard_map/concatenate | solution.py:51
  106.6 0.3 slice_bitcast_fusion.3
  107.0 2.7 %fusion.5 = (f32[16,40,136]{2,1,0:T(8,128)S(1)}, f32[16,40,136]{2,1,0:T(8,128)S(1)}, f32[16,40,136]{2,1,0:T(8,128)S(1)}, f32[16,40,136]{2,1,0:T(8,128)S(1)}, f32...) fusion(f32[18,42,138]{2,1,0:T(8,128)S(1)} %get-tuple-element.14, ...), kind=kLoop, calls=%fused_computation.15 | loop fusion | flops 3742720 | bytes 8008456 | tf_op jit(solution)/shard_map/jit(_where)/select_n | solution.py:199
  109.7 0.3 slice_add_fusion
  110.1 2.2 %fusion.11 = f32[14,38,134]{2,1,0:T(8,128)S(1)} fusion(f32[16,40,136]{2,1,0:T(8,128)S(1)} %slice_add_fusion, f32[16,40,136]{2,1,0:T(8,128)S(1)} %get-tuple-element.4, f32[16,40,136]{2,1,0:T(8,128)S(1)} %get-tuple-element.10, f32[16,40,136]{2,1,0:T(8,128)S(1)} %get-tuple-element.9, f32[16,40,136]{2,1,0:T(8,128)S(1)} %get-tuple-element.8, ...), kind=kLoop, calls=%fused_computation.34 | loop fusion | flops 1283184 | bytes 4563098 | tf_op jit(solution)/shard_map/jit(_where)/select_n | solution.py:199
  112.3 1.9 %fusion.30 = f32[12,36,132]{2,1,0:T(8,128)S(1)} fusion(f32[16,40,136]{2,1,0:T(8,128)S(1)} %slice_add_fusion, f32[14,38,134]{2,1,0:T(8,128)S(1)} %fusion.11, f32[16,40,136]{2,1,0:T(8,128)S(1)} %get-tuple-element.10, f32[16,40,136]{2,1,0:T(8,128)S(1)} %get-tuple-element.9, f32[16,40,136]{2,1,0:T(8,128)S(1)} %get-tuple-element.8, ...), kind=kLoop, calls=%fused_computation.64 | loop fusion | flops 1026432 | bytes 3650100 | tf_op jit(solution)/shard_map/jit(_where)/select_n | solution.py:199
  114.2 1.6 %fusion.39 = f32[10,34,130]{2,1,0:T(8,128)S(1)} fusion(f32[16,40,136]{2,1,0:T(8,128)S(1)} %slice_add_fusion, f32[12,36,132]{2,1,0:T(8,128)S(1)} %fusion.30, f32[16,40,136]{2,1,0:T(8,128)S(1)} %get-tuple-element.10, f32[16,40,136]{2,1,0:T(8,128)S(1)} %get-tuple-element.9, f32[16,40,136]{2,1,0:T(8,128)S(1)} %get-tuple-element.8, ...), kind=kLoop, calls=%fused_computation.81 | loop fusion | flops 795600 | bytes 2829270 | tf_op jit(solution)/shard_map/jit(_where)/select_n | solution.py:199
  115.9 1.8 %fusion.54 = (f32[]{:T(128)}, f32[8,32,128]{2,1,0:T(8,128)}) fusion(f32[16,40,136]{2,1,0:T(8,128)S(1)} %slice_add_fusion, f32[10,34,130]{2,1,0:T(8,128)S(1)} %fusion.39, f32[16,40,136]{2,1,0:T(8,128)S(1)} %get-tuple-element.10, f32[16,40,136]{2,1,0:T(8,128)S(1)} %get-tuple-element.9, f32[16,40,136]{2,1,0:T(8,128)S(1)} %get-tuple-element.8, ...), kind=kLoop, calls=%fused_computation.118 | loop fusion | flops 524287 | bytes 2097156 | tf_op jit(solution)/shard_map/reduce_sum | solution.py:207
  117.7 0.8 broadcast_in_dim.52
  118.5 32.6 %all_to_all.18 = f32[512,1,1]{2,1,0:T(1,128)S(1)} all-to-all(f32[512,1,1]{2,1,0:T(1,128)S(1)} %broadcast_in_dim.52), channel_id=1, replica_groups=mesh['gx'=16,'gy'=8,'gz'=4] {'gx','gy','gz'}, dimensions={0} | all-to-all | bytes 4096 | tf_op jit(solution)/shard_map/all_to_all | solution.py:209
  151.0 1.1 reduce_sum.49
  (41 shorter events, 0.6 us)
Async XLA Ops:
  0.6 4.2 %copy-start = (f32[128,128]{1,0:T(8,128)S(1)}, f32[128,128]{1,0:T(8,128)}, u32[]{:S(2)}) copy-start(f32[128,128]{1,0:T(8,128)} %param.15) | copy-start | bytes 196612
  0.6 28.9 %copy-start.5 = (f32[6]{0:T(128)S(1)}, f32[6]{0:T(128)}, u32[]{:S(2)}) copy-start(f32[6]{0:T(128)} %param.12) | copy-start | bytes 76
  0.7 28.9 %copy-start.6 = (s32[128]{0:T(128)S(1)}, s32[128]{0:T(128)}, u32[]{:S(2)}) copy-start(s32[128]{0:T(128)} %param.13) | copy-start | bytes 1540
  0.7 29.0 %copy-start.4 = (f32[8,32,128]{2,1,0:T(8,128)S(1)}, f32[8,32,128]{2,1,0:T(8,128)}, u32[]{:S(2)}) copy-start(f32[8,32,128]{2,1,0:T(8,128)} %param.11) | copy-start | bytes 393220
  0.7 29.0 %copy-start.1 = (f32[8,32,128]{2,1,0:T(8,128)S(1)}, f32[8,32,128]{2,1,0:T(8,128)}, u32[]{:S(2)}) copy-start(f32[8,32,128]{2,1,0:T(8,128)} %param.19) | copy-start | bytes 393220
  11.1 35.2 %all-to-all-start = ((f32[128,1,520]{2,1,0:T(1,128)}), f32[128,1,520]{2,1,0:T(1,128)S(1)}, u32[]{:S(2)}, u32[]{:S(2)}) async-start(f32[128,1,520]{2,1,0:T(1,128)} %copy.33), calls=%async_computation | async-start | bytes 655360 | tf_op jit(solution)/shard_map/all_to_all | solution.py:128
  29.7 39.9 %collective-permute-start = (f32[2,5,32,128]{3,2,1,0:T(8,128)S(1)}, f32[2,5,32,128]{3,2,1,0:T(8,128)S(1)}, u32[]{:S(2)}, u32[]{:S(2)}) collective-permute-start(f32[2,5,32,128]{3,2,1,0:T(8,128)S(1)} %get-tuple-element.31), channel_id=1, source_target_pairs={{0,32},{32,64},{64,96},{96,128},{128,160},{160,192},{192,224},{224... | collective-permute-start | bytes 491528 | tf_op jit(solution)/shard_map/ppermute | solution.py:22
  36.9 32.8 %collective-permute-start.1 = (f32[2,5,32,128]{3,2,1,0:T(8,128)S(1)}, f32[2,5,32,128]{3,2,1,0:T(8,128)S(1)}, u32[]{:S(2)}, u32[]{:S(2)}) collective-permute-start(f32[2,5,32,128]{3,2,1,0:T(8,128)S(1)} %get-tuple-element.32), channel_id=1, source_target_pairs={{32,0},{64,32},{96,64},{128,96},{160,128},{192,160},{224,192},{256... | collective-permute-start | bytes 491528 | tf_op jit(solution)/shard_map/ppermute | solution.py:23
  38.6 8.5 %copy-start.3 = (f32[8,32,128]{2,1,0:T(8,128)S(1)}, f32[8,32,128]{2,1,0:T(8,128)}, u32[]{:S(2)}) copy-start(f32[8,32,128]{2,1,0:T(8,128)} %param.10) | copy-start | bytes 393220
  47.1 5.7 %collective-permute-start.2 = (f32[2,4,32,128]{3,2,1,0:T(8,128)S(1)}, f32[2,4,32,128]{3,2,1,0:T(8,128)S(1)}, u32[]{:S(2)}, u32[]{:S(2)}) collective-permute-start(f32[2,4,32,128]{3,2,1,0:T(8,128)S(1)} %get-tuple-element.34), channel_id=1, source_target_pairs={{0,32},{32,64},{64,96},{96,128},{128,160},{160,192},{192,224},{224... | collective-permute-start | bytes 393224 | tf_op jit(solution)/shard_map/ppermute | solution.py:22
  50.3 19.3 %collective-permute-start.3 = (f32[2,4,32,128]{3,2,1,0:T(8,128)S(1)}, f32[2,4,32,128]{3,2,1,0:T(8,128)S(1)}, u32[]{:S(2)}, u32[]{:S(2)}) collective-permute-start(f32[2,4,32,128]{3,2,1,0:T(8,128)S(1)} %get-tuple-element.33), channel_id=1, source_target_pairs={{32,0},{64,32},{96,64},{128,96},{160,128},{192,160},{224,192},{256... | collective-permute-start | bytes 393224 | tf_op jit(solution)/shard_map/ppermute | solution.py:23
  69.7 9.0 %copy-start.2 = (f32[2,5,32,128]{3,2,1,0:T(8,128)}, f32[2,5,32,128]{3,2,1,0:T(8,128)S(1)}, u32[]{:S(2)}) copy-start(f32[2,5,32,128]{3,2,1,0:T(8,128)S(1)} %collective-permute-done.1) | copy-start | bytes 491524
  69.8 4.5 %collective-permute-start.4 = (f32[360,128]{1,0:T(8,128)S(1)}, f32[360,128]{1,0:T(8,128)S(1)}, u32[]{:S(2)}, u32[]{:S(2)}) collective-permute-start(f32[360,128]{1,0:T(8,128)S(1)} %reshape.305), channel_id=1, source_target_pairs={{0,4},{4,8},{8,12},{12,16},{16,20},{20,24},{24,28},{1,5},{5,9},{9,... | collective-permute-start | bytes 552968 | tf_op jit(solution)/shard_map/ppermute | solution.py:22
  71.7 6.9 %collective-permute-start.5 = (f32[360,128]{1,0:T(8,128)S(1)}, f32[360,128]{1,0:T(8,128)S(1)}, u32[]{:S(2)}, u32[]{:S(2)}) collective-permute-start(f32[360,128]{1,0:T(8,128)S(1)} %reshape.307), channel_id=1, source_target_pairs={{4,0},{8,4},{12,8},{16,12},{20,16},{24,20},{28,24},{5,1},{9,5},{13... | collective-permute-start | bytes 552968 | tf_op jit(solution)/shard_map/ppermute | solution.py:23
  84.8 8.5 %collective-permute-start.6 = (f32[20,756]{1,0:T(8,128)S(1)}, f32[20,756]{1,0:T(8,128)}, u32[]{:S(2)}, u32[]{:S(2)}) collective-permute-start(f32[20,756]{1,0:T(8,128)S(1)} %reshape.309), channel_id=1, source_target_pairs={{0,1},{1,2},{2,3},{4,5},{5,6},{6,7},{8,9},{9,10},{10,11},{12,13},{... | collective-permute-start | bytes 181448 | tf_op jit(solution)/shard_map/ppermute | solution.py:22
  91.8 5.4 %collective-permute-start.7 = (f32[20,756]{1,0:T(8,128)}, f32[20,756]{1,0:T(8,128)}, u32[]{:S(2)}, u32[]{:S(2)}) collective-permute-start(f32[20,756]{1,0:T(8,128)} %reshape.311), channel_id=1, source_target_pairs={{1,0},{2,1},{3,2},{5,4},{6,5},{7,6},{9,8},{10,9},{11,10},{13,12},{... | collective-permute-start | bytes 181448 | tf_op jit(solution)/shard_map/ppermute | solution.py:23

commit v10 on v8

--- a/solution.py
+++ b/solution.py
@@ -112,7 +112,11 @@
     earlier = order[None, :] < order[:, None]
     slot_rank = jnp.sum((same_dest & earlier).astype(jnp.int32), axis=1)
     position = block_dest * capacity + slot_rank
-    block_volts = table_lookup(gate_volts, block_gate)
+    gate_labels = jnp.arange(gate_volts.shape[0], dtype=jnp.int32)
+    gate_pick = (block_gate[:, None] == gate_labels[None, :]).astype(jnp.float32)
+    block_volts = jnp.dot(
+        gate_pick, gate_volts, precision=lax.Precision.HIGHEST, preferred_element_type=jnp.float32
+    )
     rows = jnp.concatenate(
         [
             block_cond,

time: 142 us -> 143 us (level)
  no operation moved by 1% of the time
where the time goes in v10:
time: 143 us; the launch traced here: 142 us
  starting transfers between devices  40.2 us (28%)
  blocking collectives  30.4 us (21%)
  waiting for transfers between devices  28.8 us (20%)
  other arithmetic  24.7 us (17%)
  local copies, waits for them, and re-layouts  12.2 us (9%)
  between operations  3 us (2%)
  matrix products  2.81 us (2%)
    all_to_all x1, blocking collectives, on_device(): lax.all_to_all(jnp.full((device_count,), local_total), ('gx', 'gy', 'gz')...  30.4 us
    ppermute x4, waiting for transfers between devices, exchange(): from_next = lax.ppermute(lo, axis, backward)  22.1 us
    all_to_all x1, starting transfers between devices, on_device(): lax.all_to_all(send, ('gx', 'gy'), split_axis=0, concat_axis=0, tiled=True)  18.4 us
    ppermute x4, starting transfers between devices, exchange(): from_prev = lax.ppermute(hi, axis, forward)  15.4 us
    select_n x4, other arithmetic, on_device(): updated = jnp.where(inside_mask(k), updated, 0.0)  8.51 us
    ppermute x4, starting transfers between devices, exchange(): from_next = lax.ppermute(lo, axis, backward)  6.47 us
    all_to_all x1, waiting for transfers between devices, on_device(): lax.all_to_all(send, ('gx', 'gy'), split_axis=0, concat_axis=0, tiled=True)  5.53 us
    concatenate x1, other arithmetic, with_wide_halo(): return jnp.concatenate([unpack(prev), fields, unpack(nxt)], axis=3)  4.82 us
  transfers between devices with their start and end apart: 9, of which 5 were waited for; matrix products, arithmetic and copies ran while one was open for 5% of the time, Pallas kernels for 0%

profile of v10, /device:TPU:1, one launch (start us, length us, event | category | flops | bytes accessed | tf_op | source)
XLA Modules:
  0.0 142.0 jit_solution(4799333598382230089)
XLA Ops:
  0.6 0.0 copy-start
  0.7 0.7 convert_bitcast_fusion
  1.4 0.1 copy.38
  1.5 0.9 convert_reduce_fusion
  2.4 0.7 multiply_add_fusion
  3.1 1.1 convolution_bitcast_fusion
  4.2 1.3 fusion.45
  5.5 1.4 all_to_all.13
  6.8 18.4 %all-to-all-start = ((f32[128,1,520]{2,1,0:T(1,128)}), f32[128,1,520]{2,1,0:T(1,128)S(1)}, u32[]{:S(2)}, u32[]{:S(2)}) async-start(f32[128,1,520]{2,1,0:T(1,128)} %all_to_all.13), calls=%async_computation | async-start | bytes 655360 | tf_op jit(solution)/shard_map/all_to_all | solution.py:135
  25.3 0.1 select_reduce_fusion
  25.4 7.2 %collective-permute-start = (f32[2,5,32,128]{3,2,1,0:T(8,128)S(1)}, f32[2,5,32,128]{3,2,1,0:T(8,128)S(1)}, u32[]{:S(2)}, u32[]{:S(2)}) collective-permute-start(f32[2,5,32,128]{3,2,1,0:T(8,128)S(1)} %get-tuple-element.21), channel_id=1, source_target_pairs={{0,32},{32,64},{64,96},{96,128},{128,160},{160,192},{192,224},{224... | collective-permute-start | bytes 491528 | tf_op jit(solution)/shard_map/ppermute | solution.py:22
  32.6 1.3 collective-permute-start.1
  33.9 0.5 compare_and_fusion
  34.5 0.6 compare_and_fusion.3
  35.1 0.6 compare_and_fusion.6
  35.7 0.1 broadcast_and_fusion
  35.7 0.7 broadcast_and_fusion.1
  36.4 0.1 broadcast_and_fusion.2
  36.5 5.5 %all-to-all-done = f32[128,1,520]{2,1,0:T(1,128)S(1)} async-done(((f32[128,1,520]{2,1,0:T(1,128)}), f32[128,1,520]{2,1,0:T(1,128)S(1)}, u32[]{:S(2)}, u32[]{:S(2)}) %all-to-all-start) | async-done | bytes 266272 | tf_op jit(solution)/shard_map/all_to_all | solution.py:135
  42.0 0.8 reduce.1
  42.8 0.0 copy-start.7
  42.8 0.3 reshape.266
  43.1 0.1 slice_reduce_fusion
  43.2 0.2 fusion.42
  43.4 0.1 fusion.67
  43.6 0.5 fusion.19
  44.1 3.1 %collective-permute-start.2 = (f32[2,4,32,128]{3,2,1,0:T(8,128)S(1)}, f32[2,4,32,128]{3,2,1,0:T(8,128)S(1)}, u32[]{:S(2)}, u32[]{:S(2)}) collective-permute-start(f32[2,4,32,128]{3,2,1,0:T(8,128)S(1)} %get-tuple-element.24), channel_id=1, source_target_pairs={{0,32},{32,64},{64,96},{96,128},{128,160},{160,192},{192,224},{224... | collective-permute-start | bytes 393224 | tf_op jit(solution)/shard_map/ppermute | solution.py:22
  47.3 1.3 collective-permute-start.3
  48.6 1.2 collective-permute-done.2
  49.9 15.5 %collective-permute-done.3 = f32[2,4,32,128]{3,2,1,0:T(8,128)S(1)} collective-permute-done((f32[2,4,32,128]{3,2,1,0:T(8,128)S(1)}, f32[2,4,32,128]{3,2,1,0:T(8,128)S(1)}, u32[]{:S(2)}, u32[]{:S(2)}) %collective-permute-start.3) | collective-permute-done | bytes 131104 | tf_op jit(solution)/shard_map/ppermute | solution.py:23
  65.5 1.9 %collective-permute-start.4 = (f32[360,128]{1,0:T(8,128)S(1)}, f32[360,128]{1,0:T(8,128)S(1)}, u32[]{:S(2)}, u32[]{:S(2)}) collective-permute-start(f32[360,128]{1,0:T(8,128)S(1)} %reshape.268), channel_id=1, source_target_pairs={{0,4},{4,8},{8,12},{12,16},{16,20},{20,24},{24,28},{1,5},{5,9},{9,... | collective-permute-start | bytes 552968 | tf_op jit(solution)/shard_map/ppermute | solution.py:22
  67.5 2.4 %collective-permute-start.5 = (f32[360,128]{1,0:T(8,128)S(1)}, f32[360,128]{1,0:T(8,128)S(1)}, u32[]{:S(2)}, u32[]{:S(2)}) collective-permute-start(f32[360,128]{1,0:T(8,128)S(1)} %reshape.270), channel_id=1, source_target_pairs={{4,0},{8,4},{12,8},{16,12},{20,16},{24,20},{28,24},{5,1},{9,5},{13... | collective-permute-start | bytes 552968 | tf_op jit(solution)/shard_map/ppermute | solution.py:23
  69.9 0.1 broadcast_and_fusion.3
  70.1 4.3 %collective-permute-done.5 = f32[360,128]{1,0:T(8,128)S(1)} collective-permute-done((f32[360,128]{1,0:T(8,128)S(1)}, f32[360,128]{1,0:T(8,128)S(1)}, u32[]{:S(2)}, u32[]{:S(2)}) %collective-permute-start.5) | collective-permute-done | bytes 184352 | tf_op jit(solution)/shard_map/ppermute | solution.py:23
  74.4 0.7 reshape.271
  75.1 1.2 pad_maximum_fusion.1
  76.4 0.6 slice_bitcast_fusion.1
  77.0 1.6 %copy.41 = f32[4,5,18,42]{3,2,1,0:T(8,128)} copy(f32[4,5,18,42]{1,3,2,0:T(8,128)S(1)} %get-tuple-element.15) | data formatting | bytes 120960 | tf_op jit(solution)/shard_map/transpose | solution.py:45
  78.5 1.1 reshape.272
  79.6 3.1 %collective-permute-start.6 = (f32[20,756]{1,0:T(8,128)S(1)}, f32[20,756]{1,0:T(8,128)S(1)}, u32[]{:S(2)}, u32[]{:S(2)}) collective-permute-start(f32[20,756]{1,0:T(8,128)S(1)} %reshape.272), channel_id=1, source_target_pairs={{0,1},{1,2},{2,3},{4,5},{5,6},{6,7},{8,9},{9,10},{10,11},{12,13},{... | collective-permute-start | bytes 181448 | tf_op jit(solution)/shard_map/ppermute | solution.py:22
  82.7 0.9 copy.42
  83.6 0.1 reshape.274
  83.7 1.5 %collective-permute-start.7 = (f32[20,756]{1,0:T(8,128)S(1)}, f32[20,756]{1,0:T(8,128)S(1)}, u32[]{:S(2)}, u32[]{:S(2)}) collective-permute-start(f32[20,756]{1,0:T(8,128)S(1)} %reshape.274), channel_id=1, source_target_pairs={{1,0},{2,1},{3,2},{5,4},{6,5},{7,6},{9,8},{10,9},{11,10},{13,12},{... | collective-permute-start | bytes 181448 | tf_op jit(solution)/shard_map/ppermute | solution.py:23
  85.2 0.5 compare_and_fusion.9
  85.7 0.1 reshape.273
  85.8 0.8 copy.43
  86.6 2.2 %collective-permute-done.7 = f32[20,756]{1,0:T(8,128)S(1)} collective-permute-done((f32[20,756]{1,0:T(8,128)S(1)}, f32[20,756]{1,0:T(8,128)S(1)}, u32[]{:S(2)}, u32[]{:S(2)}) %collective-permute-start.7) | collective-permute-done | bytes 60512 | tf_op jit(solution)/shard_map/ppermute | solution.py:23
  88.8 0.8 reshape.275
  89.7 1.7 %copy.44 = f32[4,18,42,5]{3,2,1,0:T(8,128)S(1)} copy(f32[4,18,42,5]{2,1,3,0:T(8,128)} %bitcast.37) | data formatting | bytes 120960 | tf_op jit(solution)/shard_map/transpose | solution.py:48
  91.3 4.8 %pad_maximum_fusion = f32[4,18,42,138]{3,2,1,0:T(8,128)S(1)} fusion(f32[4,18,42,5]{3,2,1,0:T(8,128)S(1)} %copy.44, f32[4,18,5,128]{3,2,1,0:T(8,128)} %reshape.271, f32[2,18,32,128]{3,2,1,0:T(8,128)} %copy-done.1, f32[2,5,32,128]{3,2,1,0:T(8,128)} %copy-done.6, f32[1,8,32,128]{3,2,1,0:T(8,128)} %bitcast.30, f32[1,8,32,128]{3,2,1,0:T(8,128)} %copy-done.2, ...), kind=kLoop, calls=%fused_computation | loop fusion | flops 3338496 | bytes 3338496 | tf_op jit(solution)/shard_map/concatenate | solution.py:51
  96.2 0.0 copy-start.10
  96.2 0.3 slice_bitcast_fusion.3
  96.5 0.3 copy-done.10
  96.8 2.7 %fusion.5 = (f32[16,40,136]{2,1,0:T(8,128)S(1)}, f32[16,40,136]{2,1,0:T(8,128)S(1)}, f32[16,40,136]{2,1,0:T(8,128)S(1)}, f32[16,40,136]{2,1,0:T(8,128)S(1)}, f32...) fusion(f32[18,42,138]{2,1,0:T(8,128)S(1)} %get-tuple-element.14, ...), kind=kLoop, calls=%fused_computation.16 | loop fusion | flops 3742720 | bytes 8008456 | tf_op jit(solution)/shard_map/jit(_where)/select_n | solution.py:200
  99.6 0.4 slice_add_fusion
  100.0 0.3 copy-done.9
  100.2 0.0 copy-done.13
  100.2 2.2 %fusion.11 = f32[14,38,134]{2,1,0:T(8,128)S(1)} fusion(f32[16,40,136]{2,1,0:T(8,128)S(1)} %slice_add_fusion, f32[16,40,136]{2,1,0:T(8,128)S(1)} %get-tuple-element.4, f32[16,40,136]{2,1,0:T(8,128)S(1)} %get-tuple-element.10, f32[16,40,136]{2,1,0:T(8,128)S(1)} %get-tuple-element.9, f32[16,40,136]{2,1,0:T(8,128)S(1)} %get-tuple-element.8, ...), kind=kLoop, calls=%fused_computation.35 | loop fusion | flops 1283184 | bytes 4563098 | tf_op jit(solution)/shard_map/jit(_where)/select_n | solution.py:200
  102.5 1.9 %fusion.24 = f32[12,36,132]{2,1,0:T(8,128)S(1)} fusion(f32[16,40,136]{2,1,0:T(8,128)S(1)} %slice_add_fusion, f32[14,38,134]{2,1,0:T(8,128)S(1)} %fusion.11, f32[16,40,136]{2,1,0:T(8,128)S(1)} %get-tuple-element.10, f32[16,40,136]{2,1,0:T(8,128)S(1)} %get-tuple-element.9, f32[16,40,136]{2,1,0:T(8,128)S(1)} %get-tuple-element.8, ...), kind=kLoop, calls=%fused_computation.58 | loop fusion | flops 1026432 | bytes 3650100 | tf_op jit(solution)/shard_map/jit(_where)/select_n | solution.py:200
  104.5 1.6 %fusion.33 = f32[10,34,130]{2,1,0:T(8,128)S(1)} fusion(f32[16,40,136]{2,1,0:T(8,128)S(1)} %slice_add_fusion, f32[12,36,132]{2,1,0:T(8,128)S(1)} %fusion.24, f32[16,40,136]{2,1,0:T(8,128)S(1)} %get-tuple-element.10, f32[16,40,136]{2,1,0:T(8,128)S(1)} %get-tuple-element.9, f32[16,40,136]{2,1,0:T(8,128)S(1)} %get-tuple-element.8, ...), kind=kLoop, calls=%fused_computation.75 | loop fusion | flops 795600 | bytes 2829270 | tf_op jit(solution)/shard_map/jit(_where)/select_n | solution.py:200
  106.1 1.8 %fusion.51 = (f32[]{:T(128)}, f32[8,32,128]{2,1,0:T(8,128)}) fusion(f32[16,40,136]{2,1,0:T(8,128)S(1)} %slice_add_fusion, f32[10,34,130]{2,1,0:T(8,128)S(1)} %fusion.33, f32[16,40,136]{2,1,0:T(8,128)S(1)} %get-tuple-element.10, f32[16,40,136]{2,1,0:T(8,128)S(1)} %get-tuple-element.9, f32[16,40,136]{2,1,0:T(8,128)S(1)} %get-tuple-element.8, ...), kind=kLoop, calls=%fused_computation.117 | loop fusion | flops 524287 | bytes 2097156 | tf_op jit(solution)/shard_map/reduce_sum | solution.py:208
  107.9 0.8 broadcast_in_dim.45
  108.7 30.4 %all_to_all.16 = f32[512,1,1]{2,1,0:T(1,128)S(1)} all-to-all(f32[512,1,1]{2,1,0:T(1,128)S(1)} %broadcast_in_dim.45), channel_id=1, replica_groups=mesh['gx'=16,'gy'=8,'gz'=4] {'gx','gy','gz'}, dimensions={0} | all-to-all | bytes 4096 | tf_op jit(solution)/shard_map/all_to_all | solution.py:210
  139.1 1.1 reduce_sum.39
  (52 shorter events, 0.4 us)
Async XLA Ops:
  0.6 2.5 %copy-start = (f32[1000]{0:T(1024)S(1)}, f32[1000]{0:T(1024)}, u32[]{:S(2)}) copy-start(f32[1000]{0:T(1024)} %param.14) | copy-start | bytes 12004
  0.6 24.6 %copy-start.14 = (f32[6]{0:T(128)S(1)}, f32[6]{0:T(128)}, u32[]{:S(2)}) copy-start(f32[6]{0:T(128)} %param.12) | copy-start | bytes 76
  0.7 24.6 %copy-start.15 = (s32[128]{0:T(128)S(1)}, s32[128]{0:T(128)}, u32[]{:S(2)}) copy-start(s32[128]{0:T(128)} %param.13) | copy-start | bytes 1540
  0.7 24.7 %copy-start.8 = (f32[8,32,128]{2,1,0:T(8,128)S(1)}, f32[8,32,128]{2,1,0:T(8,128)}, u32[]{:S(2)}) copy-start(f32[8,32,128]{2,1,0:T(8,128)} %param.11) | copy-start | bytes 393220
  0.7 24.7 %copy-start.4 = (f32[8,32,128]{2,1,0:T(8,128)S(1)}, f32[8,32,128]{2,1,0:T(8,128)}, u32[]{:S(2)}) copy-start(f32[8,32,128]{2,1,0:T(8,128)} %param.19) | copy-start | bytes 393220
  6.8 35.2 %all-to-all-start = ((f32[128,1,520]{2,1,0:T(1,128)}), f32[128,1,520]{2,1,0:T(1,128)S(1)}, u32[]{:S(2)}, u32[]{:S(2)}) async-start(f32[128,1,520]{2,1,0:T(1,128)} %all_to_all.13), calls=%async_computation | async-start | bytes 655360 | tf_op jit(solution)/shard_map/all_to_all | solution.py:135
  25.4 49.7 %copy-start.2 = (f32[1,8,32,128]{3,2,1,0:T(8,128)}, f32[1,8,32,128]{3,2,1,0:T(8,128)S(1)}, u32[]{:S(2)}) copy-start(f32[1,8,32,128]{3,2,1,0:T(8,128)S(1)} %multiply_bitcast_fusion) | copy-start | bytes 393220
  25.4 40.0 %collective-permute-start = (f32[2,5,32,128]{3,2,1,0:T(8,128)S(1)}, f32[2,5,32,128]{3,2,1,0:T(8,128)S(1)}, u32[]{:S(2)}, u32[]{:S(2)}) collective-permute-start(f32[2,5,32,128]{3,2,1,0:T(8,128)S(1)} %get-tuple-element.21), channel_id=1, source_target_pairs={{0,32},{32,64},{64,96},{96,128},{128,160},{160,192},{192,224},{224... | collective-permute-start | bytes 491528 | tf_op jit(solution)/shard_map/ppermute | solution.py:22
  32.6 32.8 %collective-permute-start.1 = (f32[2,5,32,128]{3,2,1,0:T(8,128)S(1)}, f32[2,5,32,128]{3,2,1,0:T(8,128)S(1)}, u32[]{:S(2)}, u32[]{:S(2)}) collective-permute-start(f32[2,5,32,128]{3,2,1,0:T(8,128)S(1)} %get-tuple-element.22), channel_id=1, source_target_pairs={{32,0},{64,32},{96,64},{128,96},{160,128},{192,160},{224,192},{256... | collective-permute-start | bytes 491528 | tf_op jit(solution)/shard_map/ppermute | solution.py:23
  42.8 1.3 copy-start.7
  44.1 5.7 %collective-permute-start.2 = (f32[2,4,32,128]{3,2,1,0:T(8,128)S(1)}, f32[2,4,32,128]{3,2,1,0:T(8,128)S(1)}, u32[]{:S(2)}, u32[]{:S(2)}) collective-permute-start(f32[2,4,32,128]{3,2,1,0:T(8,128)S(1)} %get-tuple-element.24), channel_id=1, source_target_pairs={{0,32},{32,64},{64,96},{96,128},{128,160},{160,192},{192,224},{224... | collective-permute-start | bytes 393224 | tf_op jit(solution)/shard_map/ppermute | solution.py:22
  47.3 18.1 %collective-permute-start.3 = (f32[2,4,32,128]{3,2,1,0:T(8,128)S(1)}, f32[2,4,32,128]{3,2,1,0:T(8,128)S(1)}, u32[]{:S(2)}, u32[]{:S(2)}) collective-permute-start(f32[2,4,32,128]{3,2,1,0:T(8,128)S(1)} %get-tuple-element.23), channel_id=1, source_target_pairs={{32,0},{64,32},{96,64},{128,96},{160,128},{192,160},{224,192},{256... | collective-permute-start | bytes 393224 | tf_op jit(solution)/shard_map/ppermute | solution.py:23
  65.4 9.7 %copy-start.1 = (f32[2,18,32,128]{3,2,1,0:T(8,128)}, f32[2,18,32,128]{3,2,1,0:T(8,128)S(1)}, u32[]{:S(2)}) copy-start(f32[2,18,32,128]{3,2,1,0:T(8,128)S(1)} %broadcast_dynamic-update-slice_fusion.1) | copy-start | bytes 1769476
  65.4 9.7 %copy-start.5 = (f32[2,5,32,128]{3,2,1,0:T(8,128)}, f32[2,5,32,128]{3,2,1,0:T(8,128)S(1)}, u32[]{:S(2)}) copy-start(f32[2,5,32,128]{3,2,1,0:T(8,128)S(1)} %collective-permute-done) | copy-start | bytes 491524
  65.4 9.7 %copy-start.6 = (f32[2,5,32,128]{3,2,1,0:T(8,128)}, f32[2,5,32,128]{3,2,1,0:T(8,128)S(1)}, u32[]{:S(2)}) copy-start(f32[2,5,32,128]{3,2,1,0:T(8,128)S(1)} %collective-permute-done.1) | copy-start | bytes 491524
  65.5 4.5 %collective-permute-start.4 = (f32[360,128]{1,0:T(8,128)S(1)}, f32[360,128]{1,0:T(8,128)S(1)}, u32[]{:S(2)}, u32[]{:S(2)}) collective-permute-start(f32[360,128]{1,0:T(8,128)S(1)} %reshape.268), channel_id=1, source_target_pairs={{0,4},{4,8},{8,12},{12,16},{16,20},{20,24},{24,28},{1,5},{5,9},{9,... | collective-permute-start | bytes 552968 | tf_op jit(solution)/shard_map/ppermute | solution.py:22
  67.5 6.9 %collective-permute-start.5 = (f32[360,128]{1,0:T(8,128)S(1)}, f32[360,128]{1,0:T(8,128)S(1)}, u32[]{:S(2)}, u32[]{:S(2)}) collective-permute-start(f32[360,128]{1,0:T(8,128)S(1)} %reshape.270), channel_id=1, source_target_pairs={{4,0},{8,4},{12,8},{16,12},{20,16},{24,20},{28,24},{5,1},{9,5},{13... | collective-permute-start | bytes 552968 | tf_op jit(solution)/shard_map/ppermute | solution.py:23
  70.0 5.1 %copy-start.3 = (f32[4,18,5,128]{3,2,1,0:T(8,128)}, f32[4,18,5,128]{3,2,1,0:T(8,128)S(1)}, u32[]{:S(2)}) copy-start(f32[4,18,5,128]{3,2,1,0:T(8,128)S(1)} %reshape.269) | copy-start | bytes 552964
  79.6 6.1 %collective-permute-start.6 = (f32[20,756]{1,0:T(8,128)S(1)}, f32[20,756]{1,0:T(8,128)S(1)}, u32[]{:S(2)}, u32[]{:S(2)}) collective-permute-start(f32[20,756]{1,0:T(8,128)S(1)} %reshape.272), channel_id=1, source_target_pairs={{0,1},{1,2},{2,3},{4,5},{5,6},{6,7},{8,9},{9,10},{10,11},{12,13},{... | collective-permute-start | bytes 181448 | tf_op jit(solution)/shard_map/ppermute | solution.py:22
  83.7 5.1 %collective-permute-start.7 = (f32[20,756]{1,0:T(8,128)S(1)}, f32[20,756]{1,0:T(8,128)S(1)}, u32[]{:S(2)}, u32[]{:S(2)}) collective-permute-start(f32[20,756]{1,0:T(8,128)S(1)} %reshape.274), channel_id=1, source_target_pairs={{1,0},{2,1},{3,2},{5,4},{6,5},{7,6},{9,8},{10,9},{11,10},{13,12},{... | collective-permute-start | bytes 181448 | tf_op jit(solution)/shard_map/ppermute | solution.py:23
  96.2 0.7 copy-start.10
  99.6 0.7 copy-start.9
  99.6 0.7 copy-start.13
  100.2 2.2 %copy-start.11 = (pred[132]{0:T(512)(128)(4,1)S(1)}, pred[132]{0:T(512)(128)(4,1)}, u32[]{:S(2)}) copy-start(pred[132]{0:T(512)(128)(4,1)} %compare_and_fusion.6) | copy-start | bytes 400
  102.5 2.0 %copy-start.12 = (pred[130]{0:T(512)(128)(4,1)S(1)}, pred[130]{0:T(512)(128)(4,1)}, u32[]{:S(2)}) copy-start(pred[130]{0:T(512)(128)(4,1)} %compare_and_fusion.9) | copy-start | bytes 394
